TPU v7x, 128 devices: a whole 4x4x4 slice. The times are simulated.
128 devices in a mesh: pipe: 16 (over x_hi, y, core), dp: 8 (over x_lo, z).
Axes of the slice: x: 4 (x_hi: 2, x_lo: 2; x = x_hi * 2 + x_lo), y: 4, z: 4, core: 2. Of those that a mesh axis runs over, the one named last changes fastest.
Arguments:
- inputs: bfloat16 [4, 768, 3072], P(None, 'dp'), may hold values from -24 to 24
- projection: bfloat16 [16, 3072, 3072], P('pipe'), may hold values from -0.109375 to 0.109375
- cotangent: bfloat16 [4, 768, 3072], P(None, 'dp'), may hold values from -6 to 6
Outputs:
- weight_grad: bfloat16 [16, 3072, 3072], P('pipe', 'dp')
All inputs are finite; a program needn't handle non-finite values.
Results may differ from a plain program's by a relative error of at most 0.033.
Values may be sent and summed in bfloat16 or wider, within the bound.
No kernel may reach another device: no remote copies, remote signals or barrier semaphores. Data moves between devices by JAX's collectives and lax.ppermute only.
A program may use at most 192 MiB of HBM per device.

v0:
```python
import math

import jax
import jax.numpy as jnp
from jax import lax
from jax.sharding import PartitionSpec as P

EPSILON = 1e-06


def from_behind(array, axis, by):
    count = lax.axis_size(axis)
    pairs = [(i, i + by) for i in range(count) if 0 <= i + by < count]
    return lax.ppermute(array, axis, pairs)


def norm_factor(values):
    floats = values.astype(jnp.float32)
    factor = lax.rsqrt(jnp.mean(floats * floats, axis=-1, keepdims=True) + EPSILON)
    return (floats, factor)


def forward_layer(values, weight):
    floats, factor = norm_factor(values)
    normed = (floats * factor).astype(jnp.bfloat16)
    gate_value = jnp.dot(normed, weight, preferred_element_type=jnp.float32)
    output = (floats + jax.nn.silu(gate_value)).astype(jnp.bfloat16)
    return (output, gate_value)


def backward_layer(values, gate_value, upstream, weight):
    floats, factor = norm_factor(values)
    up_float = upstream.astype(jnp.float32)
    sigma = jax.nn.sigmoid(gate_value)
    slope = (up_float * sigma * (1.0 + gate_value * (1.0 - sigma))).astype(jnp.bfloat16)
    back = lax.dot_general(
        slope, weight, (((1,), (1,)), ((), ())), preferred_element_type=jnp.float32
    )
    unit = floats * factor
    down = (
        up_float + factor * (back - unit * jnp.mean(back * unit, axis=-1, keepdims=True))
    ).astype(jnp.bfloat16)
    return (down, slope)


def on_device(inputs, projection, cotangent):
    weight = projection[0]
    micro, rows_mb, width = inputs.shape
    section = lax.axis_index("pipe")
    sections = lax.axis_size("pipe")
    replicas = lax.axis_size("dp")
    ticks = micro + sections - 1
    zero_act = jnp.zeros((rows_mb, width), jnp.bfloat16)
    zero_gate = jnp.zeros((rows_mb, width), jnp.float32)

    def run_forward(source):
        return forward_layer(source, weight)

    def skip_forward(source):
        return (zero_act, zero_gate)

    def forward_tick(carry, tick):
        incoming, kept_inputs, kept_gates = carry
        batch = tick - section
        active = (batch >= 0) & (batch < micro)
        slot = jnp.clip(batch, 0, micro - 1)
        first = lax.dynamic_index_in_dim(inputs, slot, 0, keepdims=False)
        source = jnp.where(section == 0, first, incoming)
        output, gate_value = lax.cond(active, run_forward, skip_forward, source)
        old_input = lax.dynamic_index_in_dim(kept_inputs, slot, 0, keepdims=False)
        kept_inputs = lax.dynamic_update_index_in_dim(
            kept_inputs, jnp.where(active, source, old_input), slot, 0
        )
        old_gate = lax.dynamic_index_in_dim(kept_gates, slot, 0, keepdims=False)
        kept_gates = lax.dynamic_update_index_in_dim(
            kept_gates, jnp.where(active, gate_value, old_gate), slot, 0
        )
        incoming = from_behind(output, "pipe", 1)
        return ((incoming, kept_inputs, kept_gates), None)

    start_carry = (
        zero_act,
        jnp.zeros_like(inputs),
        jnp.zeros((micro, rows_mb, width), jnp.float32),
    )
    (unused_act, kept_inputs, kept_gates), unused = lax.scan(
        forward_tick, start_carry, jnp.arange(ticks, dtype=jnp.int32)
    )

    def run_backward(operands):
        source, stored_input, stored_gate = operands
        return backward_layer(stored_input, stored_gate, source, weight)

    def skip_backward(operands):
        return (zero_act, zero_act)

    def backward_tick(carry, tick):
        incoming, kept_slopes = carry
        batch = tick - (sections - 1 - section)
        active = (batch >= 0) & (batch < micro)
        slot = jnp.clip(batch, 0, micro - 1)
        first = lax.dynamic_index_in_dim(cotangent, slot, 0, keepdims=False)
        source = jnp.where(section == sections - 1, first, incoming)
        stored_input = lax.dynamic_index_in_dim(kept_inputs, slot, 0, keepdims=False)
        stored_gate = lax.dynamic_index_in_dim(kept_gates, slot, 0, keepdims=False)
        down, slope = lax.cond(
            active, run_backward, skip_backward, (source, stored_input, stored_gate)
        )
        old_slope = lax.dynamic_index_in_dim(kept_slopes, slot, 0, keepdims=False)
        kept_slopes = lax.dynamic_update_index_in_dim(
            kept_slopes, jnp.where(active, slope, old_slope), slot, 0
        )
        incoming = from_behind(down, "pipe", -1)
        return ((incoming, kept_slopes), None)

    (unused_grad, kept_slopes), unused = lax.scan(
        backward_tick, (zero_act, jnp.zeros_like(cotangent)), jnp.arange(ticks, dtype=jnp.int32)
    )
    shard_rows = micro * rows_mb
    floats, factor = norm_factor(kept_inputs)
    normed_all = (floats * factor).astype(jnp.bfloat16).reshape(shard_rows, width)
    slope_all = kept_slopes.reshape(shard_rows, width)
    summed = lax.psum_scatter(
        lax.dot_general(
            normed_all, slope_all, (((0,), (0,)), ((), ())), preferred_element_type=jnp.float32
        ).astype(jnp.bfloat16),
        "dp",
        scatter_dimension=0,
        tiled=True,
    ).astype(jnp.float32)
    factor_out = 1.0 / math.sqrt(micro * rows_mb * replicas)
    return (summed * factor_out).astype(jnp.bfloat16)[None]


def solution(mesh):
    placed = (P(None, "dp", None), P("pipe", None, None), P(None, "dp", None))
    return jax.shard_map(
        on_device, mesh=mesh, in_specs=placed, out_specs=P("pipe", "dp", None), check_vma=False
    )
```

profile of v0, /device:TPU:6, one launch (start us, length us, event | category | flops | bytes accessed | tf_op | source)
XLA Modules:
  0.0 1119.6 jit_solution(16657084477745194645)
XLA Ops:
  11.0 407.9 %while.29 = (s32[]{:T(128)}, bf16[96,3072]{1,0:T(8,128)(2,1)S(1)}, bf16[4,96,3072]{2,1,0:T(8,128)(2,1)}, f32[4,96,3072]{2,1,0:T(8,128)}, s32[19]{0:T(128)S(1)}, ...) while((s32[]{:T(128)}, bf16[96,3072]{1,0:T(8,128)(2,1)S(1)}, ...), condition=%wide.region_4.5_spmd, body=%wide.region_0.4_spmd.sunk | while | flops 1816658048 | bytes 34212120 | solution.py:86
  20.1 10.4 collective-permute-done
  39.6 10.4 collective-permute-done
  59.1 10.4 collective-permute-done
  78.7 10.4 collective-permute-done
  98.2 10.4 collective-permute-done
  117.7 10.4 collective-permute-done
  137.2 10.4 collective-permute-done
  156.7 14.5 %collective-permute-done = bf16[96,3072]{1,0:T(8,128)(2,1)S(1)} collective-permute-done((bf16[96,3072]{1,0:T(8,128)(2,1)S(1)}, bf16[96,3072]{1,0:T(8,128)(2,1)S(1)}, u32[]{:S(2)}, u32[]{:S(2)}) %collective-permute-start) | collective-permute-done | bytes 589856 | tf_op jit(solution)/shard_map/while/body/eval_jaxpr/ppermute | solution.py:14
  188.6 10.4 collective-permute-done
  244.1 10.4 collective-permute-done
  422.8 432.7 %while.30 = (s32[]{:T(128)}, bf16[96,3072]{1,0:T(8,128)(2,1)S(1)}, bf16[4,96,3072]{2,1,0:T(8,128)(2,1)}, s32[19]{0:T(128)S(1)}, s32[]{:T(128)}, /*index=5*/pred[...) while((s32[]{:T(128)}, bf16[96,3072]{1,0:T(8,128)(2,1)S(1)}, ...), condition=%wide.region_11.12_spmd, body=%wide.region_6.11_spmd.sunk | while | flops 1820196992 | bytes 38342916 | solution.py:116
  524.7 57.4 %collective-permute-done.1 = bf16[96,3072]{1,0:T(8,128)(2,1)S(1)} collective-permute-done((bf16[96,3072]{1,0:T(8,128)(2,1)S(1)}, bf16[96,3072]{1,0:T(8,128)(2,1)S(1)}, u32[]{:S(2)}, u32[]{:S(2)}) %collective-permute-start.1) | collective-permute-done | bytes 589856 | tf_op jit(solution)/shard_map/while/body/eval_jaxpr/ppermute | solution.py:14
  583.2 16.8 %conditional.5 = (bf16[96,3072]{1,0:T(8,128)(2,1)S(1)}, bf16[96,3072]{1,0:T(8,128)(2,1)S(1)}) conditional(s32[]{:T(128)} %convert_element_type.108, () %tuple.75, (pred[]{:T(512)}, bf16[4,96,3072]{2,1,0:T(8,128)(2,1)}, s32[]{:T(128)}, bf16[96,3072]{1,0:T(8,128)(2,1)S(1)}, bf16[4,96,3072]{2,1,0:T(8,128)(2,1)}, /*index=5*/f32[4,96,3072]{2,1,0:T(8,128)}, ...), branch_computations={%region_7.7_spmd, %region_8.10_spmd} | conditional | flops 1819902080 | bytes 33033684 | solution.py:106
  585.6 12.7 %fusion.8 = (f32[96]{0:T(128)S(1)}, f32[96,3072]{1,0:T(8,128)S(1)}) fusion(f32[96]{0:T(128)S(1)} %add_rsqrt_fusion.1, bf16[4,96,3072]{2,1,0:T(8,128)(2,1)} %get-tuple-element.254, s32[]{:T(128)} %get-tuple-element.252, bf16[96,3072]{1,0:T(8,128)(2,1)S(1)} %get-tuple-element.457, bf16[3072,3072]{1,0:T(8,128)(2,1)} %get-tuple-element.256), kind=kOutput, calls=%fused_computation.22 | convolution fusion | flops 1813118848 | bytes 21234436 | tf_op jit(solution)/shard_map/while/body/eval_jaxpr/cond/branch_1_fun/dot_general | solution.py:36
  612.3 16.8 %conditional.5 = (bf16[96,3072]{1,0:T(8,128)(2,1)S(1)}, bf16[96,3072]{1,0:T(8,128)(2,1)S(1)}) conditional(s32[]{:T(128)} %convert_element_type.108, () %tuple.75, (pred[]{:T(512)}, bf16[4,96,3072]{2,1,0:T(8,128)(2,1)}, s32[]{:T(128)}, bf16[96,3072]{1,0:T(8,128)(2,1)S(1)}, bf16[4,96,3072]{2,1,0:T(8,128)(2,1)}, /*index=5*/f32[4,96,3072]{2,1,0:T(8,128)}, ...), branch_computations={%region_7.7_spmd, %region_8.10_spmd} | conditional | flops 1819902080 | bytes 33033684 | solution.py:106
  614.7 12.7 %fusion.8 = (f32[96]{0:T(128)S(1)}, f32[96,3072]{1,0:T(8,128)S(1)}) fusion(f32[96]{0:T(128)S(1)} %add_rsqrt_fusion.1, bf16[4,96,3072]{2,1,0:T(8,128)(2,1)} %get-tuple-element.254, s32[]{:T(128)} %get-tuple-element.252, bf16[96,3072]{1,0:T(8,128)(2,1)S(1)} %get-tuple-element.457, bf16[3072,3072]{1,0:T(8,128)(2,1)} %get-tuple-element.256), kind=kOutput, calls=%fused_computation.22 | convolution fusion | flops 1813118848 | bytes 21234436 | tf_op jit(solution)/shard_map/while/body/eval_jaxpr/cond/branch_1_fun/dot_general | solution.py:36
  643.2 16.8 %conditional.5 = (bf16[96,3072]{1,0:T(8,128)(2,1)S(1)}, bf16[96,3072]{1,0:T(8,128)(2,1)S(1)}) conditional(s32[]{:T(128)} %convert_element_type.108, () %tuple.75, (pred[]{:T(512)}, bf16[4,96,3072]{2,1,0:T(8,128)(2,1)}, s32[]{:T(128)}, bf16[96,3072]{1,0:T(8,128)(2,1)S(1)}, bf16[4,96,3072]{2,1,0:T(8,128)(2,1)}, /*index=5*/f32[4,96,3072]{2,1,0:T(8,128)}, ...), branch_computations={%region_7.7_spmd, %region_8.10_spmd} | conditional | flops 1819902080 | bytes 33033684 | solution.py:106
  645.6 12.7 %fusion.8 = (f32[96]{0:T(128)S(1)}, f32[96,3072]{1,0:T(8,128)S(1)}) fusion(f32[96]{0:T(128)S(1)} %add_rsqrt_fusion.1, bf16[4,96,3072]{2,1,0:T(8,128)(2,1)} %get-tuple-element.254, s32[]{:T(128)} %get-tuple-element.252, bf16[96,3072]{1,0:T(8,128)(2,1)S(1)} %get-tuple-element.457, bf16[3072,3072]{1,0:T(8,128)(2,1)} %get-tuple-element.256), kind=kOutput, calls=%fused_computation.22 | convolution fusion | flops 1813118848 | bytes 21234436 | tf_op jit(solution)/shard_map/while/body/eval_jaxpr/cond/branch_1_fun/dot_general | solution.py:36
  676.0 16.8 %conditional.5 = (bf16[96,3072]{1,0:T(8,128)(2,1)S(1)}, bf16[96,3072]{1,0:T(8,128)(2,1)S(1)}) conditional(s32[]{:T(128)} %convert_element_type.108, () %tuple.75, (pred[]{:T(512)}, bf16[4,96,3072]{2,1,0:T(8,128)(2,1)}, s32[]{:T(128)}, bf16[96,3072]{1,0:T(8,128)(2,1)S(1)}, bf16[4,96,3072]{2,1,0:T(8,128)(2,1)}, /*index=5*/f32[4,96,3072]{2,1,0:T(8,128)}, ...), branch_computations={%region_7.7_spmd, %region_8.10_spmd} | conditional | flops 1819902080 | bytes 33033684 | solution.py:106
  678.3 12.7 %fusion.8 = (f32[96]{0:T(128)S(1)}, f32[96,3072]{1,0:T(8,128)S(1)}) fusion(f32[96]{0:T(128)S(1)} %add_rsqrt_fusion.1, bf16[4,96,3072]{2,1,0:T(8,128)(2,1)} %get-tuple-element.254, s32[]{:T(128)} %get-tuple-element.252, bf16[96,3072]{1,0:T(8,128)(2,1)S(1)} %get-tuple-element.457, bf16[3072,3072]{1,0:T(8,128)(2,1)} %get-tuple-element.256), kind=kOutput, calls=%fused_computation.22 | convolution fusion | flops 1813118848 | bytes 21234436 | tf_op jit(solution)/shard_map/while/body/eval_jaxpr/cond/branch_1_fun/dot_general | solution.py:36
  708.9 24.1 %collective-permute-start.1 = (bf16[96,3072]{1,0:T(8,128)(2,1)S(1)}, bf16[96,3072]{1,0:T(8,128)(2,1)S(1)}, u32[]{:S(2)}, u32[]{:S(2)}) collective-permute-start(bf16[96,3072]{1,0:T(8,128)(2,1)S(1)} %get-tuple-element.448), channel_id=1, source_target_pairs={{8,0},{16,8},{24,16},{32,24},{40,32},{48,40},{56,48},{64,56},{72,6... | collective-permute-start | bytes 1769480 | tf_op jit(solution)/shard_map/while/body/eval_jaxpr/ppermute | solution.py:14
  855.5 16.1 %bitcast_convert_fusion = bf16[3072,3072]{1,0:T(8,128)(2,1)} fusion(bf16[4,96,3072]{2,1,0:T(8,128)(2,1)} %get-tuple-element.275, bf16[4,96,3072]{2,1,0:T(8,128)(2,1)} %get-tuple-element.504, f32[4,96]{1,0:T(4,128)S(1)} %add_rsqrt_fusion.2), kind=kOutput, calls=%fused_computation.41 | convolution fusion | flops 7260733440 | bytes 23594496 | tf_op jit(solution)/shard_map/dot_general | solution.py:124
  871.6 237.6 %reduce-scatter.2.cloned.1.call-done = bf16[384,3072]{1,0:T(8,128)(2,1)} async-done(((bf16[3072,3072]{1,0:T(8,128)(2,1)}), bf16[384,3072]{1,0:T(8,128)(2,1)}) %reduce-scatter.2.cloned.1.call-update) | async-done | bytes 2359312 | tf_op jit(solution)/shard_map/reduce_scatter | solution.py:123
  (366 shorter events, 625.5 us)
Async XLA Ops:
  6.5 1102.6 %reduce-scatter.2.cloned.1.call-start = ((), (), s32[]{:S(2)}) async-start(), calls=%async_computation.1 | async-start | bytes 21233664 | tf_op jit(solution)/shard_map/reduce_scatter | solution.py:123
  15.7 14.8 %collective-permute-start = (bf16[96,3072]{1,0:T(8,128)(2,1)S(1)}, bf16[96,3072]{1,0:T(8,128)(2,1)S(1)}, u32[]{:S(2)}, u32[]{:S(2)}) collective-permute-start(bf16[96,3072]{1,0:T(8,128)(2,1)S(1)} %get-tuple-element.435), channel_id=1, source_target_pairs={{0,8},{8,16},{16,24},{24,32},{32,40},{40,48},{48,56},{56,64},{64,7... | collective-permute-start | bytes 1769480 | tf_op jit(solution)/shard_map/while/body/eval_jaxpr/ppermute | solution.py:14
  113.2 14.8 %collective-permute-start = (bf16[96,3072]{1,0:T(8,128)(2,1)S(1)}, bf16[96,3072]{1,0:T(8,128)(2,1)S(1)}, u32[]{:S(2)}, u32[]{:S(2)}) collective-permute-start(bf16[96,3072]{1,0:T(8,128)(2,1)S(1)} %get-tuple-element.435), channel_id=1, source_target_pairs={{0,8},{8,16},{16,24},{24,32},{32,40},{40,48},{48,56},{56,64},{64,7... | collective-permute-start | bytes 1769480 | tf_op jit(solution)/shard_map/while/body/eval_jaxpr/ppermute | solution.py:14
  132.8 14.8 %collective-permute-start = (bf16[96,3072]{1,0:T(8,128)(2,1)S(1)}, bf16[96,3072]{1,0:T(8,128)(2,1)S(1)}, u32[]{:S(2)}, u32[]{:S(2)}) collective-permute-start(bf16[96,3072]{1,0:T(8,128)(2,1)S(1)} %get-tuple-element.435), channel_id=1, source_target_pairs={{0,8},{8,16},{16,24},{24,32},{32,40},{40,48},{48,56},{56,64},{64,7... | collective-permute-start | bytes 1769480 | tf_op jit(solution)/shard_map/while/body/eval_jaxpr/ppermute | solution.py:14
  152.3 18.9 %collective-permute-start = (bf16[96,3072]{1,0:T(8,128)(2,1)S(1)}, bf16[96,3072]{1,0:T(8,128)(2,1)S(1)}, u32[]{:S(2)}, u32[]{:S(2)}) collective-permute-start(bf16[96,3072]{1,0:T(8,128)(2,1)S(1)} %get-tuple-element.435), channel_id=1, source_target_pairs={{0,8},{8,16},{16,24},{24,32},{32,40},{40,48},{48,56},{56,64},{64,7... | collective-permute-start | bytes 1769480 | tf_op jit(solution)/shard_map/while/body/eval_jaxpr/ppermute | solution.py:14
  211.9 14.8 %collective-permute-start = (bf16[96,3072]{1,0:T(8,128)(2,1)S(1)}, bf16[96,3072]{1,0:T(8,128)(2,1)S(1)}, u32[]{:S(2)}, u32[]{:S(2)}) collective-permute-start(bf16[96,3072]{1,0:T(8,128)(2,1)S(1)} %get-tuple-element.435), channel_id=1, source_target_pairs={{0,8},{8,16},{16,24},{24,32},{32,40},{40,48},{48,56},{56,64},{64,7... | collective-permute-start | bytes 1769480 | tf_op jit(solution)/shard_map/while/body/eval_jaxpr/ppermute | solution.py:14
  267.4 14.8 %collective-permute-start = (bf16[96,3072]{1,0:T(8,128)(2,1)S(1)}, bf16[96,3072]{1,0:T(8,128)(2,1)S(1)}, u32[]{:S(2)}, u32[]{:S(2)}) collective-permute-start(bf16[96,3072]{1,0:T(8,128)(2,1)S(1)} %get-tuple-element.435), channel_id=1, source_target_pairs={{0,8},{8,16},{16,24},{24,32},{32,40},{40,48},{48,56},{56,64},{64,7... | collective-permute-start | bytes 1769480 | tf_op jit(solution)/shard_map/while/body/eval_jaxpr/ppermute | solution.py:14
  306.4 14.8 %collective-permute-start = (bf16[96,3072]{1,0:T(8,128)(2,1)S(1)}, bf16[96,3072]{1,0:T(8,128)(2,1)S(1)}, u32[]{:S(2)}, u32[]{:S(2)}) collective-permute-start(bf16[96,3072]{1,0:T(8,128)(2,1)S(1)} %get-tuple-element.435), channel_id=1, source_target_pairs={{0,8},{8,16},{16,24},{24,32},{32,40},{40,48},{48,56},{56,64},{64,7... | collective-permute-start | bytes 1769480 | tf_op jit(solution)/shard_map/while/body/eval_jaxpr/ppermute | solution.py:14
  434.7 14.8 %collective-permute-start.1 = (bf16[96,3072]{1,0:T(8,128)(2,1)S(1)}, bf16[96,3072]{1,0:T(8,128)(2,1)S(1)}, u32[]{:S(2)}, u32[]{:S(2)}) collective-permute-start(bf16[96,3072]{1,0:T(8,128)(2,1)S(1)} %get-tuple-element.448), channel_id=1, source_target_pairs={{8,0},{16,8},{24,16},{32,24},{40,32},{48,40},{56,48},{64,56},{72,6... | collective-permute-start | bytes 1769480 | tf_op jit(solution)/shard_map/while/body/eval_jaxpr/ppermute | solution.py:14
  450.8 14.8 %collective-permute-start.1 = (bf16[96,3072]{1,0:T(8,128)(2,1)S(1)}, bf16[96,3072]{1,0:T(8,128)(2,1)S(1)}, u32[]{:S(2)}, u32[]{:S(2)}) collective-permute-start(bf16[96,3072]{1,0:T(8,128)(2,1)S(1)} %get-tuple-element.448), channel_id=1, source_target_pairs={{8,0},{16,8},{24,16},{32,24},{40,32},{48,40},{56,48},{64,56},{72,6... | collective-permute-start | bytes 1769480 | tf_op jit(solution)/shard_map/while/body/eval_jaxpr/ppermute | solution.py:14
  466.9 14.8 %collective-permute-start.1 = (bf16[96,3072]{1,0:T(8,128)(2,1)S(1)}, bf16[96,3072]{1,0:T(8,128)(2,1)S(1)}, u32[]{:S(2)}, u32[]{:S(2)}) collective-permute-start(bf16[96,3072]{1,0:T(8,128)(2,1)S(1)} %get-tuple-element.448), channel_id=1, source_target_pairs={{8,0},{16,8},{24,16},{32,24},{40,32},{48,40},{56,48},{64,56},{72,6... | collective-permute-start | bytes 1769480 | tf_op jit(solution)/shard_map/while/body/eval_jaxpr/ppermute | solution.py:14
  483.0 14.8 %collective-permute-start.1 = (bf16[96,3072]{1,0:T(8,128)(2,1)S(1)}, bf16[96,3072]{1,0:T(8,128)(2,1)S(1)}, u32[]{:S(2)}, u32[]{:S(2)}) collective-permute-start(bf16[96,3072]{1,0:T(8,128)(2,1)S(1)} %get-tuple-element.448), channel_id=1, source_target_pairs={{8,0},{16,8},{24,16},{32,24},{40,32},{48,40},{56,48},{64,56},{72,6... | collective-permute-start | bytes 1769480 | tf_op jit(solution)/shard_map/while/body/eval_jaxpr/ppermute | solution.py:14
  499.1 14.8 %collective-permute-start.1 = (bf16[96,3072]{1,0:T(8,128)(2,1)S(1)}, bf16[96,3072]{1,0:T(8,128)(2,1)S(1)}, u32[]{:S(2)}, u32[]{:S(2)}) collective-permute-start(bf16[96,3072]{1,0:T(8,128)(2,1)S(1)} %get-tuple-element.448), channel_id=1, source_target_pairs={{8,0},{16,8},{24,16},{32,24},{40,32},{48,40},{56,48},{64,56},{72,6... | collective-permute-start | bytes 1769480 | tf_op jit(solution)/shard_map/while/body/eval_jaxpr/ppermute | solution.py:14
  515.2 66.9 %collective-permute-start.1 = (bf16[96,3072]{1,0:T(8,128)(2,1)S(1)}, bf16[96,3072]{1,0:T(8,128)(2,1)S(1)}, u32[]{:S(2)}, u32[]{:S(2)}) collective-permute-start(bf16[96,3072]{1,0:T(8,128)(2,1)S(1)} %get-tuple-element.448), channel_id=1, source_target_pairs={{8,0},{16,8},{24,16},{32,24},{40,32},{48,40},{56,48},{64,56},{72,6... | collective-permute-start | bytes 1769480 | tf_op jit(solution)/shard_map/while/body/eval_jaxpr/ppermute | solution.py:14
  660.0 14.8 %collective-permute-start.1 = (bf16[96,3072]{1,0:T(8,128)(2,1)S(1)}, bf16[96,3072]{1,0:T(8,128)(2,1)S(1)}, u32[]{:S(2)}, u32[]{:S(2)}) collective-permute-start(bf16[96,3072]{1,0:T(8,128)(2,1)S(1)} %get-tuple-element.448), channel_id=1, source_target_pairs={{8,0},{16,8},{24,16},{32,24},{40,32},{48,40},{56,48},{64,56},{72,6... | collective-permute-start | bytes 1769480 | tf_op jit(solution)/shard_map/while/body/eval_jaxpr/ppermute | solution.py:14
  692.8 14.8 %collective-permute-start.1 = (bf16[96,3072]{1,0:T(8,128)(2,1)S(1)}, bf16[96,3072]{1,0:T(8,128)(2,1)S(1)}, u32[]{:S(2)}, u32[]{:S(2)}) collective-permute-start(bf16[96,3072]{1,0:T(8,128)(2,1)S(1)} %get-tuple-element.448), channel_id=1, source_target_pairs={{8,0},{16,8},{24,16},{32,24},{40,32},{48,40},{56,48},{64,56},{72,6... | collective-permute-start | bytes 1769480 | tf_op jit(solution)/shard_map/while/body/eval_jaxpr/ppermute | solution.py:14
  708.9 31.5 %collective-permute-start.1 = (bf16[96,3072]{1,0:T(8,128)(2,1)S(1)}, bf16[96,3072]{1,0:T(8,128)(2,1)S(1)}, u32[]{:S(2)}, u32[]{:S(2)}) collective-permute-start(bf16[96,3072]{1,0:T(8,128)(2,1)S(1)} %get-tuple-element.448), channel_id=1, source_target_pairs={{8,0},{16,8},{24,16},{32,24},{40,32},{48,40},{56,48},{64,56},{72,6... | collective-permute-start | bytes 1769480 | tf_op jit(solution)/shard_map/while/body/eval_jaxpr/ppermute | solution.py:14
  741.6 14.8 %collective-permute-start.1 = (bf16[96,3072]{1,0:T(8,128)(2,1)S(1)}, bf16[96,3072]{1,0:T(8,128)(2,1)S(1)}, u32[]{:S(2)}, u32[]{:S(2)}) collective-permute-start(bf16[96,3072]{1,0:T(8,128)(2,1)S(1)} %get-tuple-element.448), channel_id=1, source_target_pairs={{8,0},{16,8},{24,16},{32,24},{40,32},{48,40},{56,48},{64,56},{72,6... | collective-permute-start | bytes 1769480 | tf_op jit(solution)/shard_map/while/body/eval_jaxpr/ppermute | solution.py:14
  757.7 14.8 %collective-permute-start.1 = (bf16[96,3072]{1,0:T(8,128)(2,1)S(1)}, bf16[96,3072]{1,0:T(8,128)(2,1)S(1)}, u32[]{:S(2)}, u32[]{:S(2)}) collective-permute-start(bf16[96,3072]{1,0:T(8,128)(2,1)S(1)} %get-tuple-element.448), channel_id=1, source_target_pairs={{8,0},{16,8},{24,16},{32,24},{40,32},{48,40},{56,48},{64,56},{72,6... | collective-permute-start | bytes 1769480 | tf_op jit(solution)/shard_map/while/body/eval_jaxpr/ppermute | solution.py:14
  773.8 14.8 %collective-permute-start.1 = (bf16[96,3072]{1,0:T(8,128)(2,1)S(1)}, bf16[96,3072]{1,0:T(8,128)(2,1)S(1)}, u32[]{:S(2)}, u32[]{:S(2)}) collective-permute-start(bf16[96,3072]{1,0:T(8,128)(2,1)S(1)} %get-tuple-element.448), channel_id=1, source_target_pairs={{8,0},{16,8},{24,16},{32,24},{40,32},{48,40},{56,48},{64,56},{72,6... | collective-permute-start | bytes 1769480 | tf_op jit(solution)/shard_map/while/body/eval_jaxpr/ppermute | solution.py:14
  789.9 17.3 %collective-permute-start.1 = (bf16[96,3072]{1,0:T(8,128)(2,1)S(1)}, bf16[96,3072]{1,0:T(8,128)(2,1)S(1)}, u32[]{:S(2)}, u32[]{:S(2)}) collective-permute-start(bf16[96,3072]{1,0:T(8,128)(2,1)S(1)} %get-tuple-element.448), channel_id=1, source_target_pairs={{8,0},{16,8},{24,16},{32,24},{40,32},{48,40},{56,48},{64,56},{72,6... | collective-permute-start | bytes 1769480 | tf_op jit(solution)/shard_map/while/body/eval_jaxpr/ppermute | solution.py:14
  808.5 14.8 %collective-permute-start.1 = (bf16[96,3072]{1,0:T(8,128)(2,1)S(1)}, bf16[96,3072]{1,0:T(8,128)(2,1)S(1)}, u32[]{:S(2)}, u32[]{:S(2)}) collective-permute-start(bf16[96,3072]{1,0:T(8,128)(2,1)S(1)} %get-tuple-element.448), channel_id=1, source_target_pairs={{8,0},{16,8},{24,16},{32,24},{40,32},{48,40},{56,48},{64,56},{72,6... | collective-permute-start | bytes 1769480 | tf_op jit(solution)/shard_map/while/body/eval_jaxpr/ppermute | solution.py:14
  824.6 14.8 %collective-permute-start.1 = (bf16[96,3072]{1,0:T(8,128)(2,1)S(1)}, bf16[96,3072]{1,0:T(8,128)(2,1)S(1)}, u32[]{:S(2)}, u32[]{:S(2)}) collective-permute-start(bf16[96,3072]{1,0:T(8,128)(2,1)S(1)} %get-tuple-element.448), channel_id=1, source_target_pairs={{8,0},{16,8},{24,16},{32,24},{40,32},{48,40},{56,48},{64,56},{72,6... | collective-permute-start | bytes 1769480 | tf_op jit(solution)/shard_map/while/body/eval_jaxpr/ppermute | solution.py:14
  840.7 14.8 %collective-permute-start.1 = (bf16[96,3072]{1,0:T(8,128)(2,1)S(1)}, bf16[96,3072]{1,0:T(8,128)(2,1)S(1)}, u32[]{:S(2)}, u32[]{:S(2)}) collective-permute-start(bf16[96,3072]{1,0:T(8,128)(2,1)S(1)} %get-tuple-element.448), channel_id=1, source_target_pairs={{8,0},{16,8},{24,16},{32,24},{40,32},{48,40},{56,48},{64,56},{72,6... | collective-permute-start | bytes 1769480 | tf_op jit(solution)/shard_map/while/body/eval_jaxpr/ppermute | solution.py:14
  (23 other events, 269.0 us)
Sparse Core Ops, SparseCore 0:
  871.7 237.3 reduce-scatter.1
where the time goes:
time: 1130 us; the launch traced here: 1120 us
  waiting for transfers between devices  593 us (52%)
  starting transfers between devices  184 us (16%)
  other arithmetic  104 us (9%)
  local copies, waits for them, and re-layouts  101 us (9%)
  matrix products  99.5 us (9%)
  loops' own time  25 us (2%)
  between operations  13.4 us (1%)
    ppermute x38, waiting for transfers between devices, from_behind(): return lax.ppermute(array, axis, pairs)  356 us
    reduce_scatter x1, waiting for transfers between devices, on_device(): lax.psum_scatter(lax.dot_general(normed_all, slope_all, (((0,), (0,)), ((...  238 us
    ppermute x38, starting transfers between devices, from_behind(): return lax.ppermute(array, axis, pairs)  184 us
    dot_general x4, matrix products, backward_layer(): lax.dot_general(slope, weight, (((1,), (1,)), ((), ())), preferred_elemen...  50.7 us
    dynamic_update_slice x19, other arithmetic, forward_tick(): lax.dynamic_update_index_in_dim(kept_inputs, jnp.where(active, source, ol...  40.7 us
    dot_general x4, matrix products, forward_layer(): gate_value = jnp.dot(normed, weight, preferred_element_type=jnp.float32)  32.7 us
    dynamic_slice x19, local copies, waits for them, and re-layouts, forward_tick(): old_gate = lax.dynamic_index_in_dim(kept_gates, slot, 0, keepdims=False)  25.7 us
    dynamic_slice x38, local copies, waits for them, and re-layouts, on_device(): lax.scan(forward_tick, start_carry, jnp.arange(ticks, dtype=jnp.int32))  23 us
  transfers between devices with their start and end apart: 39, of which 39 were waited for; matrix products, arithmetic and copies ran while one was open for 8% of the time, Pallas kernels for 0%

commit v1 on v0

v1 whole, which is shorter than its diff:
```python
import math

import jax
import jax.numpy as jnp
from jax import lax
from jax.experimental.layout import Layout, with_layout_constraint
from jax.sharding import PartitionSpec as P

EPSILON = 1e-06


def from_behind(array, axis, by):
    count = lax.axis_size(axis)
    pairs = [(i, i + by) for i in range(count) if 0 <= i + by < count]
    return lax.ppermute(array, axis, pairs)


def norm_factor(values):
    floats = values.astype(jnp.float32)
    factor = lax.rsqrt(jnp.mean(floats * floats, axis=-1, keepdims=True) + EPSILON)
    return (floats, factor)


def forward_layer(values, weight):
    floats, factor = norm_factor(values)
    normed = (floats * factor).astype(jnp.bfloat16)
    gate_value = jnp.dot(normed, weight, preferred_element_type=jnp.float32)
    output = (floats + jax.nn.silu(gate_value)).astype(jnp.bfloat16)
    return (output, gate_value)


def backward_layer(values, gate_value, upstream, weight_t):
    floats, factor = norm_factor(values)
    up_float = upstream.astype(jnp.float32)
    sigma = jax.nn.sigmoid(gate_value)
    slope = (up_float * sigma * (1.0 + gate_value * (1.0 - sigma))).astype(jnp.bfloat16)
    back = jnp.dot(slope, weight_t, preferred_element_type=jnp.float32)
    unit = floats * factor
    down = (
        up_float + factor * (back - unit * jnp.mean(back * unit, axis=-1, keepdims=True))
    ).astype(jnp.bfloat16)
    return (down, slope)


def on_device(inputs, projection, cotangent):
    weight = projection[0]
    micro, rows_mb, width = inputs.shape
    section = lax.axis_index("pipe")
    sections = lax.axis_size("pipe")
    replicas = lax.axis_size("dp")
    ticks = micro + sections - 1
    kept_inputs = jnp.zeros((micro + 2, rows_mb, width), jnp.bfloat16)
    kept_gates = jnp.zeros((micro + 2, rows_mb, width), jnp.float32)
    incoming = jnp.zeros((rows_mb, width), jnp.bfloat16)
    for tick in range(ticks):
        batch = tick - section
        slot = jnp.clip(batch + 1, 0, micro + 1)
        first = lax.dynamic_index_in_dim(inputs, jnp.clip(batch, 0, micro - 1), 0, keepdims=False)
        source = jnp.where(section == 0, first, incoming)
        output, gate_value = forward_layer(source, weight)
        kept_inputs = lax.dynamic_update_index_in_dim(kept_inputs, source, slot, 0)
        kept_gates = lax.dynamic_update_index_in_dim(kept_gates, gate_value, slot, 0)
        if tick + 1 < ticks:
            incoming = from_behind(output, "pipe", 1)

    weight_t = with_layout_constraint(jnp.transpose(weight), Layout((0, 1)))
    kept_slopes = jnp.zeros((micro + 2, rows_mb, width), jnp.bfloat16)
    incoming = jnp.zeros((rows_mb, width), jnp.bfloat16)
    cols = width // replicas
    grad_rows = jnp.zeros((cols, width), jnp.float32)
    for tick in range(ticks):
        batch = tick - (sections - 1 - section)
        slot = jnp.clip(batch + 1, 0, micro + 1)
        first = lax.dynamic_index_in_dim(cotangent, jnp.clip(batch, 0, micro - 1), 0, keepdims=False)
        source = jnp.where(section == sections - 1, first, incoming)
        stored_input = lax.dynamic_index_in_dim(kept_inputs, slot, 0, keepdims=False)
        stored_gate = lax.dynamic_index_in_dim(kept_gates, slot, 0, keepdims=False)
        down, slope = backward_layer(stored_input, stored_gate, source, weight_t)
        kept_slopes = lax.dynamic_update_index_in_dim(kept_slopes, slope, slot, 0)
        if tick + 1 < ticks:
            incoming = from_behind(down, "pipe", -1)
        done = tick - (sections - 1)
        if done >= 0:
            floats, factor = norm_factor(kept_inputs[done + 1])
            normed = (floats * factor).astype(jnp.bfloat16)
            normed_cols = lax.all_to_all(normed, "dp", 1, 0, tiled=True)
            slope_all = lax.all_gather(kept_slopes[done + 1], "dp", axis=0, tiled=True)
            grad_rows = grad_rows + lax.dot_general(
                normed_cols, slope_all, (((0,), (0,)), ((), ())), preferred_element_type=jnp.float32
            )
    factor_out = 1.0 / math.sqrt(micro * rows_mb * replicas)
    return (grad_rows * factor_out).astype(jnp.bfloat16)[None]


def solution(mesh):
    placed = (P(None, "dp", None), P("pipe", None, None), P(None, "dp", None))
    return jax.shard_map(
        on_device, mesh=mesh, in_specs=placed, out_specs=P("pipe", "dp", None), check_vma=False
    )
```

time: 1130 us -> 1170 us (1.035)
  matrix products: 99.5 us -> 275 us
  waiting for transfers between devices: 593 us -> 521 us
  local copies, waits for them, and re-layouts: 101 us -> 39.2 us
  loops' own time: 25 us -> 0 us
  other arithmetic: 104 us -> 122 us
    reduce_scatter x1 -> x0, waiting for transfers between devices: 238 us -> none  [on_device(): lax.psum_scatter(lax.dot_general(normed_all, slope_all, (((0,), (0,)), ((...]
    all_gather x0 -> x4, waiting for transfers between devices: none -> 145 us  [on_device(): slope_all = lax.all_gather(kept_slopes[done + 1], 'dp', axis=0, tiled=True)]
    dot_general x5 -> x22, matrix products: 66.8 us -> 179 us  [the longest x18 149 us: backward_layer(): back = jnp.dot(slope, weight_t, preferred_element_type=jnp.float32)]
    dynamic_slice x95 -> x0, local copies, waits for them, and re-layouts: 90.9 us -> none  [the longest x19 25.7 us: forward_tick(): old_gate = lax.dynamic_index_in_dim(kept_gates, slot, 0, keepdims=False)]
    dot_general x4 -> x19, matrix products: 32.7 us -> 95.9 us  [forward_layer(): gate_value = jnp.dot(normed, weight, preferred_element_type=jnp.float32)]
    convert_element_type x4 -> x18, other arithmetic: 6.84 us -> 43.7 us  [backward_layer(): down = (up_float + factor * (back - unit * jnp.mean(back * unit, axis=-1,...]
    unnamed x0 -> x53, local copies, waits for them, and re-layouts: none -> 30 us
    dynamic_update_slice x57 -> x19, other arithmetic: 81.3 us -> 52.9 us  [the longest x18 52.8 us: on_device(): kept_slopes = lax.dynamic_update_index_in_dim(kept_slopes, slope, slot, 0)]
  transfers between devices with their start and end apart: 39 -> 44, of which waited for: 39 -> 40; matrix products, arithmetic and copies ran while one was open for 8% -> 7% of each run, Pallas kernels for 0% -> 0%
where the time goes in v1:
time: 1170 us; the launch traced here: 1160 us
  waiting for transfers between devices  521 us (45%)
  matrix products  275 us (24%)
  starting transfers between devices  188 us (16%)
  other arithmetic  122 us (10%)
  local copies, waits for them, and re-layouts  39.2 us (3%)
  between operations  15.3 us (1%)
    ppermute x36, waiting for transfers between devices, from_behind(): return lax.ppermute(array, axis, pairs)  361 us
    ppermute x36, starting transfers between devices, from_behind(): return lax.ppermute(array, axis, pairs)  167 us
    dot_general x18, matrix products, backward_layer(): back = jnp.dot(slope, weight_t, preferred_element_type=jnp.float32)  149 us
    all_gather x4, waiting for transfers between devices, on_device(): slope_all = lax.all_gather(kept_slopes[done + 1], 'dp', axis=0, tiled=True)  145 us
    dot_general x19, matrix products, forward_layer(): gate_value = jnp.dot(normed, weight, preferred_element_type=jnp.float32)  95.9 us
    dynamic_update_slice x18, other arithmetic, on_device(): kept_slopes = lax.dynamic_update_index_in_dim(kept_slopes, slope, slot, 0)  52.8 us
    convert_element_type x18, other arithmetic, backward_layer(): down = (up_float + factor * (back - unit * jnp.mean(back * unit, axis=-1,...  43.7 us
    dot_general x4, matrix products, on_device(): lax.dot_general(normed_cols, slope_all, (((0,), (0,)), ((), ())), preferr...  30.3 us
  transfers between devices with their start and end apart: 44, of which 40 were waited for; matrix products, arithmetic and copies ran while one was open for 7% of the time, Pallas kernels for 0%

profile of v1, /device:TPU:6, one launch (start us, length us, event | category | flops | bytes accessed | tf_op | source)
XLA Modules:
  0.0 1161.3 jit_solution(12127758742047273274)
XLA Ops:
  11.7 10.6 bitcast_dynamic-update-slice_fusion.17
  25.5 24.7 %copy.5 = bf16[1,3072,3072]{1,2,0:T(8,128)(2,1)} copy(bf16[1,3072,3072]{2,1,0:T(8,128)(2,1)} %param.4) | data formatting | bytes 37748736 | tf_op args[1]
  53.5 10.8 bitcast_dynamic-update-slice_fusion.16
  68.4 11.2 collective-permute-done.1
  87.1 12.3 %collective-permute-done.2 = bf16[96,3072]{1,0:T(8,128)(2,1)S(1)} collective-permute-done((bf16[96,3072]{1,0:T(8,128)(2,1)S(1)}, bf16[96,3072]{1,0:T(8,128)(2,1)S(1)}, u32[]{:S(2)}, u32[]{:S(2)}) %collective-permute-start.2) | collective-permute-done | bytes 589856 | tf_op jit(solution)/shard_map/ppermute | solution.py:15
  106.4 12.8 %collective-permute-done.3 = bf16[96,3072]{1,0:T(8,128)(2,1)S(1)} collective-permute-done((bf16[96,3072]{1,0:T(8,128)(2,1)S(1)}, bf16[96,3072]{1,0:T(8,128)(2,1)S(1)}, u32[]{:S(2)}, u32[]{:S(2)}) %collective-permute-start.3) | collective-permute-done | bytes 589856 | tf_op jit(solution)/shard_map/ppermute | solution.py:15
  126.2 12.8 %collective-permute-done.4 = bf16[96,3072]{1,0:T(8,128)(2,1)S(1)} collective-permute-done((bf16[96,3072]{1,0:T(8,128)(2,1)S(1)}, bf16[96,3072]{1,0:T(8,128)(2,1)S(1)}, u32[]{:S(2)}, u32[]{:S(2)}) %collective-permute-start.4) | collective-permute-done | bytes 589856 | tf_op jit(solution)/shard_map/ppermute | solution.py:15
  146.2 12.7 %collective-permute-done.5 = bf16[96,3072]{1,0:T(8,128)(2,1)S(1)} collective-permute-done((bf16[96,3072]{1,0:T(8,128)(2,1)S(1)}, bf16[96,3072]{1,0:T(8,128)(2,1)S(1)}, u32[]{:S(2)}, u32[]{:S(2)}) %collective-permute-start.5) | collective-permute-done | bytes 589856 | tf_op jit(solution)/shard_map/ppermute | solution.py:15
  165.8 12.8 %collective-permute-done.6 = bf16[96,3072]{1,0:T(8,128)(2,1)S(1)} collective-permute-done((bf16[96,3072]{1,0:T(8,128)(2,1)S(1)}, bf16[96,3072]{1,0:T(8,128)(2,1)S(1)}, u32[]{:S(2)}, u32[]{:S(2)}) %collective-permute-start.6) | collective-permute-done | bytes 589856 | tf_op jit(solution)/shard_map/ppermute | solution.py:15
  185.6 12.8 %collective-permute-done.7 = bf16[96,3072]{1,0:T(8,128)(2,1)S(1)} collective-permute-done((bf16[96,3072]{1,0:T(8,128)(2,1)S(1)}, bf16[96,3072]{1,0:T(8,128)(2,1)S(1)}, u32[]{:S(2)}, u32[]{:S(2)}) %collective-permute-start.7) | collective-permute-done | bytes 589856 | tf_op jit(solution)/shard_map/ppermute | solution.py:15
  205.7 12.6 %collective-permute-done.8 = bf16[96,3072]{1,0:T(8,128)(2,1)S(1)} collective-permute-done((bf16[96,3072]{1,0:T(8,128)(2,1)S(1)}, bf16[96,3072]{1,0:T(8,128)(2,1)S(1)}, u32[]{:S(2)}, u32[]{:S(2)}) %collective-permute-start.8) | collective-permute-done | bytes 589856 | tf_op jit(solution)/shard_map/ppermute | solution.py:15
  225.3 12.8 %collective-permute-done.9 = bf16[96,3072]{1,0:T(8,128)(2,1)S(1)} collective-permute-done((bf16[96,3072]{1,0:T(8,128)(2,1)S(1)}, bf16[96,3072]{1,0:T(8,128)(2,1)S(1)}, u32[]{:S(2)}, u32[]{:S(2)}) %collective-permute-start.9) | collective-permute-done | bytes 589856 | tf_op jit(solution)/shard_map/ppermute | solution.py:15
  245.1 12.8 %collective-permute-done.10 = bf16[96,3072]{1,0:T(8,128)(2,1)S(1)} collective-permute-done((bf16[96,3072]{1,0:T(8,128)(2,1)S(1)}, bf16[96,3072]{1,0:T(8,128)(2,1)S(1)}, u32[]{:S(2)}, u32[]{:S(2)}) %collective-permute-start.10) | collective-permute-done | bytes 589856 | tf_op jit(solution)/shard_map/ppermute | solution.py:15
  265.3 12.4 %collective-permute-done.11 = bf16[96,3072]{1,0:T(8,128)(2,1)S(1)} collective-permute-done((bf16[96,3072]{1,0:T(8,128)(2,1)S(1)}, bf16[96,3072]{1,0:T(8,128)(2,1)S(1)}, u32[]{:S(2)}, u32[]{:S(2)}) %collective-permute-start.11) | collective-permute-done | bytes 589856 | tf_op jit(solution)/shard_map/ppermute | solution.py:15
  284.7 12.8 %collective-permute-done.12 = bf16[96,3072]{1,0:T(8,128)(2,1)S(1)} collective-permute-done((bf16[96,3072]{1,0:T(8,128)(2,1)S(1)}, bf16[96,3072]{1,0:T(8,128)(2,1)S(1)}, u32[]{:S(2)}, u32[]{:S(2)}) %collective-permute-start.12) | collective-permute-done | bytes 589856 | tf_op jit(solution)/shard_map/ppermute | solution.py:15
  304.6 12.8 %collective-permute-done.13 = bf16[96,3072]{1,0:T(8,128)(2,1)S(1)} collective-permute-done((bf16[96,3072]{1,0:T(8,128)(2,1)S(1)}, bf16[96,3072]{1,0:T(8,128)(2,1)S(1)}, u32[]{:S(2)}, u32[]{:S(2)}) %collective-permute-start.13) | collective-permute-done | bytes 589856 | tf_op jit(solution)/shard_map/ppermute | solution.py:15
  324.7 12.7 %collective-permute-done.14 = bf16[96,3072]{1,0:T(8,128)(2,1)S(1)} collective-permute-done((bf16[96,3072]{1,0:T(8,128)(2,1)S(1)}, bf16[96,3072]{1,0:T(8,128)(2,1)S(1)}, u32[]{:S(2)}, u32[]{:S(2)}) %collective-permute-start.14) | collective-permute-done | bytes 589856 | tf_op jit(solution)/shard_map/ppermute | solution.py:15
  344.4 12.8 %collective-permute-done.15 = bf16[96,3072]{1,0:T(8,128)(2,1)S(1)} collective-permute-done((bf16[96,3072]{1,0:T(8,128)(2,1)S(1)}, bf16[96,3072]{1,0:T(8,128)(2,1)S(1)}, u32[]{:S(2)}, u32[]{:S(2)}) %collective-permute-start.15) | collective-permute-done | bytes 589856 | tf_op jit(solution)/shard_map/ppermute | solution.py:15
  364.3 12.8 %collective-permute-done.16 = bf16[96,3072]{1,0:T(8,128)(2,1)S(1)} collective-permute-done((bf16[96,3072]{1,0:T(8,128)(2,1)S(1)}, bf16[96,3072]{1,0:T(8,128)(2,1)S(1)}, u32[]{:S(2)}, u32[]{:S(2)}) %collective-permute-start.16) | collective-permute-done | bytes 589856 | tf_op jit(solution)/shard_map/ppermute | solution.py:15
  384.4 12.6 %collective-permute-done.17 = bf16[96,3072]{1,0:T(8,128)(2,1)S(1)} collective-permute-done((bf16[96,3072]{1,0:T(8,128)(2,1)S(1)}, bf16[96,3072]{1,0:T(8,128)(2,1)S(1)}, u32[]{:S(2)}, u32[]{:S(2)}) %collective-permute-start.17) | collective-permute-done | bytes 589856 | tf_op jit(solution)/shard_map/ppermute | solution.py:15
  904.7 21.3 %collective-permute-done.35 = bf16[96,3072]{1,0:T(8,128)(2,1)} collective-permute-done((bf16[96,3072]{1,0:T(8,128)(2,1)}, bf16[96,3072]{1,0:T(8,128)(2,1)}, u32[]{:S(2)}, u32[]{:S(2)}) %collective-permute-start.35) | collective-permute-done | bytes 589856 | tf_op jit(solution)/shard_map/ppermute | solution.py:15
  979.8 43.4 %all-gather.15.cloned.1.call-done = bf16[1,768,3072]{2,1,0:T(8,128)(2,1)} async-done(((bf16[1,96,3072]{2,1,0:T(8,128)(2,1)}), bf16[1,768,3072]{2,1,0:T(8,128)(2,1)}) %all-gather.15.cloned.1.call-update) | async-done | bytes 4718608 | tf_op jit(solution)/shard_map/all_gather | solution.py:87
  1035.2 50.8 %all-gather.13.cloned.1.call-done = bf16[1,768,3072]{2,1,0:T(8,128)(2,1)} async-done(((bf16[1,96,3072]{2,1,0:T(8,128)(2,1)}), bf16[1,768,3072]{2,1,0:T(8,128)(2,1)}) %all-gather.13.cloned.1.call-update) | async-done | bytes 4718608 | tf_op jit(solution)/shard_map/all_gather | solution.py:87
  1092.6 51.1 %all-gather.9.cloned.1.call-done = bf16[1,768,3072]{2,1,0:T(8,128)(2,1)} async-done(((bf16[1,96,3072]{2,1,0:T(8,128)(2,1)}), bf16[1,768,3072]{2,1,0:T(8,128)(2,1)}) %all-gather.9.cloned.1.call-update) | async-done | bytes 4718608 | tf_op jit(solution)/shard_map/all_gather | solution.py:87
  (326 shorter events, 718.4 us)
Async XLA Ops:
  6.5 957.9 %all-gather.11.cloned.1.call-start = ((), (), s32[]{:S(2)}) async-start(), calls=%async_computation.5 | async-start | bytes 5308416 | tf_op jit(solution)/shard_map/all_gather | solution.py:87
  23.4 28.5 %collective-permute-start = (bf16[96,3072]{1,0:T(8,128)(2,1)}, bf16[96,3072]{1,0:T(8,128)(2,1)}, u32[]{:S(2)}, u32[]{:S(2)}) collective-permute-start(bf16[96,3072]{1,0:T(8,128)(2,1)} %fusion.246), channel_id=1, source_target_pairs={{0,8},{8,16},{16,24},{24,32},{32,40},{40,48},{48,56},{56,64},{64,7... | collective-permute-start | bytes 1769480 | tf_op jit(solution)/shard_map/ppermute | solution.py:15
  436.7 15.1 %collective-permute-start.19 = (bf16[96,3072]{1,0:T(8,128)(2,1)}, bf16[96,3072]{1,0:T(8,128)(2,1)}, u32[]{:S(2)}, u32[]{:S(2)}) collective-permute-start(bf16[96,3072]{1,0:T(8,128)(2,1)} %fusion.196), channel_id=1, source_target_pairs={{8,0},{16,8},{24,16},{32,24},{40,32},{48,40},{56,48},{64,56},{72,6... | collective-permute-start | bytes 1769480 | tf_op jit(solution)/shard_map/ppermute | solution.py:15
  465.4 15.1 %collective-permute-start.20 = (bf16[96,3072]{1,0:T(8,128)(2,1)}, bf16[96,3072]{1,0:T(8,128)(2,1)}, u32[]{:S(2)}, u32[]{:S(2)}) collective-permute-start(bf16[96,3072]{1,0:T(8,128)(2,1)} %fusion.199), channel_id=1, source_target_pairs={{8,0},{16,8},{24,16},{32,24},{40,32},{48,40},{56,48},{64,56},{72,6... | collective-permute-start | bytes 1769480 | tf_op jit(solution)/shard_map/ppermute | solution.py:15
  494.1 15.1 %collective-permute-start.21 = (bf16[96,3072]{1,0:T(8,128)(2,1)}, bf16[96,3072]{1,0:T(8,128)(2,1)}, u32[]{:S(2)}, u32[]{:S(2)}) collective-permute-start(bf16[96,3072]{1,0:T(8,128)(2,1)} %fusion.202), channel_id=1, source_target_pairs={{8,0},{16,8},{24,16},{32,24},{40,32},{48,40},{56,48},{64,56},{72,6... | collective-permute-start | bytes 1769480 | tf_op jit(solution)/shard_map/ppermute | solution.py:15
  522.8 15.1 %collective-permute-start.22 = (bf16[96,3072]{1,0:T(8,128)(2,1)}, bf16[96,3072]{1,0:T(8,128)(2,1)}, u32[]{:S(2)}, u32[]{:S(2)}) collective-permute-start(bf16[96,3072]{1,0:T(8,128)(2,1)} %fusion.205), channel_id=1, source_target_pairs={{8,0},{16,8},{24,16},{32,24},{40,32},{48,40},{56,48},{64,56},{72,6... | collective-permute-start | bytes 1769480 | tf_op jit(solution)/shard_map/ppermute | solution.py:15
  551.5 15.1 %collective-permute-start.23 = (bf16[96,3072]{1,0:T(8,128)(2,1)}, bf16[96,3072]{1,0:T(8,128)(2,1)}, u32[]{:S(2)}, u32[]{:S(2)}) collective-permute-start(bf16[96,3072]{1,0:T(8,128)(2,1)} %fusion.208), channel_id=1, source_target_pairs={{8,0},{16,8},{24,16},{32,24},{40,32},{48,40},{56,48},{64,56},{72,6... | collective-permute-start | bytes 1769480 | tf_op jit(solution)/shard_map/ppermute | solution.py:15
  580.2 15.1 %collective-permute-start.24 = (bf16[96,3072]{1,0:T(8,128)(2,1)}, bf16[96,3072]{1,0:T(8,128)(2,1)}, u32[]{:S(2)}, u32[]{:S(2)}) collective-permute-start(bf16[96,3072]{1,0:T(8,128)(2,1)} %fusion.211), channel_id=1, source_target_pairs={{8,0},{16,8},{24,16},{32,24},{40,32},{48,40},{56,48},{64,56},{72,6... | collective-permute-start | bytes 1769480 | tf_op jit(solution)/shard_map/ppermute | solution.py:15
  608.9 15.1 %collective-permute-start.25 = (bf16[96,3072]{1,0:T(8,128)(2,1)}, bf16[96,3072]{1,0:T(8,128)(2,1)}, u32[]{:S(2)}, u32[]{:S(2)}) collective-permute-start(bf16[96,3072]{1,0:T(8,128)(2,1)} %fusion.214), channel_id=1, source_target_pairs={{8,0},{16,8},{24,16},{32,24},{40,32},{48,40},{56,48},{64,56},{72,6... | collective-permute-start | bytes 1769480 | tf_op jit(solution)/shard_map/ppermute | solution.py:15
  637.6 15.1 %collective-permute-start.26 = (bf16[96,3072]{1,0:T(8,128)(2,1)}, bf16[96,3072]{1,0:T(8,128)(2,1)}, u32[]{:S(2)}, u32[]{:S(2)}) collective-permute-start(bf16[96,3072]{1,0:T(8,128)(2,1)} %fusion.217), channel_id=1, source_target_pairs={{8,0},{16,8},{24,16},{32,24},{40,32},{48,40},{56,48},{64,56},{72,6... | collective-permute-start | bytes 1769480 | tf_op jit(solution)/shard_map/ppermute | solution.py:15
  694.9 15.1 %collective-permute-start.28 = (bf16[96,3072]{1,0:T(8,128)(2,1)}, bf16[96,3072]{1,0:T(8,128)(2,1)}, u32[]{:S(2)}, u32[]{:S(2)}) collective-permute-start(bf16[96,3072]{1,0:T(8,128)(2,1)} %fusion.223), channel_id=1, source_target_pairs={{8,0},{16,8},{24,16},{32,24},{40,32},{48,40},{56,48},{64,56},{72,6... | collective-permute-start | bytes 1769480 | tf_op jit(solution)/shard_map/ppermute | solution.py:15
  752.3 15.1 %collective-permute-start.30 = (bf16[96,3072]{1,0:T(8,128)(2,1)}, bf16[96,3072]{1,0:T(8,128)(2,1)}, u32[]{:S(2)}, u32[]{:S(2)}) collective-permute-start(bf16[96,3072]{1,0:T(8,128)(2,1)} %fusion.229), channel_id=1, source_target_pairs={{8,0},{16,8},{24,16},{32,24},{40,32},{48,40},{56,48},{64,56},{72,6... | collective-permute-start | bytes 1769480 | tf_op jit(solution)/shard_map/ppermute | solution.py:15
  781.0 15.1 %collective-permute-start.31 = (bf16[96,3072]{1,0:T(8,128)(2,1)}, bf16[96,3072]{1,0:T(8,128)(2,1)}, u32[]{:S(2)}, u32[]{:S(2)}) collective-permute-start(bf16[96,3072]{1,0:T(8,128)(2,1)} %fusion.232), channel_id=1, source_target_pairs={{8,0},{16,8},{24,16},{32,24},{40,32},{48,40},{56,48},{64,56},{72,6... | collective-permute-start | bytes 1769480 | tf_op jit(solution)/shard_map/ppermute | solution.py:15
  809.7 15.1 %collective-permute-start.32 = (bf16[96,3072]{1,0:T(8,128)(2,1)}, bf16[96,3072]{1,0:T(8,128)(2,1)}, u32[]{:S(2)}, u32[]{:S(2)}) collective-permute-start(bf16[96,3072]{1,0:T(8,128)(2,1)} %fusion.235), channel_id=1, source_target_pairs={{8,0},{16,8},{24,16},{32,24},{40,32},{48,40},{56,48},{64,56},{72,6... | collective-permute-start | bytes 1769480 | tf_op jit(solution)/shard_map/ppermute | solution.py:15
  838.3 15.1 %collective-permute-start.33 = (bf16[96,3072]{1,0:T(8,128)(2,1)}, bf16[96,3072]{1,0:T(8,128)(2,1)}, u32[]{:S(2)}, u32[]{:S(2)}) collective-permute-start(bf16[96,3072]{1,0:T(8,128)(2,1)} %fusion.238), channel_id=1, source_target_pairs={{8,0},{16,8},{24,16},{32,24},{40,32},{48,40},{56,48},{64,56},{72,6... | collective-permute-start | bytes 1769480 | tf_op jit(solution)/shard_map/ppermute | solution.py:15
  867.3 15.1 %collective-permute-start.34 = (bf16[96,3072]{1,0:T(8,128)(2,1)}, bf16[96,3072]{1,0:T(8,128)(2,1)}, u32[]{:S(2)}, u32[]{:S(2)}) collective-permute-start(bf16[96,3072]{1,0:T(8,128)(2,1)} %fusion.241), channel_id=1, source_target_pairs={{8,0},{16,8},{24,16},{32,24},{40,32},{48,40},{56,48},{64,56},{72,6... | collective-permute-start | bytes 1769480 | tf_op jit(solution)/shard_map/ppermute | solution.py:15
  886.0 137.2 %all-gather.15.cloned.1.call-start = ((), (), s32[]{:S(2)}) async-start(), calls=%async_computation.7 | async-start | bytes 5308416 | tf_op jit(solution)/shard_map/all_gather | solution.py:87
  896.9 29.1 %collective-permute-start.35 = (bf16[96,3072]{1,0:T(8,128)(2,1)}, bf16[96,3072]{1,0:T(8,128)(2,1)}, u32[]{:S(2)}, u32[]{:S(2)}) collective-permute-start(bf16[96,3072]{1,0:T(8,128)(2,1)} %fusion.244), channel_id=1, source_target_pairs={{8,0},{16,8},{24,16},{32,24},{40,32},{48,40},{56,48},{64,56},{72,6... | collective-permute-start | bytes 1769480 | tf_op jit(solution)/shard_map/ppermute | solution.py:15
  931.2 154.8 %all-gather.13.cloned.1.call-start = ((), (), s32[]{:S(2)}) async-start(), calls=%async_computation.6 | async-start | bytes 5308416 | tf_op jit(solution)/shard_map/all_gather | solution.py:87
  931.9 211.8 %all-gather.9.cloned.1.call-start = ((), (), s32[]{:S(2)}) async-start(), calls=%async_computation.4 | async-start | bytes 5308416 | tf_op jit(solution)/shard_map/all_gather | solution.py:87
  938.6 21.2 %all-to-all-start.1 = ((bf16[96,8,384]{2,0,1:T(8,128)(2,1)}), bf16[96,8,384]{2,0,1:T(8,128)(2,1)}, u32[]{:S(2)}, u32[]{:S(2)}) async-start(bf16[96,8,384]{2,0,1:T(8,128)(2,1)} %fusion.397), calls=%async_computation.1 | async-start | bytes 1179648 | tf_op jit(solution)/shard_map/all_to_all | solution.py:86
  959.8 16.5 %all-to-all-start.3 = ((bf16[96,8,384]{2,0,1:T(8,128)(2,1)}), bf16[96,8,384]{2,0,1:T(8,128)(2,1)S(1)}, u32[]{:S(2)}, u32[]{:S(2)}) async-start(bf16[96,8,384]{2,0,1:T(8,128)(2,1)} %fusion.395), calls=%async_computation.3 | async-start | bytes 1179648 | tf_op jit(solution)/shard_map/all_to_all | solution.py:86
  976.3 53.5 %all-to-all-start.2 = ((bf16[96,8,384]{2,0,1:T(8,128)(2,1)}), bf16[96,8,384]{2,0,1:T(8,128)(2,1)S(1)}, u32[]{:S(2)}, u32[]{:S(2)}) async-start(bf16[96,8,384]{2,0,1:T(8,128)(2,1)} %fusion.396), calls=%async_computation.2 | async-start | bytes 1179648 | tf_op jit(solution)/shard_map/all_to_all | solution.py:86
  1029.7 62.9 %all-to-all-start = ((bf16[96,8,384]{2,0,1:T(8,128)(2,1)}), bf16[96,8,384]{2,0,1:T(8,128)(2,1)S(1)}, u32[]{:S(2)}, u32[]{:S(2)}) async-start(bf16[96,8,384]{2,0,1:T(8,128)(2,1)} %fusion.398), calls=%async_computation | async-start | bytes 1179648 | tf_op jit(solution)/shard_map/all_to_all | solution.py:86
  (44 other events, 568.7 us)
Sparse Core Ops, SparseCore 0:
  886.1 75.3 all-gather.10
  963.1 60.0 all-gather.14
  1024.8 61.0 all-gather.12
  1087.5 56.2 all-gather.8

commit v2 on v1

--- a/solution.py
+++ b/solution.py
@@ -9,10 +9,20 @@
 EPSILON = 1e-06
 
 
-def from_behind(array, axis, by):
-    count = lax.axis_size(axis)
-    pairs = [(i, i + by) for i in range(count) if 0 <= i + by < count]
-    return lax.ppermute(array, axis, pairs)
+def relay(array, by):
+    sections = lax.axis_size("pipe")
+    replicas = lax.axis_size("dp")
+    middle = sections // 2
+    pairs = []
+    for section in range(sections):
+        target = section + by
+        if not 0 <= target < sections:
+            continue
+        crossing = {section, target} == {middle - 1, middle}
+        for replica in range(replicas):
+            other = (replica + replicas // 2) % replicas if crossing else replica
+            pairs.append((section * replicas + replica, target * replicas + other))
+    return lax.ppermute(array, ("pipe", "dp"), pairs)
 
 
 def norm_factor(values):
@@ -61,8 +71,10 @@
         kept_inputs = lax.dynamic_update_index_in_dim(kept_inputs, source, slot, 0)
         kept_gates = lax.dynamic_update_index_in_dim(kept_gates, gate_value, slot, 0)
         if tick + 1 < ticks:
-            incoming = from_behind(output, "pipe", 1)
+            incoming = relay(output, 1)
 
+    half = replicas // 2
+    cotangent = lax.ppermute(cotangent, "dp", [(r, (r + half) % replicas) for r in range(replicas)])
     weight_t = with_layout_constraint(jnp.transpose(weight), Layout((0, 1)))
     kept_slopes = jnp.zeros((micro + 2, rows_mb, width), jnp.bfloat16)
     incoming = jnp.zeros((rows_mb, width), jnp.bfloat16)
@@ -78,13 +90,14 @@
         down, slope = backward_layer(stored_input, stored_gate, source, weight_t)
         kept_slopes = lax.dynamic_update_index_in_dim(kept_slopes, slope, slot, 0)
         if tick + 1 < ticks:
-            incoming = from_behind(down, "pipe", -1)
+            incoming = relay(down, -1)
         done = tick - (sections - 1)
         if done >= 0:
             floats, factor = norm_factor(kept_inputs[done + 1])
             normed = (floats * factor).astype(jnp.bfloat16)
             normed_cols = lax.all_to_all(normed, "dp", 1, 0, tiled=True)
-            slope_all = lax.all_gather(kept_slopes[done + 1], "dp", axis=0, tiled=True)
+            finished, kept_slopes = lax.optimization_barrier((kept_slopes[done + 1], kept_slopes))
+            slope_all = lax.all_gather(finished, "dp", axis=0, tiled=True)
             grad_rows = grad_rows + lax.dot_general(
                 normed_cols, slope_all, (((0,), (0,)), ((), ())), preferred_element_type=jnp.float32
             )

time: 1170 us -> 1090 us (0.932)
  waiting for transfers between devices: 521 us -> 439 us
  local copies, waits for them, and re-layouts: 39.2 us -> 65 us
  matrix products: 275 us -> 260 us
    all_gather x4, waiting for transfers between devices: 145 us -> 87.8 us  [on_device(): slope_all = lax.all_gather(finished, 'dp', axis=0, tiled=True)]
    ppermute x36 -> x37, waiting for transfers between devices: 361 us -> 323 us  [the longest x36 323 us: relay(): return lax.ppermute(array, ('pipe', 'dp'), pairs)]
    dynamic_update_slice x0 -> x18, local copies, waits for them, and re-layouts: none -> 19.7 us  [on_device(): lax.dynamic_update_index_in_dim(kept_gates, gate_value, slot, 0)]
    dot_general x19, matrix products: 95.9 us -> 79.8 us  [forward_layer(): gate_value = jnp.dot(normed, weight, preferred_element_type=jnp.float32)]
    all_to_all x4, waiting for transfers between devices: 14.1 us -> 28.3 us  [on_device(): normed_cols = lax.all_to_all(normed, 'dp', 1, 0, tiled=True)]
    ppermute x36 -> x37, starting transfers between devices: 167 us -> 163 us  [the longest x36 162 us: relay(): return lax.ppermute(array, ('pipe', 'dp'), pairs)]
    dynamic_update_slice x18 -> x19, other arithmetic: 52.8 us -> 56.1 us  [on_device(): kept_slopes = lax.dynamic_update_index_in_dim(kept_slopes, slope, slot, 0)]
    unnamed x53 -> x51, local copies, waits for them, and re-layouts: 30 us -> 33.3 us
  transfers between devices with their start and end apart: 44 -> 45, of which waited for: 40 -> 40; matrix products, arithmetic and copies ran while one was open for 7% -> 19% of each run, Pallas kernels for 0% -> 0%
where the time goes in v2:
time: 1090 us; the launch traced here: 1080 us
  waiting for transfers between devices  439 us (40%)
  matrix products  260 us (24%)
  starting transfers between devices  182 us (17%)
  other arithmetic  117 us (11%)
  local copies, waits for them, and re-layouts  65 us (6%)
  between operations  15.3 us (1%)
    ppermute x36, waiting for transfers between devices, relay(): return lax.ppermute(array, ('pipe', 'dp'), pairs)  323 us
    ppermute x36, starting transfers between devices, relay(): return lax.ppermute(array, ('pipe', 'dp'), pairs)  162 us
    dot_general x18, matrix products, backward_layer(): back = jnp.dot(slope, weight_t, preferred_element_type=jnp.float32)  149 us
    all_gather x4, waiting for transfers between devices, on_device(): slope_all = lax.all_gather(finished, 'dp', axis=0, tiled=True)  87.8 us
    dot_general x19, matrix products, forward_layer(): gate_value = jnp.dot(normed, weight, preferred_element_type=jnp.float32)  79.8 us
    dynamic_update_slice x19, other arithmetic, on_device(): kept_slopes = lax.dynamic_update_index_in_dim(kept_slopes, slope, slot, 0)  56.1 us
    convert_element_type x18, other arithmetic, backward_layer(): down = (up_float + factor * (back - unit * jnp.mean(back * unit, axis=-1,...  45 us
    unnamed x51, local copies, waits for them, and re-layouts  33.3 us
  transfers between devices with their start and end apart: 45, of which 40 were waited for; matrix products, arithmetic and copies ran while one was open for 19% of the time, Pallas kernels for 0%

profile of v2, /device:TPU:6, one launch (start us, length us, event | category | flops | bytes accessed | tf_op | source)
XLA Modules:
  0.0 1078.0 jit_solution(6463080919196691117)
XLA Ops:
  7.9 11.2 %fusion.234 = (bf16[96,3072]{1,0:T(8,128)(2,1)}, f32[96,3072]{1,0:T(8,128)}) fusion(bf16[4,96,3072]{2,1,0:T(8,128)(2,1)} %param.3, s32[]{:T(128)S(6)} %min.229, pred[]{:T(512)S(6)} %eq.4, bf16[1,3072,3072]{2,1,0:T(8,128)(2,1)} %param.4, f32[96]{0:T(128)S(1)} %add_rsqrt_fusion.40), kind=kOutput, calls=%fused_computation.358 | convolution fusion | flops 1815478272 | bytes 21825920 | tf_op jit(solution)/shard_map/dot_general | solution.py:37
  21.9 24.7 %copy.5 = bf16[1,3072,3072]{1,2,0:T(8,128)(2,1)} copy(bf16[1,3072,3072]{2,1,0:T(8,128)(2,1)} %param.4) | data formatting | bytes 37748736 | tf_op args[1]
  67.4 10.0 collective-permute-done.1
  84.9 10.9 %collective-permute-done.2 = bf16[96,3072]{1,0:T(8,128)(2,1)S(1)} collective-permute-done((bf16[96,3072]{1,0:T(8,128)(2,1)S(1)}, bf16[96,3072]{1,0:T(8,128)(2,1)S(1)}, u32[]{:S(2)}, u32[]{:S(2)}) %collective-permute-start.2) | collective-permute-done | bytes 589856 | tf_op jit(solution)/shard_map/ppermute | solution.py:25
  102.8 11.4 %collective-permute-done.3 = bf16[96,3072]{1,0:T(8,128)(2,1)S(1)} collective-permute-done((bf16[96,3072]{1,0:T(8,128)(2,1)S(1)}, bf16[96,3072]{1,0:T(8,128)(2,1)S(1)}, u32[]{:S(2)}, u32[]{:S(2)}) %collective-permute-start.3) | collective-permute-done | bytes 589856 | tf_op jit(solution)/shard_map/ppermute | solution.py:25
  121.1 11.4 %collective-permute-done.4 = bf16[96,3072]{1,0:T(8,128)(2,1)S(1)} collective-permute-done((bf16[96,3072]{1,0:T(8,128)(2,1)S(1)}, bf16[96,3072]{1,0:T(8,128)(2,1)S(1)}, u32[]{:S(2)}, u32[]{:S(2)}) %collective-permute-start.4) | collective-permute-done | bytes 589856 | tf_op jit(solution)/shard_map/ppermute | solution.py:25
  139.6 11.2 %collective-permute-done.5 = bf16[96,3072]{1,0:T(8,128)(2,1)S(1)} collective-permute-done((bf16[96,3072]{1,0:T(8,128)(2,1)S(1)}, bf16[96,3072]{1,0:T(8,128)(2,1)S(1)}, u32[]{:S(2)}, u32[]{:S(2)}) %collective-permute-start.5) | collective-permute-done | bytes 589856 | tf_op jit(solution)/shard_map/ppermute | solution.py:25
  157.8 11.4 %collective-permute-done.6 = bf16[96,3072]{1,0:T(8,128)(2,1)S(1)} collective-permute-done((bf16[96,3072]{1,0:T(8,128)(2,1)S(1)}, bf16[96,3072]{1,0:T(8,128)(2,1)S(1)}, u32[]{:S(2)}, u32[]{:S(2)}) %collective-permute-start.6) | collective-permute-done | bytes 589856 | tf_op jit(solution)/shard_map/ppermute | solution.py:25
  176.1 11.4 %collective-permute-done.7 = bf16[96,3072]{1,0:T(8,128)(2,1)S(1)} collective-permute-done((bf16[96,3072]{1,0:T(8,128)(2,1)S(1)}, bf16[96,3072]{1,0:T(8,128)(2,1)S(1)}, u32[]{:S(2)}, u32[]{:S(2)}) %collective-permute-start.7) | collective-permute-done | bytes 589856 | tf_op jit(solution)/shard_map/ppermute | solution.py:25
  194.7 11.2 %collective-permute-done.8 = bf16[96,3072]{1,0:T(8,128)(2,1)S(1)} collective-permute-done((bf16[96,3072]{1,0:T(8,128)(2,1)S(1)}, bf16[96,3072]{1,0:T(8,128)(2,1)S(1)}, u32[]{:S(2)}, u32[]{:S(2)}) %collective-permute-start.8) | collective-permute-done | bytes 589856 | tf_op jit(solution)/shard_map/ppermute | solution.py:25
  212.8 11.4 %collective-permute-done.9 = bf16[96,3072]{1,0:T(8,128)(2,1)S(1)} collective-permute-done((bf16[96,3072]{1,0:T(8,128)(2,1)S(1)}, bf16[96,3072]{1,0:T(8,128)(2,1)S(1)}, u32[]{:S(2)}, u32[]{:S(2)}) %collective-permute-start.9) | collective-permute-done | bytes 589856 | tf_op jit(solution)/shard_map/ppermute | solution.py:25
  231.2 11.4 %collective-permute-done.10 = bf16[96,3072]{1,0:T(8,128)(2,1)S(1)} collective-permute-done((bf16[96,3072]{1,0:T(8,128)(2,1)S(1)}, bf16[96,3072]{1,0:T(8,128)(2,1)S(1)}, u32[]{:S(2)}, u32[]{:S(2)}) %collective-permute-start.10) | collective-permute-done | bytes 589856 | tf_op jit(solution)/shard_map/ppermute | solution.py:25
  249.9 11.0 %collective-permute-done.11 = bf16[96,3072]{1,0:T(8,128)(2,1)S(1)} collective-permute-done((bf16[96,3072]{1,0:T(8,128)(2,1)S(1)}, bf16[96,3072]{1,0:T(8,128)(2,1)S(1)}, u32[]{:S(2)}, u32[]{:S(2)}) %collective-permute-start.11) | collective-permute-done | bytes 589856 | tf_op jit(solution)/shard_map/ppermute | solution.py:25
  267.9 11.3 %collective-permute-done.12 = bf16[96,3072]{1,0:T(8,128)(2,1)S(1)} collective-permute-done((bf16[96,3072]{1,0:T(8,128)(2,1)S(1)}, bf16[96,3072]{1,0:T(8,128)(2,1)S(1)}, u32[]{:S(2)}, u32[]{:S(2)}) %collective-permute-start.12) | collective-permute-done | bytes 589856 | tf_op jit(solution)/shard_map/ppermute | solution.py:25
  286.3 11.3 %collective-permute-done.13 = bf16[96,3072]{1,0:T(8,128)(2,1)S(1)} collective-permute-done((bf16[96,3072]{1,0:T(8,128)(2,1)S(1)}, bf16[96,3072]{1,0:T(8,128)(2,1)S(1)}, u32[]{:S(2)}, u32[]{:S(2)}) %collective-permute-start.13) | collective-permute-done | bytes 589856 | tf_op jit(solution)/shard_map/ppermute | solution.py:25
  304.8 11.2 %collective-permute-done.14 = bf16[96,3072]{1,0:T(8,128)(2,1)S(1)} collective-permute-done((bf16[96,3072]{1,0:T(8,128)(2,1)S(1)}, bf16[96,3072]{1,0:T(8,128)(2,1)S(1)}, u32[]{:S(2)}, u32[]{:S(2)}) %collective-permute-start.14) | collective-permute-done | bytes 589856 | tf_op jit(solution)/shard_map/ppermute | solution.py:25
  323.0 11.3 %collective-permute-done.15 = bf16[96,3072]{1,0:T(8,128)(2,1)S(1)} collective-permute-done((bf16[96,3072]{1,0:T(8,128)(2,1)S(1)}, bf16[96,3072]{1,0:T(8,128)(2,1)S(1)}, u32[]{:S(2)}, u32[]{:S(2)}) %collective-permute-start.15) | collective-permute-done | bytes 589856 | tf_op jit(solution)/shard_map/ppermute | solution.py:25
  341.3 11.3 %collective-permute-done.16 = bf16[96,3072]{1,0:T(8,128)(2,1)S(1)} collective-permute-done((bf16[96,3072]{1,0:T(8,128)(2,1)S(1)}, bf16[96,3072]{1,0:T(8,128)(2,1)S(1)}, u32[]{:S(2)}, u32[]{:S(2)}) %collective-permute-start.16) | collective-permute-done | bytes 589856 | tf_op jit(solution)/shard_map/ppermute | solution.py:25
  359.9 11.1 %collective-permute-done.17 = bf16[96,3072]{1,0:T(8,128)(2,1)S(1)} collective-permute-done((bf16[96,3072]{1,0:T(8,128)(2,1)S(1)}, bf16[96,3072]{1,0:T(8,128)(2,1)S(1)}, u32[]{:S(2)}, u32[]{:S(2)}) %collective-permute-start.17) | collective-permute-done | bytes 589856 | tf_op jit(solution)/shard_map/ppermute | solution.py:25
  376.1 10.6 fusion.253
  911.8 15.6 %all-to-all-done = bf16[96,8,384]{2,0,1:T(8,128)(2,1)} async-done(((bf16[96,8,384]{2,0,1:T(8,128)(2,1)}), bf16[96,8,384]{2,0,1:T(8,128)(2,1)}, u32[]{:S(2)}, u32[]{:S(2)}) %all-to-all-start) | async-done | bytes 589856 | tf_op jit(solution)/shard_map/all_to_all | solution.py:98
  966.2 38.2 %all-gather.9.cloned.1.call-done = bf16[768,3072]{1,0:T(8,128)(2,1)} async-done(((bf16[96,3072]{1,0:T(8,128)(2,1)}), bf16[768,3072]{1,0:T(8,128)(2,1)}) %all-gather.9.cloned.1.call-update) | async-done | bytes 4718608 | tf_op jit(solution)/shard_map/all_gather | solution.py:100
  1010.9 49.6 %all-gather.11.cloned.1.call-done = bf16[768,3072]{1,0:T(8,128)(2,1)} async-done(((bf16[96,3072]{1,0:T(8,128)(2,1)}), bf16[768,3072]{1,0:T(8,128)(2,1)}) %all-gather.11.cloned.1.call-update) | async-done | bytes 4718608 | tf_op jit(solution)/shard_map/all_gather | solution.py:100
  1060.5 10.4 fusion.74
  (329 shorter events, 711.8 us)
Async XLA Ops:
  6.5 925.2 %all-gather.5.cloned.1.call-start = ((), (), s32[]{:S(2)}) async-start(), calls=%async_computation.4 | async-start | bytes 5308416 | tf_op jit(solution)/shard_map/all_gather | solution.py:100
  19.1 33.6 %collective-permute-start = (bf16[96,3072]{1,0:T(8,128)(2,1)}, bf16[96,3072]{1,0:T(8,128)(2,1)}, u32[]{:S(2)}, u32[]{:S(2)}) collective-permute-start(bf16[96,3072]{1,0:T(8,128)(2,1)} %get-tuple-element.117), channel_id=1, source_target_pairs={{0,8},{1,9},{2,10},{3,11},{4,12},{5,13},{6,14},{7,15},{8,16},{9,17... | collective-permute-start | bytes 1769480 | tf_op jit(solution)/shard_map/ppermute | solution.py:25
  21.0 355.1 %collective-permute-start.18 = (bf16[4,96,3072]{2,1,0:T(8,128)(2,1)}, bf16[4,96,3072]{2,1,0:T(8,128)(2,1)}, u32[]{:S(2)}, u32[]{:S(2)}) collective-permute-start(bf16[4,96,3072]{2,1,0:T(8,128)(2,1)} %param.5), channel_id=1, source_target_pairs={{0,4},{1,5},{2,6},{3,7},{4,0},{5,1},{6,2},{7,3},{8,12},{9,13},{10,... | collective-permute-start | bytes 7077896 | tf_op jit(solution)/shard_map/ppermute | solution.py:77
  412.2 14.8 %collective-permute-start.20 = (bf16[96,3072]{1,0:T(8,128)(2,1)}, bf16[96,3072]{1,0:T(8,128)(2,1)}, u32[]{:S(2)}, u32[]{:S(2)}) collective-permute-start(bf16[96,3072]{1,0:T(8,128)(2,1)} %fusion.184), channel_id=1, source_target_pairs={{8,0},{9,1},{10,2},{11,3},{12,4},{13,5},{14,6},{15,7},{16,8},{17,9... | collective-permute-start | bytes 1769480 | tf_op jit(solution)/shard_map/ppermute | solution.py:25
  440.7 14.8 %collective-permute-start.21 = (bf16[96,3072]{1,0:T(8,128)(2,1)}, bf16[96,3072]{1,0:T(8,128)(2,1)}, u32[]{:S(2)}, u32[]{:S(2)}) collective-permute-start(bf16[96,3072]{1,0:T(8,128)(2,1)} %fusion.187), channel_id=1, source_target_pairs={{8,0},{9,1},{10,2},{11,3},{12,4},{13,5},{14,6},{15,7},{16,8},{17,9... | collective-permute-start | bytes 1769480 | tf_op jit(solution)/shard_map/ppermute | solution.py:25
  469.1 14.8 %collective-permute-start.22 = (bf16[96,3072]{1,0:T(8,128)(2,1)}, bf16[96,3072]{1,0:T(8,128)(2,1)}, u32[]{:S(2)}, u32[]{:S(2)}) collective-permute-start(bf16[96,3072]{1,0:T(8,128)(2,1)} %fusion.190), channel_id=1, source_target_pairs={{8,0},{9,1},{10,2},{11,3},{12,4},{13,5},{14,6},{15,7},{16,8},{17,9... | collective-permute-start | bytes 1769480 | tf_op jit(solution)/shard_map/ppermute | solution.py:25
  497.5 14.8 %collective-permute-start.23 = (bf16[96,3072]{1,0:T(8,128)(2,1)}, bf16[96,3072]{1,0:T(8,128)(2,1)}, u32[]{:S(2)}, u32[]{:S(2)}) collective-permute-start(bf16[96,3072]{1,0:T(8,128)(2,1)} %fusion.193), channel_id=1, source_target_pairs={{8,0},{9,1},{10,2},{11,3},{12,4},{13,5},{14,6},{15,7},{16,8},{17,9... | collective-permute-start | bytes 1769480 | tf_op jit(solution)/shard_map/ppermute | solution.py:25
  526.0 14.8 %collective-permute-start.24 = (bf16[96,3072]{1,0:T(8,128)(2,1)}, bf16[96,3072]{1,0:T(8,128)(2,1)}, u32[]{:S(2)}, u32[]{:S(2)}) collective-permute-start(bf16[96,3072]{1,0:T(8,128)(2,1)} %fusion.196), channel_id=1, source_target_pairs={{8,0},{9,1},{10,2},{11,3},{12,4},{13,5},{14,6},{15,7},{16,8},{17,9... | collective-permute-start | bytes 1769480 | tf_op jit(solution)/shard_map/ppermute | solution.py:25
  554.4 14.8 %collective-permute-start.25 = (bf16[96,3072]{1,0:T(8,128)(2,1)}, bf16[96,3072]{1,0:T(8,128)(2,1)}, u32[]{:S(2)}, u32[]{:S(2)}) collective-permute-start(bf16[96,3072]{1,0:T(8,128)(2,1)} %fusion.199), channel_id=1, source_target_pairs={{8,0},{9,1},{10,2},{11,3},{12,4},{13,5},{14,6},{15,7},{16,8},{17,9... | collective-permute-start | bytes 1769480 | tf_op jit(solution)/shard_map/ppermute | solution.py:25
  582.8 14.9 %collective-permute-start.26 = (bf16[96,3072]{1,0:T(8,128)(2,1)}, bf16[96,3072]{1,0:T(8,128)(2,1)}, u32[]{:S(2)}, u32[]{:S(2)}) collective-permute-start(bf16[96,3072]{1,0:T(8,128)(2,1)} %fusion.202), channel_id=1, source_target_pairs={{8,0},{9,1},{10,2},{11,3},{12,4},{13,5},{14,6},{15,7},{16,8},{17,9... | collective-permute-start | bytes 1769480 | tf_op jit(solution)/shard_map/ppermute | solution.py:25
  611.3 14.8 %collective-permute-start.27 = (bf16[96,3072]{1,0:T(8,128)(2,1)}, bf16[96,3072]{1,0:T(8,128)(2,1)}, u32[]{:S(2)}, u32[]{:S(2)}) collective-permute-start(bf16[96,3072]{1,0:T(8,128)(2,1)} %fusion.205), channel_id=1, source_target_pairs={{8,0},{9,1},{10,2},{11,3},{12,4},{13,5},{14,6},{15,7},{16,8},{17,9... | collective-permute-start | bytes 1769480 | tf_op jit(solution)/shard_map/ppermute | solution.py:25
  668.0 14.9 %collective-permute-start.29 = (bf16[96,3072]{1,0:T(8,128)(2,1)}, bf16[96,3072]{1,0:T(8,128)(2,1)}, u32[]{:S(2)}, u32[]{:S(2)}) collective-permute-start(bf16[96,3072]{1,0:T(8,128)(2,1)} %fusion.211), channel_id=1, source_target_pairs={{8,0},{9,1},{10,2},{11,3},{12,4},{13,5},{14,6},{15,7},{16,8},{17,9... | collective-permute-start | bytes 1769480 | tf_op jit(solution)/shard_map/ppermute | solution.py:25
  724.8 14.8 %collective-permute-start.31 = (bf16[96,3072]{1,0:T(8,128)(2,1)}, bf16[96,3072]{1,0:T(8,128)(2,1)}, u32[]{:S(2)}, u32[]{:S(2)}) collective-permute-start(bf16[96,3072]{1,0:T(8,128)(2,1)} %fusion.217), channel_id=1, source_target_pairs={{8,0},{9,1},{10,2},{11,3},{12,4},{13,5},{14,6},{15,7},{16,8},{17,9... | collective-permute-start | bytes 1769480 | tf_op jit(solution)/shard_map/ppermute | solution.py:25
  753.2 14.8 %collective-permute-start.32 = (bf16[96,3072]{1,0:T(8,128)(2,1)}, bf16[96,3072]{1,0:T(8,128)(2,1)}, u32[]{:S(2)}, u32[]{:S(2)}) collective-permute-start(bf16[96,3072]{1,0:T(8,128)(2,1)} %fusion.220), channel_id=1, source_target_pairs={{8,0},{9,1},{10,2},{11,3},{12,4},{13,5},{14,6},{15,7},{16,8},{17,9... | collective-permute-start | bytes 1769480 | tf_op jit(solution)/shard_map/ppermute | solution.py:25
  781.6 14.8 %collective-permute-start.33 = (bf16[96,3072]{1,0:T(8,128)(2,1)}, bf16[96,3072]{1,0:T(8,128)(2,1)}, u32[]{:S(2)}, u32[]{:S(2)}) collective-permute-start(bf16[96,3072]{1,0:T(8,128)(2,1)} %fusion.223), channel_id=1, source_target_pairs={{8,0},{9,1},{10,2},{11,3},{12,4},{13,5},{14,6},{15,7},{16,8},{17,9... | collective-permute-start | bytes 1769480 | tf_op jit(solution)/shard_map/ppermute | solution.py:25
  801.5 144.9 %all-gather.7.cloned.1.call-start = ((), (), s32[]{:S(2)}) async-start(), calls=%async_computation.5 | async-start | bytes 5308416 | tf_op jit(solution)/shard_map/all_gather | solution.py:100
  812.3 14.8 %collective-permute-start.34 = (bf16[96,3072]{1,0:T(8,128)(2,1)}, bf16[96,3072]{1,0:T(8,128)(2,1)}, u32[]{:S(2)}, u32[]{:S(2)}) collective-permute-start(bf16[96,3072]{1,0:T(8,128)(2,1)} %fusion.226), channel_id=1, source_target_pairs={{8,0},{9,1},{10,2},{11,3},{12,4},{13,5},{14,6},{15,7},{16,8},{17,9... | collective-permute-start | bytes 1769480 | tf_op jit(solution)/shard_map/ppermute | solution.py:25
  832.3 172.2 %all-gather.9.cloned.1.call-start = ((), (), s32[]{:S(2)}) async-start(), calls=%async_computation.6 | async-start | bytes 5308416 | tf_op jit(solution)/shard_map/all_gather | solution.py:100
  843.4 14.8 %collective-permute-start.35 = (bf16[96,3072]{1,0:T(8,128)(2,1)}, bf16[96,3072]{1,0:T(8,128)(2,1)}, u32[]{:S(2)}, u32[]{:S(2)}) collective-permute-start(bf16[96,3072]{1,0:T(8,128)(2,1)} %fusion.229), channel_id=1, source_target_pairs={{8,0},{9,1},{10,2},{11,3},{12,4},{13,5},{14,6},{15,7},{16,8},{17,9... | collective-permute-start | bytes 1769480 | tf_op jit(solution)/shard_map/ppermute | solution.py:25
  863.2 197.3 %all-gather.11.cloned.1.call-start = ((), (), s32[]{:S(2)}) async-start(), calls=%async_computation.7 | async-start | bytes 5308416 | tf_op jit(solution)/shard_map/all_gather | solution.py:100
  874.1 14.8 %collective-permute-start.36 = (bf16[96,3072]{1,0:T(8,128)(2,1)}, bf16[96,3072]{1,0:T(8,128)(2,1)}, u32[]{:S(2)}, u32[]{:S(2)}) collective-permute-start(bf16[96,3072]{1,0:T(8,128)(2,1)} %fusion.232), channel_id=1, source_target_pairs={{8,0},{9,1},{10,2},{11,3},{12,4},{13,5},{14,6},{15,7},{16,8},{17,9... | collective-permute-start | bytes 1769480 | tf_op jit(solution)/shard_map/ppermute | solution.py:25
  899.9 27.5 %all-to-all-start = ((bf16[96,8,384]{2,0,1:T(8,128)(2,1)}), bf16[96,8,384]{2,0,1:T(8,128)(2,1)}, u32[]{:S(2)}, u32[]{:S(2)}) async-start(bf16[96,8,384]{2,0,1:T(8,128)(2,1)} %fusion.386), calls=%async_computation | async-start | bytes 1179648 | tf_op jit(solution)/shard_map/all_to_all | solution.py:98
  942.2 19.9 %all-to-all-start.2 = ((bf16[96,8,384]{2,0,1:T(8,128)(2,1)}), bf16[96,8,384]{2,0,1:T(8,128)(2,1)S(1)}, u32[]{:S(2)}, u32[]{:S(2)}) async-start(bf16[96,8,384]{2,0,1:T(8,128)(2,1)} %fusion.384), calls=%async_computation.2 | async-start | bytes 1179648 | tf_op jit(solution)/shard_map/all_to_all | solution.py:98
  962.0 48.9 %all-to-all-start.3 = ((bf16[96,8,384]{2,0,1:T(8,128)(2,1)}), bf16[96,8,384]{2,0,1:T(8,128)(2,1)S(1)}, u32[]{:S(2)}, u32[]{:S(2)}) async-start(bf16[96,8,384]{2,0,1:T(8,128)(2,1)} %fusion.383), calls=%async_computation.3 | async-start | bytes 1179648 | tf_op jit(solution)/shard_map/all_to_all | solution.py:98
  (44 other events, 554.5 us)
Sparse Core Ops, SparseCore 0:
  801.6 59.0 all-gather.4
  862.3 68.7 all-gather.6
  932.8 71.5 all-gather.8
  1005.9 54.5 all-gather.10

commit v3 on v2

--- a/solution.py
+++ b/solution.py
@@ -3,7 +3,6 @@
 import jax
 import jax.numpy as jnp
 from jax import lax
-from jax.experimental.layout import Layout, with_layout_constraint
 from jax.sharding import PartitionSpec as P
 
 EPSILON = 1e-06
@@ -62,6 +61,9 @@
     kept_inputs = jnp.zeros((micro + 2, rows_mb, width), jnp.bfloat16)
     kept_gates = jnp.zeros((micro + 2, rows_mb, width), jnp.float32)
     incoming = jnp.zeros((rows_mb, width), jnp.bfloat16)
+    pieces = sections
+    piece = width // pieces
+    weight_t = jnp.zeros((width, width), jnp.bfloat16)
     for tick in range(ticks):
         batch = tick - section
         slot = jnp.clip(batch + 1, 0, micro + 1)
@@ -72,10 +74,13 @@
         kept_gates = lax.dynamic_update_index_in_dim(kept_gates, gate_value, slot, 0)
         if tick + 1 < ticks:
             incoming = relay(output, 1)
+        if tick < pieces:
+            block = jnp.transpose(lax.slice_in_dim(weight, tick * piece, (tick + 1) * piece, axis=0))
+            weight_t = lax.dynamic_update_slice_in_dim(weight_t, block, tick * piece, axis=1)
+            weight_t, incoming = lax.optimization_barrier((weight_t, incoming))
 
     half = replicas // 2
     cotangent = lax.ppermute(cotangent, "dp", [(r, (r + half) % replicas) for r in range(replicas)])
-    weight_t = with_layout_constraint(jnp.transpose(weight), Layout((0, 1)))
     kept_slopes = jnp.zeros((micro + 2, rows_mb, width), jnp.bfloat16)
     incoming = jnp.zeros((rows_mb, width), jnp.bfloat16)
     cols = width // replicas

time: 1090 us -> 1160 us (1.064)
  matrix products: 260 us -> 351 us
  waiting for transfers between devices: 439 us -> 405 us
    dot_general x18, matrix products: 149 us -> 246 us  [backward_layer(): back = jnp.dot(slope, weight_t, preferred_element_type=jnp.float32)]
    unnamed x51 -> x52, local copies, waits for them, and re-layouts: 33.3 us -> 5.02 us
    dynamic_update_slice x0 -> x16, local copies, waits for them, and re-layouts: none -> 27 us  [on_device(): lax.dynamic_update_slice_in_dim(weight_t, block, tick * piece, axis=1)]
    ppermute x36, waiting for transfers between devices: 323 us -> 305 us  [relay(): return lax.ppermute(array, ('pipe', 'dp'), pairs)]
    all_gather x4, waiting for transfers between devices: 87.8 us -> 71.8 us  [on_device(): slope_all = lax.all_gather(finished, 'dp', axis=0, tiled=True)]
  transfers between devices with their start and end apart: 45 -> 45, of which waited for: 40 -> 40; matrix products, arithmetic and copies ran while one was open for 19% -> 20% of each run, Pallas kernels for 0% -> 0%
where the time goes in v3:
time: 1160 us; the launch traced here: 1150 us
  waiting for transfers between devices  405 us (35%)
  matrix products  351 us (30%)
  starting transfers between devices  183 us (16%)
  other arithmetic  126 us (11%)
  local copies, waits for them, and re-layouts  70 us (6%)
  between operations  15.2 us (1%)
    ppermute x36, waiting for transfers between devices, relay(): return lax.ppermute(array, ('pipe', 'dp'), pairs)  305 us
    dot_general x18, matrix products, backward_layer(): back = jnp.dot(slope, weight_t, preferred_element_type=jnp.float32)  246 us
    ppermute x36, starting transfers between devices, relay(): return lax.ppermute(array, ('pipe', 'dp'), pairs)  163 us
    dot_general x19, matrix products, forward_layer(): gate_value = jnp.dot(normed, weight, preferred_element_type=jnp.float32)  75 us
    all_gather x4, waiting for transfers between devices, on_device(): slope_all = lax.all_gather(finished, 'dp', axis=0, tiled=True)  71.8 us
    dynamic_update_slice x19, other arithmetic, on_device(): kept_slopes = lax.dynamic_update_index_in_dim(kept_slopes, slope, slot, 0)  59.3 us
    convert_element_type x18, other arithmetic, backward_layer(): down = (up_float + factor * (back - unit * jnp.mean(back * unit, axis=-1,...  50.7 us
    dot_general x4, matrix products, on_device(): lax.dot_general(normed_cols, slope_all, (((0,), (0,)), ((), ())), preferr...  30.1 us
  transfers between devices with their start and end apart: 45, of which 40 were waited for; matrix products, arithmetic and copies ran while one was open for 20% of the time, Pallas kernels for 0%

profile of v3, /device:TPU:6, one launch (start us, length us, event | category | flops | bytes accessed | tf_op | source)
XLA Modules:
  0.0 1150.2 jit_solution(17903061134257569995)
XLA Ops:
  7.9 11.2 fusion.198
  325.7 11.3 collective-permute-done.16
  344.3 11.1 collective-permute-done.17
  360.5 13.6 %fusion.217 = (f32[96]{0:T(128)S(1)}, f32[96]{0:T(128)S(1)}, f32[96]{0:T(128)}, f32[96]{0:T(128)}, f32[96]{0:T(128)}, /*index=5*/f32[96]{0:T(128)}, f32[96]{0:T(...) fusion(bf16[6,96,3072]{2,1,0:T(8,128)(2,1)S(1)} %bitcast_dynami, ...), kind=kOutput, calls=%fused_computation.341 | convolution fusion | flops 1829632000 | bytes 31276928 | tf_op jit(solution)/shard_map/dot_general | solution.py:46
  389.5 13.8 %fusion.202 = (f32[96]{0:T(128)S(1)}, f32[96]{0:T(128)S(1)}, f32[96,3072]{1,0:T(8,128)}) fusion(bf16[6,96,3072]{2,1,0:T(8,128)(2,1)S(1)} %bitcast_dynamic-update-slice_fusion.51, s32[]{:T(128)S(6)} %min.272, f32[96]{0:T(128)S(1)} %add_rsqrt_fusion.19, s32[]{:T(128)S(6)} %min.270, bf16[96,3072]{1,0:T(8,128)(2,1)} %get-tuple-element.140, ...), kind=kOutput, calls=%fused_computation.326 | convolution fusion | flops 1814003456 | bytes 21824648 | tf_op jit(solution)/shard_map/dot_general | solution.py:46
  424.1 13.6 %fusion.130 = (f32[96]{0:T(128)S(1)}, f32[96,3072]{1,0:T(8,128)}) fusion(f32[96]{0:T(128)S(1)} %add_rsqrt_fusion.18, bf16[6,96,3072]{2,1,0:T(8,128)(2,1)S(1)} %bitcast_dynamic-update-slice_fusion.51, s32[]{:T(128)S(6)} %min.272, bf16[96,3072]{1,0:T(8,128)(2,1)} %get-tuple-element.138, bf16[3072,3072]{0,1:T(8,128)(2,1)} %bitcast_dynamic-update-slice_fusion), kind=kOutput, calls=%fused_computation.254 | convolution fusion | flops 1813118848 | bytes 21234436 | tf_op jit(solution)/shard_map/dot_general | solution.py:46
  458.6 13.6 %fusion.127 = (f32[96]{0:T(128)S(1)}, f32[96,3072]{1,0:T(8,128)}) fusion(f32[96]{0:T(128)S(1)} %add_rsqrt_fusion.17, bf16[6,96,3072]{2,1,0:T(8,128)(2,1)S(1)} %bitcast_dynamic-update-slice_fusion.51, s32[]{:T(128)S(6)} %min.274, bf16[96,3072]{1,0:T(8,128)(2,1)} %get-tuple-element.136, bf16[3072,3072]{0,1:T(8,128)(2,1)} %bitcast_dynamic-update-slice_fusion), kind=kOutput, calls=%fused_computation.251 | convolution fusion | flops 1813118848 | bytes 21234436 | tf_op jit(solution)/shard_map/dot_general | solution.py:46
  493.1 13.6 %fusion.124 = (f32[96]{0:T(128)S(1)}, f32[96,3072]{1,0:T(8,128)}) fusion(f32[96]{0:T(128)S(1)} %add_rsqrt_fusion.16, bf16[6,96,3072]{2,1,0:T(8,128)(2,1)S(1)} %bitcast_dynamic-update-slice_fusion.51, s32[]{:T(128)S(6)} %min.276, bf16[96,3072]{1,0:T(8,128)(2,1)} %get-tuple-element.134, bf16[3072,3072]{0,1:T(8,128)(2,1)} %bitcast_dynamic-update-slice_fusion), kind=kOutput, calls=%fused_computation.248 | convolution fusion | flops 1813118848 | bytes 21234436 | tf_op jit(solution)/shard_map/dot_general | solution.py:46
  527.5 13.6 %fusion.121 = (f32[96]{0:T(128)S(1)}, f32[96,3072]{1,0:T(8,128)}) fusion(f32[96]{0:T(128)S(1)} %add_rsqrt_fusion.15, bf16[6,96,3072]{2,1,0:T(8,128)(2,1)S(1)} %bitcast_dynamic-update-slice_fusion.51, s32[]{:T(128)S(6)} %min.278, bf16[96,3072]{1,0:T(8,128)(2,1)} %get-tuple-element.132, bf16[3072,3072]{0,1:T(8,128)(2,1)} %bitcast_dynamic-update-slice_fusion), kind=kOutput, calls=%fused_computation.245 | convolution fusion | flops 1813118848 | bytes 21234436 | tf_op jit(solution)/shard_map/dot_general | solution.py:46
  562.0 13.6 %fusion.118 = (f32[96]{0:T(128)S(1)}, f32[96,3072]{1,0:T(8,128)}) fusion(f32[96]{0:T(128)S(1)} %add_rsqrt_fusion.14, bf16[6,96,3072]{2,1,0:T(8,128)(2,1)S(1)} %bitcast_dynamic-update-slice_fusion.51, s32[]{:T(128)S(6)} %min.280, bf16[96,3072]{1,0:T(8,128)(2,1)} %get-tuple-element.130, bf16[3072,3072]{0,1:T(8,128)(2,1)} %bitcast_dynamic-update-slice_fusion), kind=kOutput, calls=%fused_computation.242 | convolution fusion | flops 1813118848 | bytes 21234436 | tf_op jit(solution)/shard_map/dot_general | solution.py:46
  596.4 13.6 %fusion.115 = (f32[96]{0:T(128)S(1)}, f32[96,3072]{1,0:T(8,128)}) fusion(f32[96]{0:T(128)S(1)} %add_rsqrt_fusion.13, bf16[6,96,3072]{2,1,0:T(8,128)(2,1)S(1)} %bitcast_dynamic-update-slice_fusion.51, s32[]{:T(128)S(6)} %min.282, bf16[96,3072]{1,0:T(8,128)(2,1)} %get-tuple-element.128, bf16[3072,3072]{0,1:T(8,128)(2,1)} %bitcast_dynamic-update-slice_fusion), kind=kOutput, calls=%fused_computation.239 | convolution fusion | flops 1813118848 | bytes 21234436 | tf_op jit(solution)/shard_map/dot_general | solution.py:46
  631.0 13.6 %fusion.112 = (f32[96]{0:T(128)S(1)}, f32[96,3072]{1,0:T(8,128)}) fusion(f32[96]{0:T(128)S(1)} %add_rsqrt_fusion.12, bf16[6,96,3072]{2,1,0:T(8,128)(2,1)S(1)} %bitcast_dynamic-update-slice_fusion.51, s32[]{:T(128)S(6)} %min.284, bf16[96,3072]{1,0:T(8,128)(2,1)} %get-tuple-element.126, bf16[3072,3072]{0,1:T(8,128)(2,1)} %bitcast_dynamic-update-slice_fusion), kind=kOutput, calls=%fused_computation.236 | convolution fusion | flops 1813118848 | bytes 21234436 | tf_op jit(solution)/shard_map/dot_general | solution.py:46
  665.4 13.6 %fusion.109 = (f32[96]{0:T(128)S(1)}, f32[96,3072]{1,0:T(8,128)}) fusion(f32[96]{0:T(128)S(1)} %add_rsqrt_fusion.11, bf16[6,96,3072]{2,1,0:T(8,128)(2,1)S(1)} %bitcast_dynamic-update-slice_fusion.51, s32[]{:T(128)S(6)} %min.286, bf16[96,3072]{1,0:T(8,128)(2,1)} %get-tuple-element.124, bf16[3072,3072]{0,1:T(8,128)(2,1)} %bitcast_dynamic-update-slice_fusion), kind=kOutput, calls=%fused_computation.233 | convolution fusion | flops 1813118848 | bytes 21234436 | tf_op jit(solution)/shard_map/dot_general | solution.py:46
  699.8 13.6 %fusion.106 = (f32[96]{0:T(128)S(1)}, f32[96,3072]{1,0:T(8,128)}) fusion(f32[96]{0:T(128)S(1)} %add_rsqrt_fusion.10, bf16[6,96,3072]{2,1,0:T(8,128)(2,1)S(1)} %bitcast_dynamic-update-slice_fusion.51, s32[]{:T(128)S(6)} %min.288, bf16[96,3072]{1,0:T(8,128)(2,1)} %get-tuple-element.122, bf16[3072,3072]{0,1:T(8,128)(2,1)} %bitcast_dynamic-update-slice_fusion), kind=kOutput, calls=%fused_computation.230 | convolution fusion | flops 1813118848 | bytes 21234436 | tf_op jit(solution)/shard_map/dot_general | solution.py:46
  734.3 13.6 %fusion.103 = (f32[96]{0:T(128)S(1)}, f32[96,3072]{1,0:T(8,128)}) fusion(f32[96]{0:T(128)S(1)} %add_rsqrt_fusion.9, bf16[6,96,3072]{2,1,0:T(8,128)(2,1)S(1)} %bitcast_dynamic-update-slice_fusion.51, s32[]{:T(128)S(6)} %min.290, bf16[96,3072]{1,0:T(8,128)(2,1)} %get-tuple-element.120, bf16[3072,3072]{0,1:T(8,128)(2,1)} %bitcast_dynamic-update-slice_fusion), kind=kOutput, calls=%fused_computation.227 | convolution fusion | flops 1813118848 | bytes 21234436 | tf_op jit(solution)/shard_map/dot_general | solution.py:46
  768.7 13.6 %fusion.100 = (f32[96]{0:T(128)S(1)}, f32[96,3072]{1,0:T(8,128)}) fusion(f32[96]{0:T(128)S(1)} %add_rsqrt_fusion.8, bf16[6,96,3072]{2,1,0:T(8,128)(2,1)S(1)} %bitcast_dynamic-update-slice_fusion.51, s32[]{:T(128)S(6)} %min.292, bf16[96,3072]{1,0:T(8,128)(2,1)} %get-tuple-element.118, bf16[3072,3072]{0,1:T(8,128)(2,1)} %bitcast_dynamic-update-slice_fusion), kind=kOutput, calls=%fused_computation.224 | convolution fusion | flops 1813118848 | bytes 21234436 | tf_op jit(solution)/shard_map/dot_general | solution.py:46
  803.2 13.6 %fusion.97 = (f32[96]{0:T(128)S(1)}, f32[96,3072]{1,0:T(8,128)}) fusion(f32[96]{0:T(128)S(1)} %add_rsqrt_fusion.7, bf16[6,96,3072]{2,1,0:T(8,128)(2,1)S(1)} %bitcast_dynamic-update-slice_fusion.51, s32[]{:T(128)S(6)} %min.294, bf16[96,3072]{1,0:T(8,128)(2,1)} %get-tuple-element.116, bf16[3072,3072]{0,1:T(8,128)(2,1)} %bitcast_dynamic-update-slice_fusion), kind=kOutput, calls=%fused_computation.221 | convolution fusion | flops 1813118848 | bytes 21234436 | tf_op jit(solution)/shard_map/dot_general | solution.py:46
  837.7 13.6 %fusion.94 = (f32[96]{0:T(128)S(1)}, f32[96,3072]{1,0:T(8,128)}) fusion(f32[96]{0:T(128)S(1)} %add_rsqrt_fusion.6, bf16[6,96,3072]{2,1,0:T(8,128)(2,1)S(1)} %bitcast_dynamic-update-slice_fusion.51, s32[]{:T(128)S(6)} %min.296, bf16[96,3072]{1,0:T(8,128)(2,1)} %get-tuple-element.114, bf16[3072,3072]{0,1:T(8,128)(2,1)} %bitcast_dynamic-update-slice_fusion), kind=kOutput, calls=%fused_computation.218 | convolution fusion | flops 1813118848 | bytes 21234436 | tf_op jit(solution)/shard_map/dot_general | solution.py:46
  874.3 13.6 %fusion.91 = (f32[96]{0:T(128)S(1)}, f32[96,3072]{1,0:T(8,128)}) fusion(f32[96]{0:T(128)S(1)} %add_rsqrt_fusion.4, bf16[6,96,3072]{2,1,0:T(8,128)(2,1)S(1)} %bitcast_dynamic-update-slice_fusion.51, s32[]{:T(128)S(6)} %min.298, bf16[96,3072]{1,0:T(8,128)(2,1)} %get-tuple-element.112, bf16[3072,3072]{0,1:T(8,128)(2,1)} %bitcast_dynamic-update-slice_fusion), kind=kOutput, calls=%fused_computation.215 | convolution fusion | flops 1813118848 | bytes 21234436 | tf_op jit(solution)/shard_map/dot_general | solution.py:46
  910.9 13.8 %fusion.88 = (f32[96]{0:T(128)S(1)}, f32[96,3072]{1,0:T(8,128)}) fusion(f32[96]{0:T(128)S(1)} %add_rsqrt_fusion.2, bf16[6,96,3072]{2,1,0:T(8,128)(2,1)S(1)} %bitcast_dynamic-update-slice_fusion.51, s32[]{:T(128)S(6)} %min.300, bf16[96,3072]{1,0:T(8,128)(2,1)} %get-tuple-element.110, bf16[3072,3072]{0,1:T(8,128)(2,1)} %bitcast_dynamic-update-slice_fusion), kind=kOutput, calls=%fused_computation.212 | convolution fusion | flops 1813118848 | bytes 21234436 | tf_op jit(solution)/shard_map/dot_general | solution.py:46
  947.9 13.8 %fusion.85 = (f32[96]{0:T(128)S(1)}, f32[96,3072]{1,0:T(8,128)}) fusion(f32[96]{0:T(128)S(1)} %add_rsqrt_fusion, bf16[6,96,3072]{2,1,0:T(8,128)(2,1)S(1)} %bitcast_dynamic-update-slice_fusion.51, s32[]{:T(128)S(6)} %min.302, bf16[96,3072]{1,0:T(8,128)(2,1)} %get-tuple-element.108, bf16[3072,3072]{0,1:T(8,128)(2,1)} %bitcast_dynamic-update-slice_fusion), kind=kOutput, calls=%fused_computation.209 | convolution fusion | flops 1813118848 | bytes 21234436 | tf_op jit(solution)/shard_map/dot_general | solution.py:46
  1018.8 13.4 %all-to-all-done.1 = bf16[96,8,384]{2,0,1:T(8,128)(2,1)S(1)} async-done(((bf16[96,8,384]{2,0,1:T(8,128)(2,1)}), bf16[96,8,384]{2,0,1:T(8,128)(2,1)S(1)}, u32[]{:S(2)}, u32[]{:S(2)}) %all-to-all-start.1) | async-done | bytes 589856 | tf_op jit(solution)/shard_map/all_to_all | solution.py:103
  1054.5 22.2 %all-gather.9.cloned.1.call-done = bf16[768,3072]{1,0:T(8,128)(2,1)} async-done(((bf16[96,3072]{1,0:T(8,128)(2,1)}), bf16[768,3072]{1,0:T(8,128)(2,1)}) %all-gather.9.cloned.1.call-update) | async-done | bytes 4718608 | tf_op jit(solution)/shard_map/all_gather | solution.py:105
  1083.1 49.6 %all-gather.11.cloned.1.call-done = bf16[768,3072]{1,0:T(8,128)(2,1)} async-done(((bf16[96,3072]{1,0:T(8,128)(2,1)}), bf16[768,3072]{1,0:T(8,128)(2,1)}) %all-gather.11.cloned.1.call-update) | async-done | bytes 4718608 | tf_op jit(solution)/shard_map/all_gather | solution.py:105
  (347 shorter events, 770.1 us)
Async XLA Ops:
  6.5 1005.7 %all-gather.5.cloned.1.call-start = ((), (), s32[]{:S(2)}) async-start(), calls=%async_computation.4 | async-start | bytes 5308416 | tf_op jit(solution)/shard_map/all_gather | solution.py:105
  19.1 22.2 %collective-permute-start = (bf16[96,3072]{1,0:T(8,128)(2,1)}, bf16[96,3072]{1,0:T(8,128)(2,1)}, u32[]{:S(2)}, u32[]{:S(2)}) collective-permute-start(bf16[96,3072]{1,0:T(8,128)(2,1)} %get-tuple-element.181), channel_id=1, source_target_pairs={{0,8},{1,9},{2,10},{3,11},{4,12},{5,13},{6,14},{7,15},{8,16},{9,17... | collective-permute-start | bytes 1769480 | tf_op jit(solution)/shard_map/ppermute | solution.py:24
  21.0 339.4 %collective-permute-start.18 = (bf16[4,96,3072]{2,1,0:T(8,128)(2,1)}, bf16[4,96,3072]{2,1,0:T(8,128)(2,1)}, u32[]{:S(2)}, u32[]{:S(2)}) collective-permute-start(bf16[4,96,3072]{2,1,0:T(8,128)(2,1)} %param.5), channel_id=1, source_target_pairs={{0,4},{1,5},{2,6},{3,7},{4,0},{5,1},{6,2},{7,3},{8,12},{9,13},{10,... | collective-permute-start | bytes 7077896 | tf_op jit(solution)/shard_map/ppermute | solution.py:83
  406.1 14.8 %collective-permute-start.20 = (bf16[96,3072]{1,0:T(8,128)(2,1)}, bf16[96,3072]{1,0:T(8,128)(2,1)}, u32[]{:S(2)}, u32[]{:S(2)}) collective-permute-start(bf16[96,3072]{1,0:T(8,128)(2,1)} %fusion.148), channel_id=1, source_target_pairs={{8,0},{9,1},{10,2},{11,3},{12,4},{13,5},{14,6},{15,7},{16,8},{17,9... | collective-permute-start | bytes 1769480 | tf_op jit(solution)/shard_map/ppermute | solution.py:24
  440.6 14.8 %collective-permute-start.21 = (bf16[96,3072]{1,0:T(8,128)(2,1)}, bf16[96,3072]{1,0:T(8,128)(2,1)}, u32[]{:S(2)}, u32[]{:S(2)}) collective-permute-start(bf16[96,3072]{1,0:T(8,128)(2,1)} %fusion.151), channel_id=1, source_target_pairs={{8,0},{9,1},{10,2},{11,3},{12,4},{13,5},{14,6},{15,7},{16,8},{17,9... | collective-permute-start | bytes 1769480 | tf_op jit(solution)/shard_map/ppermute | solution.py:24
  475.1 14.8 %collective-permute-start.22 = (bf16[96,3072]{1,0:T(8,128)(2,1)}, bf16[96,3072]{1,0:T(8,128)(2,1)}, u32[]{:S(2)}, u32[]{:S(2)}) collective-permute-start(bf16[96,3072]{1,0:T(8,128)(2,1)} %fusion.154), channel_id=1, source_target_pairs={{8,0},{9,1},{10,2},{11,3},{12,4},{13,5},{14,6},{15,7},{16,8},{17,9... | collective-permute-start | bytes 1769480 | tf_op jit(solution)/shard_map/ppermute | solution.py:24
  509.6 14.8 %collective-permute-start.23 = (bf16[96,3072]{1,0:T(8,128)(2,1)}, bf16[96,3072]{1,0:T(8,128)(2,1)}, u32[]{:S(2)}, u32[]{:S(2)}) collective-permute-start(bf16[96,3072]{1,0:T(8,128)(2,1)} %fusion.157), channel_id=1, source_target_pairs={{8,0},{9,1},{10,2},{11,3},{12,4},{13,5},{14,6},{15,7},{16,8},{17,9... | collective-permute-start | bytes 1769480 | tf_op jit(solution)/shard_map/ppermute | solution.py:24
  544.0 14.8 %collective-permute-start.24 = (bf16[96,3072]{1,0:T(8,128)(2,1)}, bf16[96,3072]{1,0:T(8,128)(2,1)}, u32[]{:S(2)}, u32[]{:S(2)}) collective-permute-start(bf16[96,3072]{1,0:T(8,128)(2,1)} %fusion.160), channel_id=1, source_target_pairs={{8,0},{9,1},{10,2},{11,3},{12,4},{13,5},{14,6},{15,7},{16,8},{17,9... | collective-permute-start | bytes 1769480 | tf_op jit(solution)/shard_map/ppermute | solution.py:24
  578.5 14.8 %collective-permute-start.25 = (bf16[96,3072]{1,0:T(8,128)(2,1)}, bf16[96,3072]{1,0:T(8,128)(2,1)}, u32[]{:S(2)}, u32[]{:S(2)}) collective-permute-start(bf16[96,3072]{1,0:T(8,128)(2,1)} %fusion.163), channel_id=1, source_target_pairs={{8,0},{9,1},{10,2},{11,3},{12,4},{13,5},{14,6},{15,7},{16,8},{17,9... | collective-permute-start | bytes 1769480 | tf_op jit(solution)/shard_map/ppermute | solution.py:24
  612.9 14.9 %collective-permute-start.26 = (bf16[96,3072]{1,0:T(8,128)(2,1)}, bf16[96,3072]{1,0:T(8,128)(2,1)}, u32[]{:S(2)}, u32[]{:S(2)}) collective-permute-start(bf16[96,3072]{1,0:T(8,128)(2,1)} %fusion.166), channel_id=1, source_target_pairs={{8,0},{9,1},{10,2},{11,3},{12,4},{13,5},{14,6},{15,7},{16,8},{17,9... | collective-permute-start | bytes 1769480 | tf_op jit(solution)/shard_map/ppermute | solution.py:24
  681.9 14.8 %collective-permute-start.28 = (bf16[96,3072]{1,0:T(8,128)(2,1)}, bf16[96,3072]{1,0:T(8,128)(2,1)}, u32[]{:S(2)}, u32[]{:S(2)}) collective-permute-start(bf16[96,3072]{1,0:T(8,128)(2,1)} %fusion.172), channel_id=1, source_target_pairs={{8,0},{9,1},{10,2},{11,3},{12,4},{13,5},{14,6},{15,7},{16,8},{17,9... | collective-permute-start | bytes 1769480 | tf_op jit(solution)/shard_map/ppermute | solution.py:24
  716.3 14.9 %collective-permute-start.29 = (bf16[96,3072]{1,0:T(8,128)(2,1)}, bf16[96,3072]{1,0:T(8,128)(2,1)}, u32[]{:S(2)}, u32[]{:S(2)}) collective-permute-start(bf16[96,3072]{1,0:T(8,128)(2,1)} %fusion.175), channel_id=1, source_target_pairs={{8,0},{9,1},{10,2},{11,3},{12,4},{13,5},{14,6},{15,7},{16,8},{17,9... | collective-permute-start | bytes 1769480 | tf_op jit(solution)/shard_map/ppermute | solution.py:24
  785.2 14.8 %collective-permute-start.31 = (bf16[96,3072]{1,0:T(8,128)(2,1)}, bf16[96,3072]{1,0:T(8,128)(2,1)}, u32[]{:S(2)}, u32[]{:S(2)}) collective-permute-start(bf16[96,3072]{1,0:T(8,128)(2,1)} %fusion.181), channel_id=1, source_target_pairs={{8,0},{9,1},{10,2},{11,3},{12,4},{13,5},{14,6},{15,7},{16,8},{17,9... | collective-permute-start | bytes 1769480 | tf_op jit(solution)/shard_map/ppermute | solution.py:24
  819.7 14.8 %collective-permute-start.32 = (bf16[96,3072]{1,0:T(8,128)(2,1)}, bf16[96,3072]{1,0:T(8,128)(2,1)}, u32[]{:S(2)}, u32[]{:S(2)}) collective-permute-start(bf16[96,3072]{1,0:T(8,128)(2,1)} %fusion.184), channel_id=1, source_target_pairs={{8,0},{9,1},{10,2},{11,3},{12,4},{13,5},{14,6},{15,7},{16,8},{17,9... | collective-permute-start | bytes 1769480 | tf_op jit(solution)/shard_map/ppermute | solution.py:24
  854.1 14.8 %collective-permute-start.33 = (bf16[96,3072]{1,0:T(8,128)(2,1)}, bf16[96,3072]{1,0:T(8,128)(2,1)}, u32[]{:S(2)}, u32[]{:S(2)}) collective-permute-start(bf16[96,3072]{1,0:T(8,128)(2,1)} %fusion.187), channel_id=1, source_target_pairs={{8,0},{9,1},{10,2},{11,3},{12,4},{13,5},{14,6},{15,7},{16,8},{17,9... | collective-permute-start | bytes 1769480 | tf_op jit(solution)/shard_map/ppermute | solution.py:24
  874.1 161.8 %all-gather.7.cloned.1.call-start = ((), (), s32[]{:S(2)}) async-start(), calls=%async_computation.5 | async-start | bytes 5308416 | tf_op jit(solution)/shard_map/all_gather | solution.py:105
  890.8 14.9 %collective-permute-start.34 = (bf16[96,3072]{1,0:T(8,128)(2,1)}, bf16[96,3072]{1,0:T(8,128)(2,1)}, u32[]{:S(2)}, u32[]{:S(2)}) collective-permute-start(bf16[96,3072]{1,0:T(8,128)(2,1)} %fusion.190), channel_id=1, source_target_pairs={{8,0},{9,1},{10,2},{11,3},{12,4},{13,5},{14,6},{15,7},{16,8},{17,9... | collective-permute-start | bytes 1769480 | tf_op jit(solution)/shard_map/ppermute | solution.py:24
  910.8 165.8 %all-gather.9.cloned.1.call-start = ((), (), s32[]{:S(2)}) async-start(), calls=%async_computation.6 | async-start | bytes 5308416 | tf_op jit(solution)/shard_map/all_gather | solution.py:105
  927.6 14.8 %collective-permute-start.35 = (bf16[96,3072]{1,0:T(8,128)(2,1)}, bf16[96,3072]{1,0:T(8,128)(2,1)}, u32[]{:S(2)}, u32[]{:S(2)}) collective-permute-start(bf16[96,3072]{1,0:T(8,128)(2,1)} %fusion.193), channel_id=1, source_target_pairs={{8,0},{9,1},{10,2},{11,3},{12,4},{13,5},{14,6},{15,7},{16,8},{17,9... | collective-permute-start | bytes 1769480 | tf_op jit(solution)/shard_map/ppermute | solution.py:24
  947.7 185.1 %all-gather.11.cloned.1.call-start = ((), (), s32[]{:S(2)}) async-start(), calls=%async_computation.7 | async-start | bytes 5308416 | tf_op jit(solution)/shard_map/all_gather | solution.py:105
  990.5 17.5 %all-to-all-start = ((bf16[96,8,384]{2,0,1:T(8,128)(2,1)}), bf16[96,8,384]{2,0,1:T(8,128)(2,1)S(1)}, u32[]{:S(2)}, u32[]{:S(2)}) async-start(bf16[96,8,384]{2,0,1:T(8,128)(2,1)} %fusion.350), calls=%async_computation | async-start | bytes 1179648 | tf_op jit(solution)/shard_map/all_to_all | solution.py:103
  1008.0 24.1 %all-to-all-start.1 = ((bf16[96,8,384]{2,0,1:T(8,128)(2,1)}), bf16[96,8,384]{2,0,1:T(8,128)(2,1)S(1)}, u32[]{:S(2)}, u32[]{:S(2)}) async-start(bf16[96,8,384]{2,0,1:T(8,128)(2,1)} %fusion.349), calls=%async_computation.1 | async-start | bytes 1179648 | tf_op jit(solution)/shard_map/all_to_all | solution.py:103
  1032.2 17.8 %all-to-all-start.2 = ((bf16[96,8,384]{2,0,1:T(8,128)(2,1)}), bf16[96,8,384]{2,0,1:T(8,128)(2,1)S(1)}, u32[]{:S(2)}, u32[]{:S(2)}) async-start(bf16[96,8,384]{2,0,1:T(8,128)(2,1)} %fusion.348), calls=%async_computation.2 | async-start | bytes 1179648 | tf_op jit(solution)/shard_map/all_to_all | solution.py:103
  1050.0 33.1 %all-to-all-start.3 = ((bf16[96,8,384]{2,0,1:T(8,128)(2,1)}), bf16[96,8,384]{2,0,1:T(8,128)(2,1)S(1)}, u32[]{:S(2)}, u32[]{:S(2)}) async-start(bf16[96,8,384]{2,0,1:T(8,128)(2,1)} %fusion.347), calls=%async_computation.3 | async-start | bytes 1179648 | tf_op jit(solution)/shard_map/all_to_all | solution.py:103
  (45 other events, 522.2 us)
Sparse Core Ops, SparseCore 0:
  874.2 59.0 all-gather.4
  934.9 56.9 all-gather.6
  993.5 83.0 all-gather.8
  1078.1 54.5 all-gather.10

commit v4 on v3

--- a/solution.py
+++ b/solution.py
@@ -3,6 +3,7 @@
 import jax
 import jax.numpy as jnp
 from jax import lax
+from jax.experimental.layout import Layout, with_layout_constraint
 from jax.sharding import PartitionSpec as P
 
 EPSILON = 1e-06
@@ -63,7 +64,7 @@
     incoming = jnp.zeros((rows_mb, width), jnp.bfloat16)
     pieces = sections
     piece = width // pieces
-    weight_t = jnp.zeros((width, width), jnp.bfloat16)
+    weight_t = with_layout_constraint(jnp.zeros((width, width), jnp.bfloat16), Layout((0, 1)))
     for tick in range(ticks):
         batch = tick - section
         slot = jnp.clip(batch + 1, 0, micro + 1)
@@ -77,6 +78,7 @@
         if tick < pieces:
             block = jnp.transpose(lax.slice_in_dim(weight, tick * piece, (tick + 1) * piece, axis=0))
             weight_t = lax.dynamic_update_slice_in_dim(weight_t, block, tick * piece, axis=1)
+            weight_t = with_layout_constraint(weight_t, Layout((0, 1)))
             weight_t, incoming = lax.optimization_barrier((weight_t, incoming))
 
     half = replicas // 2

time: 1160 us -> 1360 us (1.17)
  local copies, waits for them, and re-layouts: 70 us -> 367 us
  waiting for transfers between devices: 405 us -> 271 us
  matrix products: 351 us -> 368 us
    dynamic_update_slice x16, local copies, waits for them, and re-layouts: 27 us -> 256 us  [on_device(): lax.dynamic_update_slice_in_dim(weight_t, block, tick * piece, axis=1)]
    ppermute x36, waiting for transfers between devices: 305 us -> 155 us  [relay(): return lax.ppermute(array, ('pipe', 'dp'), pairs)]
    dot_general x19, matrix products: 75 us -> 188 us  [forward_layer(): gate_value = jnp.dot(normed, weight, preferred_element_type=jnp.float32)]
    dot_general x18, matrix products: 246 us -> 149 us  [backward_layer(): back = jnp.dot(slope, weight_t, preferred_element_type=jnp.float32)]
    unnamed x52 -> x132, local copies, waits for them, and re-layouts: 5.02 us -> 41.7 us
    dynamic_update_slice x18, local copies, waits for them, and re-layouts: 20.6 us -> 40.7 us  [on_device(): lax.dynamic_update_index_in_dim(kept_gates, gate_value, slot, 0)]
    reduce_sum x21, other arithmetic: 8.81 us -> 27.8 us  [norm_factor(): jnp.mean(floats * floats, axis=-1, keepdims=True) + EPSILON]
    all_gather x4, waiting for transfers between devices: 71.8 us -> 87.6 us  [on_device(): slope_all = lax.all_gather(finished, 'dp', axis=0, tiled=True)]
  transfers between devices with their start and end apart: 45 -> 45, of which waited for: 40 -> 25; matrix products, arithmetic and copies ran while one was open for 20% -> 48% of each run, Pallas kernels for 0% -> 0%
where the time goes in v4:
time: 1360 us; the launch traced here: 1340 us
  matrix products  368 us (27%)
  local copies, waits for them, and re-layouts  367 us (27%)
  waiting for transfers between devices  271 us (20%)
  starting transfers between devices  186 us (14%)
  other arithmetic  136 us (10%)
  between operations  15.4 us (1%)
    dynamic_update_slice x16, local copies, waits for them, and re-layouts, on_device(): lax.dynamic_update_slice_in_dim(weight_t, block, tick * piece, axis=1)  256 us
    dot_general x19, matrix products, forward_layer(): gate_value = jnp.dot(normed, weight, preferred_element_type=jnp.float32)  188 us
    ppermute x36, starting transfers between devices, relay(): return lax.ppermute(array, ('pipe', 'dp'), pairs)  165 us
    ppermute x36, waiting for transfers between devices, relay(): return lax.ppermute(array, ('pipe', 'dp'), pairs)  155 us
    dot_general x18, matrix products, backward_layer(): back = jnp.dot(slope, weight_t, preferred_element_type=jnp.float32)  149 us
    all_gather x4, waiting for transfers between devices, on_device(): slope_all = lax.all_gather(finished, 'dp', axis=0, tiled=True)  87.6 us
    dynamic_update_slice x19, other arithmetic, on_device(): kept_slopes = lax.dynamic_update_index_in_dim(kept_slopes, slope, slot, 0)  55.4 us
    convert_element_type x18, other arithmetic, backward_layer(): down = (up_float + factor * (back - unit * jnp.mean(back * unit, axis=-1,...  45 us
  transfers between devices with their start and end apart: 45, of which 25 were waited for; matrix products, arithmetic and copies ran while one was open for 48% of the time, Pallas kernels for 0%

profile of v4, /device:TPU:6, one launch (start us, length us, event | category | flops | bytes accessed | tf_op | source)
XLA Modules:
  0.0 1343.0 jit_solution(10251575765147969125)
XLA Ops:
  7.9 11.2 fusion.198
  22.1 12.2 fusion.418
  73.8 12.1 pad
  100.7 17.3 %dynamic_update_slice.224 = bf16[3072,3072]{1,0:T(8,128)(2,1)} dynamic-update-slice(bf16[3072,3072]{1,0:T(8,128)(2,1)} %pad, bf16[3072,192]{1,0:T(8,128)(2,1)} %bitcast.943, s32[]{:T(128)} %constant.513.clone.1, s32[]{:T(128)} %constant.522.clone.1) | dynamic-update-slice | bytes 2359300 | tf_op jit(solution)/shard_map/dynamic_update_slice | solution.py:80
  135.5 15.3 %dynamic_update_slice.226 = bf16[3072,3072]{1,0:T(8,128)(2,1)} dynamic-update-slice(bf16[3072,3072]{1,0:T(8,128)(2,1)} %dynamic_update_slice.224, bf16[3072,192]{1,0:T(8,128)(2,1)} %bitcast.942, s32[]{:T(128)} %constant.513.clone.1, s32[]{:T(128)} %constant.523.clone.1) | dynamic-update-slice | bytes 2359300 | tf_op jit(solution)/shard_map/dynamic_update_slice | solution.py:80
  169.3 17.3 %dynamic_update_slice.228 = bf16[3072,3072]{1,0:T(8,128)(2,1)} dynamic-update-slice(bf16[3072,3072]{1,0:T(8,128)(2,1)} %dynamic_update_slice.226, bf16[3072,192]{1,0:T(8,128)(2,1)} %bitcast.941, s32[]{:T(128)} %constant.513.clone.1, s32[]{:T(128)} %constant.525.clone.1) | dynamic-update-slice | bytes 2359300 | tf_op jit(solution)/shard_map/dynamic_update_slice | solution.py:80
  204.5 15.3 %dynamic_update_slice.230 = bf16[3072,3072]{1,0:T(8,128)(2,1)} dynamic-update-slice(bf16[3072,3072]{1,0:T(8,128)(2,1)} %dynamic_update_slice.228, bf16[3072,192]{1,0:T(8,128)(2,1)} %bitcast.940, s32[]{:T(128)} %constant.513.clone.1, s32[]{:T(128)} %constant.526.clone.1) | dynamic-update-slice | bytes 2359300 | tf_op jit(solution)/shard_map/dynamic_update_slice | solution.py:80
  238.0 17.3 %dynamic_update_slice.232 = bf16[3072,3072]{1,0:T(8,128)(2,1)} dynamic-update-slice(bf16[3072,3072]{1,0:T(8,128)(2,1)} %dynamic_update_slice.230, bf16[3072,192]{1,0:T(8,128)(2,1)} %bitcast.939, s32[]{:T(128)} %constant.513.clone.1, s32[]{:T(128)} %constant.528.clone.1) | dynamic-update-slice | bytes 2359300 | tf_op jit(solution)/shard_map/dynamic_update_slice | solution.py:80
  272.8 15.2 %dynamic_update_slice.234 = bf16[3072,3072]{1,0:T(8,128)(2,1)} dynamic-update-slice(bf16[3072,3072]{1,0:T(8,128)(2,1)} %dynamic_update_slice.232, bf16[3072,192]{1,0:T(8,128)(2,1)} %bitcast.938, s32[]{:T(128)} %constant.513.clone.1, s32[]{:T(128)} %constant.530.clone.1) | dynamic-update-slice | bytes 2359300 | tf_op jit(solution)/shard_map/dynamic_update_slice | solution.py:80
  305.4 17.3 %dynamic_update_slice.236 = bf16[3072,3072]{1,0:T(8,128)(2,1)} dynamic-update-slice(bf16[3072,3072]{1,0:T(8,128)(2,1)} %dynamic_update_slice.234, bf16[3072,192]{1,0:T(8,128)(2,1)} %bitcast.937, s32[]{:T(128)} %constant.513.clone.1, s32[]{:T(128)} %constant.532.clone.1) | dynamic-update-slice | bytes 2359300 | tf_op jit(solution)/shard_map/dynamic_update_slice | solution.py:80
  326.8 11.2 fusion.241
  339.9 15.3 %dynamic_update_slice.238 = bf16[3072,3072]{1,0:T(8,128)(2,1)} dynamic-update-slice(bf16[3072,3072]{1,0:T(8,128)(2,1)} %dynamic_update_slice.236, bf16[3072,192]{1,0:T(8,128)(2,1)} %bitcast.936, s32[]{:T(128)} %constant.513.clone.1, s32[]{:T(128)} %constant.534.clone.1) | dynamic-update-slice | bytes 2359300 | tf_op jit(solution)/shard_map/dynamic_update_slice | solution.py:80
  372.4 17.3 %dynamic_update_slice.240 = bf16[3072,3072]{1,0:T(8,128)(2,1)} dynamic-update-slice(bf16[3072,3072]{1,0:T(8,128)(2,1)} %dynamic_update_slice.238, bf16[3072,192]{1,0:T(8,128)(2,1)} %bitcast.935, s32[]{:T(128)} %constant.513.clone.1, s32[]{:T(128)} %constant.536.clone.1) | dynamic-update-slice | bytes 2359300 | tf_op jit(solution)/shard_map/dynamic_update_slice | solution.py:80
  407.1 15.3 %dynamic_update_slice.242 = bf16[3072,3072]{1,0:T(8,128)(2,1)} dynamic-update-slice(bf16[3072,3072]{1,0:T(8,128)(2,1)} %dynamic_update_slice.240, bf16[3072,192]{1,0:T(8,128)(2,1)} %bitcast.934, s32[]{:T(128)} %constant.513.clone.1, s32[]{:T(128)} %constant.538.clone.1) | dynamic-update-slice | bytes 2359300 | tf_op jit(solution)/shard_map/dynamic_update_slice | solution.py:80
  439.6 17.3 %dynamic_update_slice.244 = bf16[3072,3072]{1,0:T(8,128)(2,1)} dynamic-update-slice(bf16[3072,3072]{1,0:T(8,128)(2,1)} %dynamic_update_slice.242, bf16[3072,192]{1,0:T(8,128)(2,1)} %bitcast.933, s32[]{:T(128)} %constant.513.clone.1, s32[]{:T(128)} %constant.540.clone.1) | dynamic-update-slice | bytes 2359300 | tf_op jit(solution)/shard_map/dynamic_update_slice | solution.py:80
  474.1 15.2 %dynamic_update_slice.246 = bf16[3072,3072]{1,0:T(8,128)(2,1)} dynamic-update-slice(bf16[3072,3072]{1,0:T(8,128)(2,1)} %dynamic_update_slice.244, bf16[3072,192]{1,0:T(8,128)(2,1)} %bitcast.932, s32[]{:T(128)} %constant.513.clone.1, s32[]{:T(128)} %constant.542.clone.1) | dynamic-update-slice | bytes 2359300 | tf_op jit(solution)/shard_map/dynamic_update_slice | solution.py:80
  507.0 17.3 %dynamic_update_slice.248 = bf16[3072,3072]{1,0:T(8,128)(2,1)} dynamic-update-slice(bf16[3072,3072]{1,0:T(8,128)(2,1)} %dynamic_update_slice.246, bf16[3072,192]{1,0:T(8,128)(2,1)} %bitcast.931, s32[]{:T(128)} %constant.513.clone.1, s32[]{:T(128)} %constant.544.clone.1) | dynamic-update-slice | bytes 2359300 | tf_op jit(solution)/shard_map/dynamic_update_slice | solution.py:80
  541.5 15.1 %dynamic_update_slice.250 = bf16[3072,3072]{1,0:T(8,128)(2,1)} dynamic-update-slice(bf16[3072,3072]{1,0:T(8,128)(2,1)} %dynamic_update_slice.248, bf16[3072,192]{1,0:T(8,128)(2,1)} %bitcast.930, s32[]{:T(128)} %constant.513.clone.1, s32[]{:T(128)} %constant.546.clone.1) | dynamic-update-slice | bytes 2359300 | tf_op jit(solution)/shard_map/dynamic_update_slice | solution.py:80
  573.8 16.6 %dynamic_update_slice.252 = bf16[3072,3072]{1,0:T(8,128)(2,1)} dynamic-update-slice(bf16[3072,3072]{1,0:T(8,128)(2,1)} %dynamic_update_slice.250, bf16[3072,192]{1,0:T(8,128)(2,1)} %bitcast.929, s32[]{:T(128)} %constant.513.clone.1, s32[]{:T(128)} %constant.548.clone.1) | dynamic-update-slice | bytes 2359300 | tf_op jit(solution)/shard_map/dynamic_update_slice | solution.py:80
  607.7 11.2 collective-permute-done.16
  626.0 11.3 collective-permute-done.17
  1177.7 15.7 %all-to-all-done = bf16[96,8,384]{2,0,1:T(8,128)(2,1)S(1)} async-done(((bf16[96,8,384]{2,0,1:T(8,128)(2,1)}), bf16[96,8,384]{2,0,1:T(8,128)(2,1)S(1)}, u32[]{:S(2)}, u32[]{:S(2)}) %all-to-all-start) | async-done | bytes 589856 | tf_op jit(solution)/shard_map/all_to_all | solution.py:105
  1231.7 38.5 %all-gather.9.cloned.1.call-done = bf16[768,3072]{1,0:T(8,128)(2,1)} async-done(((bf16[96,3072]{1,0:T(8,128)(2,1)}), bf16[768,3072]{1,0:T(8,128)(2,1)}) %all-gather.9.cloned.1.call-update) | async-done | bytes 4718608 | tf_op jit(solution)/shard_map/all_gather | solution.py:107
  1276.7 49.1 %all-gather.11.cloned.1.call-done = bf16[768,3072]{1,0:T(8,128)(2,1)} async-done(((bf16[96,3072]{1,0:T(8,128)(2,1)}), bf16[768,3072]{1,0:T(8,128)(2,1)}) %all-gather.11.cloned.1.call-update) | async-done | bytes 4718608 | tf_op jit(solution)/shard_map/all_gather | solution.py:107
  (428 shorter events, 910.9 us)
Async XLA Ops:
  6.5 1191.3 %all-gather.5.cloned.1.call-start = ((), (), s32[]{:S(2)}) async-start(), calls=%async_computation.4 | async-start | bytes 5308416 | tf_op jit(solution)/shard_map/all_gather | solution.py:107
  19.1 71.8 %collective-permute-start = (bf16[96,3072]{1,0:T(8,128)(2,1)}, bf16[96,3072]{1,0:T(8,128)(2,1)}, u32[]{:S(2)}, u32[]{:S(2)}) collective-permute-start(bf16[96,3072]{1,0:T(8,128)(2,1)} %get-tuple-element.197), channel_id=1, source_target_pairs={{0,8},{1,9},{2,10},{3,11},{4,12},{5,13},{6,14},{7,15},{8,16},{9,17... | collective-permute-start | bytes 1769480 | tf_op jit(solution)/shard_map/ppermute | solution.py:25
  21.0 621.4 %collective-permute-start.18 = (bf16[4,96,3072]{2,1,0:T(8,128)(2,1)}, bf16[4,96,3072]{2,1,0:T(8,128)(2,1)}, u32[]{:S(2)}, u32[]{:S(2)}) collective-permute-start(bf16[4,96,3072]{2,1,0:T(8,128)(2,1)} %param.5), channel_id=1, source_target_pairs={{0,4},{1,5},{2,6},{3,7},{4,0},{5,1},{6,2},{7,3},{8,12},{9,13},{10,... | collective-permute-start | bytes 7077896 | tf_op jit(solution)/shard_map/ppermute | solution.py:85
  97.2 23.3 %collective-permute-start.1 = (bf16[96,3072]{1,0:T(8,128)(2,1)}, bf16[96,3072]{1,0:T(8,128)(2,1)}, u32[]{:S(2)}, u32[]{:S(2)}) collective-permute-start(bf16[96,3072]{1,0:T(8,128)(2,1)} %get-tuple-element.199), channel_id=1, source_target_pairs={{0,8},{1,9},{2,10},{3,11},{4,12},{5,13},{6,14},{7,15},{8,16},{9,17... | collective-permute-start | bytes 1769480 | tf_op jit(solution)/shard_map/ppermute | solution.py:25
  133.3 20.0 %collective-permute-start.2 = (bf16[96,3072]{1,0:T(8,128)(2,1)}, bf16[96,3072]{1,0:T(8,128)(2,1)}, u32[]{:S(2)}, u32[]{:S(2)}) collective-permute-start(bf16[96,3072]{1,0:T(8,128)(2,1)} %get-tuple-element.201), channel_id=1, source_target_pairs={{0,8},{1,9},{2,10},{3,11},{4,12},{5,13},{6,14},{7,15},{8,16},{9,17... | collective-permute-start | bytes 1769480 | tf_op jit(solution)/shard_map/ppermute | solution.py:25
  166.0 23.1 %collective-permute-start.3 = (bf16[96,3072]{1,0:T(8,128)(2,1)}, bf16[96,3072]{1,0:T(8,128)(2,1)}, u32[]{:S(2)}, u32[]{:S(2)}) collective-permute-start(bf16[96,3072]{1,0:T(8,128)(2,1)} %get-tuple-element.203), channel_id=1, source_target_pairs={{0,8},{1,9},{2,10},{3,11},{4,12},{5,13},{6,14},{7,15},{8,16},{9,17... | collective-permute-start | bytes 1769480 | tf_op jit(solution)/shard_map/ppermute | solution.py:25
  201.9 20.4 %collective-permute-start.4 = (bf16[96,3072]{1,0:T(8,128)(2,1)}, bf16[96,3072]{1,0:T(8,128)(2,1)}, u32[]{:S(2)}, u32[]{:S(2)}) collective-permute-start(bf16[96,3072]{1,0:T(8,128)(2,1)} %get-tuple-element.205), channel_id=1, source_target_pairs={{0,8},{1,9},{2,10},{3,11},{4,12},{5,13},{6,14},{7,15},{8,16},{9,17... | collective-permute-start | bytes 1769480 | tf_op jit(solution)/shard_map/ppermute | solution.py:25
  235.0 22.8 %collective-permute-start.5 = (bf16[96,3072]{1,0:T(8,128)(2,1)}, bf16[96,3072]{1,0:T(8,128)(2,1)}, u32[]{:S(2)}, u32[]{:S(2)}) collective-permute-start(bf16[96,3072]{1,0:T(8,128)(2,1)} %get-tuple-element.207), channel_id=1, source_target_pairs={{0,8},{1,9},{2,10},{3,11},{4,12},{5,13},{6,14},{7,15},{8,16},{9,17... | collective-permute-start | bytes 1769480 | tf_op jit(solution)/shard_map/ppermute | solution.py:25
  270.6 20.0 %collective-permute-start.6 = (bf16[96,3072]{1,0:T(8,128)(2,1)}, bf16[96,3072]{1,0:T(8,128)(2,1)}, u32[]{:S(2)}, u32[]{:S(2)}) collective-permute-start(bf16[96,3072]{1,0:T(8,128)(2,1)} %get-tuple-element.209), channel_id=1, source_target_pairs={{0,8},{1,9},{2,10},{3,11},{4,12},{5,13},{6,14},{7,15},{8,16},{9,17... | collective-permute-start | bytes 1769480 | tf_op jit(solution)/shard_map/ppermute | solution.py:25
  303.3 21.9 %collective-permute-start.7 = (bf16[96,3072]{1,0:T(8,128)(2,1)}, bf16[96,3072]{1,0:T(8,128)(2,1)}, u32[]{:S(2)}, u32[]{:S(2)}) collective-permute-start(bf16[96,3072]{1,0:T(8,128)(2,1)} %get-tuple-element.211), channel_id=1, source_target_pairs={{0,8},{1,9},{2,10},{3,11},{4,12},{5,13},{6,14},{7,15},{8,16},{9,17... | collective-permute-start | bytes 1769480 | tf_op jit(solution)/shard_map/ppermute | solution.py:25
  338.0 19.8 %collective-permute-start.8 = (bf16[96,3072]{1,0:T(8,128)(2,1)}, bf16[96,3072]{1,0:T(8,128)(2,1)}, u32[]{:S(2)}, u32[]{:S(2)}) collective-permute-start(bf16[96,3072]{1,0:T(8,128)(2,1)} %get-tuple-element.213), channel_id=1, source_target_pairs={{0,8},{1,9},{2,10},{3,11},{4,12},{5,13},{6,14},{7,15},{8,16},{9,17... | collective-permute-start | bytes 1769480 | tf_op jit(solution)/shard_map/ppermute | solution.py:25
  370.5 21.7 %collective-permute-start.9 = (bf16[96,3072]{1,0:T(8,128)(2,1)}, bf16[96,3072]{1,0:T(8,128)(2,1)}, u32[]{:S(2)}, u32[]{:S(2)}) collective-permute-start(bf16[96,3072]{1,0:T(8,128)(2,1)} %get-tuple-element.215), channel_id=1, source_target_pairs={{0,8},{1,9},{2,10},{3,11},{4,12},{5,13},{6,14},{7,15},{8,16},{9,17... | collective-permute-start | bytes 1769480 | tf_op jit(solution)/shard_map/ppermute | solution.py:25
  405.0 19.9 %collective-permute-start.10 = (bf16[96,3072]{1,0:T(8,128)(2,1)}, bf16[96,3072]{1,0:T(8,128)(2,1)}, u32[]{:S(2)}, u32[]{:S(2)}) collective-permute-start(bf16[96,3072]{1,0:T(8,128)(2,1)} %get-tuple-element.217), channel_id=1, source_target_pairs={{0,8},{1,9},{2,10},{3,11},{4,12},{5,13},{6,14},{7,15},{8,16},{9,17... | collective-permute-start | bytes 1769480 | tf_op jit(solution)/shard_map/ppermute | solution.py:25
  437.7 21.7 %collective-permute-start.11 = (bf16[96,3072]{1,0:T(8,128)(2,1)}, bf16[96,3072]{1,0:T(8,128)(2,1)}, u32[]{:S(2)}, u32[]{:S(2)}) collective-permute-start(bf16[96,3072]{1,0:T(8,128)(2,1)} %get-tuple-element.219), channel_id=1, source_target_pairs={{0,8},{1,9},{2,10},{3,11},{4,12},{5,13},{6,14},{7,15},{8,16},{9,17... | collective-permute-start | bytes 1769480 | tf_op jit(solution)/shard_map/ppermute | solution.py:25
  472.2 19.7 %collective-permute-start.12 = (bf16[96,3072]{1,0:T(8,128)(2,1)}, bf16[96,3072]{1,0:T(8,128)(2,1)}, u32[]{:S(2)}, u32[]{:S(2)}) collective-permute-start(bf16[96,3072]{1,0:T(8,128)(2,1)} %get-tuple-element.221), channel_id=1, source_target_pairs={{0,8},{1,9},{2,10},{3,11},{4,12},{5,13},{6,14},{7,15},{8,16},{9,17... | collective-permute-start | bytes 1769480 | tf_op jit(solution)/shard_map/ppermute | solution.py:25
  504.6 22.2 %collective-permute-start.13 = (bf16[96,3072]{1,0:T(8,128)(2,1)}, bf16[96,3072]{1,0:T(8,128)(2,1)}, u32[]{:S(2)}, u32[]{:S(2)}) collective-permute-start(bf16[96,3072]{1,0:T(8,128)(2,1)} %get-tuple-element.223), channel_id=1, source_target_pairs={{0,8},{1,9},{2,10},{3,11},{4,12},{5,13},{6,14},{7,15},{8,16},{9,17... | collective-permute-start | bytes 1769480 | tf_op jit(solution)/shard_map/ppermute | solution.py:25
  539.6 19.6 %collective-permute-start.14 = (bf16[96,3072]{1,0:T(8,128)(2,1)}, bf16[96,3072]{1,0:T(8,128)(2,1)}, u32[]{:S(2)}, u32[]{:S(2)}) collective-permute-start(bf16[96,3072]{1,0:T(8,128)(2,1)} %get-tuple-element.225), channel_id=1, source_target_pairs={{0,8},{1,9},{2,10},{3,11},{4,12},{5,13},{6,14},{7,15},{8,16},{9,17... | collective-permute-start | bytes 1769480 | tf_op jit(solution)/shard_map/ppermute | solution.py:25
  571.9 22.2 %collective-permute-start.15 = (bf16[96,3072]{1,0:T(8,128)(2,1)}, bf16[96,3072]{1,0:T(8,128)(2,1)}, u32[]{:S(2)}, u32[]{:S(2)}) collective-permute-start(bf16[96,3072]{1,0:T(8,128)(2,1)} %get-tuple-element.227), channel_id=1, source_target_pairs={{0,8},{1,9},{2,10},{3,11},{4,12},{5,13},{6,14},{7,15},{8,16},{9,17... | collective-permute-start | bytes 1769480 | tf_op jit(solution)/shard_map/ppermute | solution.py:25
  1067.2 145.1 %all-gather.7.cloned.1.call-start = ((), (), s32[]{:S(2)}) async-start(), calls=%async_computation.5 | async-start | bytes 5308416 | tf_op jit(solution)/shard_map/all_gather | solution.py:107
  1098.2 172.0 %all-gather.9.cloned.1.call-start = ((), (), s32[]{:S(2)}) async-start(), calls=%async_computation.6 | async-start | bytes 5308416 | tf_op jit(solution)/shard_map/all_gather | solution.py:107
  1129.2 196.6 %all-gather.11.cloned.1.call-start = ((), (), s32[]{:S(2)}) async-start(), calls=%async_computation.7 | async-start | bytes 5308416 | tf_op jit(solution)/shard_map/all_gather | solution.py:107
  1165.8 27.6 %all-to-all-start = ((bf16[96,8,384]{2,0,1:T(8,128)(2,1)}), bf16[96,8,384]{2,0,1:T(8,128)(2,1)S(1)}, u32[]{:S(2)}, u32[]{:S(2)}) async-start(bf16[96,8,384]{2,0,1:T(8,128)(2,1)} %fusion.350), calls=%async_computation | async-start | bytes 1179648 | tf_op jit(solution)/shard_map/all_to_all | solution.py:105
  1208.2 19.6 %all-to-all-start.2 = ((bf16[96,8,384]{2,0,1:T(8,128)(2,1)}), bf16[96,8,384]{2,0,1:T(8,128)(2,1)S(1)}, u32[]{:S(2)}, u32[]{:S(2)}) async-start(bf16[96,8,384]{2,0,1:T(8,128)(2,1)} %fusion.348), calls=%async_computation.2 | async-start | bytes 1179648 | tf_op jit(solution)/shard_map/all_to_all | solution.py:105
  1227.8 48.9 %all-to-all-start.3 = ((bf16[96,8,384]{2,0,1:T(8,128)(2,1)}), bf16[96,8,384]{2,0,1:T(8,128)(2,1)S(1)}, u32[]{:S(2)}, u32[]{:S(2)}) async-start(bf16[96,8,384]{2,0,1:T(8,128)(2,1)} %fusion.347), calls=%async_computation.3 | async-start | bytes 1179648 | tf_op jit(solution)/shard_map/all_to_all | solution.py:105
  (77 other events, 852.8 us)
Sparse Core Ops, SparseCore 0:
  1067.4 59.0 all-gather.4
  1128.1 68.7 all-gather.6
  1198.6 71.5 all-gather.8
  1271.7 54.0 all-gather.10

commit v5 on v2

--- a/solution.py
+++ b/solution.py
@@ -79,7 +79,11 @@
     kept_slopes = jnp.zeros((micro + 2, rows_mb, width), jnp.bfloat16)
     incoming = jnp.zeros((rows_mb, width), jnp.bfloat16)
     cols = width // replicas
-    grad_rows = jnp.zeros((cols, width), jnp.float32)
+    ring = replicas // 2
+    rep = lax.axis_index("dp")
+    side = rep // ring
+    place = rep % ring
+    partial = jnp.zeros((2 * cols, width), jnp.float32)
     for tick in range(ticks):
         batch = tick - (sections - 1 - section)
         slot = jnp.clip(batch + 1, 0, micro + 1)
@@ -93,16 +97,42 @@
             incoming = relay(down, -1)
         done = tick - (sections - 1)
         if done >= 0:
+            finished, kept_slopes = lax.optimization_barrier((kept_slopes[done + 1], kept_slopes))
             floats, factor = norm_factor(kept_inputs[done + 1])
-            normed = (floats * factor).astype(jnp.bfloat16)
-            normed_cols = lax.all_to_all(normed, "dp", 1, 0, tiled=True)
-            finished, kept_slopes = lax.optimization_barrier((kept_slopes[done + 1], kept_slopes))
-            slope_all = lax.all_gather(finished, "dp", axis=0, tiled=True)
-            grad_rows = grad_rows + lax.dot_general(
-                normed_cols, slope_all, (((0,), (0,)), ((), ())), preferred_element_type=jnp.float32
+            normed = (floats * factor).astype(jnp.bfloat16).reshape(rows_mb, replicas, cols)
+            slope_rows = []
+            normed_rows = []
+            for shift in range(ring):
+                target = (place + shift) % ring
+                wanted = jnp.concatenate(
+                    [
+                        lax.dynamic_slice_in_dim(normed, target, 1, axis=1),
+                        lax.dynamic_slice_in_dim(normed, target + ring, 1, axis=1),
+                    ],
+                    axis=1,
+                )
+                if shift == 0:
+                    slope_rows.append(finished)
+                    normed_rows.append(wanted)
+                    continue
+                pairs = [
+                    (row * ring + r, row * ring + (r + shift) % ring)
+                    for row in range(2)
+                    for r in range(ring)
+                ]
+                slope_rows.append(lax.ppermute(finished, "dp", pairs))
+                normed_rows.append(lax.ppermute(wanted, "dp", pairs))
+            slope_rows = jnp.concatenate(slope_rows, axis=0)
+            normed_rows = jnp.concatenate(normed_rows, axis=0).reshape(ring * rows_mb, 2 * cols)
+            partial = partial + lax.dot_general(
+                normed_rows, slope_rows, (((0,), (0,)), ((), ())), preferred_element_type=jnp.float32
             )
+    partial = partial.reshape(2, cols, width)
+    mine = lax.dynamic_index_in_dim(partial, side, 0, keepdims=False)
+    theirs = lax.dynamic_index_in_dim(partial, 1 - side, 0, keepdims=False).astype(jnp.bfloat16)
+    theirs = lax.ppermute(theirs, "dp", [(r, (r + ring) % replicas) for r in range(replicas)])
     factor_out = 1.0 / math.sqrt(micro * rows_mb * replicas)
-    return (grad_rows * factor_out).astype(jnp.bfloat16)[None]
+    return ((mine + theirs.astype(jnp.float32)) * factor_out).astype(jnp.bfloat16)[None]
 
 
 def solution(mesh):

time: 1090 us -> 977 us (0.90)
  waiting for transfers between devices: 439 us -> 338 us
  matrix products: 260 us -> 216 us
  other arithmetic: 117 us -> 143 us
  between operations: 15.3 us -> 2.35 us
  local copies, waits for them, and re-layouts: 65 us -> 77.8 us
    all_gather x4 -> x0, waiting for transfers between devices: 87.8 us -> none  [on_device(): slope_all = lax.all_gather(finished, 'dp', axis=0, tiled=True)]
    ppermute x0 -> x25, waiting for transfers between devices: none -> 87.1 us  [the longest x1 54.2 us: on_device(): lax.ppermute(theirs, 'dp', [(r, (r + ring) % replicas) for r in range(rep...]
    ppermute x36, waiting for transfers between devices: 323 us -> 251 us  [relay(): return lax.ppermute(array, ('pipe', 'dp'), pairs)]
    dot_general x18, matrix products: 149 us -> 101 us  [backward_layer(): back = jnp.dot(slope, weight_t, preferred_element_type=jnp.float32)]
    ppermute x0 -> x25, starting transfers between devices: none -> 41.7 us  [the longest x12 22.9 us: on_device(): normed_rows.append(lax.ppermute(wanted, 'dp', pairs))]
    concatenate x0 -> x16, other arithmetic: none -> 32.5 us  [the longest x4 21.2 us: on_device(): jnp.concatenate(normed_rows, axis=0).reshape(ring * rows_mb, 2 * cols)]
    all_to_all x4 -> x0, waiting for transfers between devices: 28.3 us -> none  [on_device(): normed_cols = lax.all_to_all(normed, 'dp', 1, 0, tiled=True)]
    all_to_all x4 -> x0, starting transfers between devices: 19.4 us -> none  [on_device(): normed_cols = lax.all_to_all(normed, 'dp', 1, 0, tiled=True)]
  transfers between devices with their start and end apart: 45 -> 62, of which waited for: 40 -> 40; matrix products, arithmetic and copies ran while one was open for 19% -> 34% of each run, Pallas kernels for 0% -> 0%
where the time goes in v5:
time: 977 us; the launch traced here: 966 us
  waiting for transfers between devices  338 us (35%)
  matrix products  216 us (22%)
  starting transfers between devices  189 us (19%)
  other arithmetic  143 us (15%)
  local copies, waits for them, and re-layouts  77.8 us (8%)
    ppermute x36, waiting for transfers between devices, relay(): return lax.ppermute(array, ('pipe', 'dp'), pairs)  251 us
    ppermute x36, starting transfers between devices, relay(): return lax.ppermute(array, ('pipe', 'dp'), pairs)  146 us
    dot_general x18, matrix products, backward_layer(): back = jnp.dot(slope, weight_t, preferred_element_type=jnp.float32)  101 us
    dot_general x19, matrix products, forward_layer(): gate_value = jnp.dot(normed, weight, preferred_element_type=jnp.float32)  79.7 us
    ppermute x1, waiting for transfers between devices, on_device(): lax.ppermute(theirs, 'dp', [(r, (r + ring) % replicas) for r in range(rep...  54.2 us
    dynamic_update_slice x19, other arithmetic, on_device(): kept_slopes = lax.dynamic_update_index_in_dim(kept_slopes, slope, slot, 0)  51.3 us
    convert_element_type x18, other arithmetic, backward_layer(): down = (up_float + factor * (back - unit * jnp.mean(back * unit, axis=-1,...  38.3 us
    unnamed x163, local copies, waits for them, and re-layouts  37.3 us
  transfers between devices with their start and end apart: 62, of which 40 were waited for; matrix products, arithmetic and copies ran while one was open for 34% of the time, Pallas kernels for 0%

profile of v5, /device:TPU:6, one launch (start us, length us, event | category | flops | bytes accessed | tf_op | source)
XLA Modules:
  0.0 966.4 jit_solution(2433461227296449759)
XLA Ops:
  1.3 11.2 %fusion.271 = (bf16[96,3072]{1,0:T(8,128)(2,1)}, f32[96,3072]{1,0:T(8,128)}) fusion(bf16[4,96,3072]{2,1,0:T(8,128)(2,1)} %param.3, s32[]{:T(128)S(6)} %min.229, pred[]{:T(512)S(6)} %eq.22, bf16[1,3072,3072]{2,1,0:T(8,128)(2,1)} %param.4, f32[96]{0:T(128)S(1)} %add_rsqrt_fusion.40), kind=kOutput, calls=%fused_computation.395 | convolution fusion | flops 1815478272 | bytes 21825920 | tf_op jit(solution)/shard_map/dot_general | solution.py:37
  15.4 24.6 %copy.4 = bf16[1,3072,3072]{1,2,0:T(8,128)(2,1)} copy(bf16[1,3072,3072]{2,1,0:T(8,128)(2,1)} %param.4) | data formatting | bytes 37748736 | tf_op args[1]
  47.7 8.3 fusion.293
  60.8 10.1 %collective-permute-done.1 = bf16[96,3072]{1,0:T(8,128)(2,1)S(1)} collective-permute-done((bf16[96,3072]{1,0:T(8,128)(2,1)S(1)}, bf16[96,3072]{1,0:T(8,128)(2,1)S(1)}, u32[]{:S(2)}, u32[]{:S(2)}) %collective-permute-start.1) | collective-permute-done | bytes 589856 | tf_op jit(solution)/shard_map/ppermute | solution.py:25
  78.0 11.2 %collective-permute-done.2 = bf16[96,3072]{1,0:T(8,128)(2,1)S(1)} collective-permute-done((bf16[96,3072]{1,0:T(8,128)(2,1)S(1)}, bf16[96,3072]{1,0:T(8,128)(2,1)S(1)}, u32[]{:S(2)}, u32[]{:S(2)}) %collective-permute-start.2) | collective-permute-done | bytes 589856 | tf_op jit(solution)/shard_map/ppermute | solution.py:25
  96.1 11.4 %collective-permute-done.3 = bf16[96,3072]{1,0:T(8,128)(2,1)S(1)} collective-permute-done((bf16[96,3072]{1,0:T(8,128)(2,1)S(1)}, bf16[96,3072]{1,0:T(8,128)(2,1)S(1)}, u32[]{:S(2)}, u32[]{:S(2)}) %collective-permute-start.3) | collective-permute-done | bytes 589856 | tf_op jit(solution)/shard_map/ppermute | solution.py:25
  114.5 11.4 %collective-permute-done.4 = bf16[96,3072]{1,0:T(8,128)(2,1)S(1)} collective-permute-done((bf16[96,3072]{1,0:T(8,128)(2,1)S(1)}, bf16[96,3072]{1,0:T(8,128)(2,1)S(1)}, u32[]{:S(2)}, u32[]{:S(2)}) %collective-permute-start.4) | collective-permute-done | bytes 589856 | tf_op jit(solution)/shard_map/ppermute | solution.py:25
  133.2 11.0 %collective-permute-done.5 = bf16[96,3072]{1,0:T(8,128)(2,1)S(1)} collective-permute-done((bf16[96,3072]{1,0:T(8,128)(2,1)S(1)}, bf16[96,3072]{1,0:T(8,128)(2,1)S(1)}, u32[]{:S(2)}, u32[]{:S(2)}) %collective-permute-start.5) | collective-permute-done | bytes 589856 | tf_op jit(solution)/shard_map/ppermute | solution.py:25
  151.2 11.4 %collective-permute-done.6 = bf16[96,3072]{1,0:T(8,128)(2,1)S(1)} collective-permute-done((bf16[96,3072]{1,0:T(8,128)(2,1)S(1)}, bf16[96,3072]{1,0:T(8,128)(2,1)S(1)}, u32[]{:S(2)}, u32[]{:S(2)}) %collective-permute-start.6) | collective-permute-done | bytes 589856 | tf_op jit(solution)/shard_map/ppermute | solution.py:25
  169.5 11.4 %collective-permute-done.7 = bf16[96,3072]{1,0:T(8,128)(2,1)S(1)} collective-permute-done((bf16[96,3072]{1,0:T(8,128)(2,1)S(1)}, bf16[96,3072]{1,0:T(8,128)(2,1)S(1)}, u32[]{:S(2)}, u32[]{:S(2)}) %collective-permute-start.7) | collective-permute-done | bytes 589856 | tf_op jit(solution)/shard_map/ppermute | solution.py:25
  188.0 11.3 %collective-permute-done.8 = bf16[96,3072]{1,0:T(8,128)(2,1)S(1)} collective-permute-done((bf16[96,3072]{1,0:T(8,128)(2,1)S(1)}, bf16[96,3072]{1,0:T(8,128)(2,1)S(1)}, u32[]{:S(2)}, u32[]{:S(2)}) %collective-permute-start.8) | collective-permute-done | bytes 589856 | tf_op jit(solution)/shard_map/ppermute | solution.py:25
  206.2 11.4 %collective-permute-done.9 = bf16[96,3072]{1,0:T(8,128)(2,1)S(1)} collective-permute-done((bf16[96,3072]{1,0:T(8,128)(2,1)S(1)}, bf16[96,3072]{1,0:T(8,128)(2,1)S(1)}, u32[]{:S(2)}, u32[]{:S(2)}) %collective-permute-start.9) | collective-permute-done | bytes 589856 | tf_op jit(solution)/shard_map/ppermute | solution.py:25
  224.6 11.4 %collective-permute-done.10 = bf16[96,3072]{1,0:T(8,128)(2,1)S(1)} collective-permute-done((bf16[96,3072]{1,0:T(8,128)(2,1)S(1)}, bf16[96,3072]{1,0:T(8,128)(2,1)S(1)}, u32[]{:S(2)}, u32[]{:S(2)}) %collective-permute-start.10) | collective-permute-done | bytes 589856 | tf_op jit(solution)/shard_map/ppermute | solution.py:25
  243.2 11.1 %collective-permute-done.11 = bf16[96,3072]{1,0:T(8,128)(2,1)S(1)} collective-permute-done((bf16[96,3072]{1,0:T(8,128)(2,1)S(1)}, bf16[96,3072]{1,0:T(8,128)(2,1)S(1)}, u32[]{:S(2)}, u32[]{:S(2)}) %collective-permute-start.11) | collective-permute-done | bytes 589856 | tf_op jit(solution)/shard_map/ppermute | solution.py:25
  261.3 11.4 %collective-permute-done.12 = bf16[96,3072]{1,0:T(8,128)(2,1)S(1)} collective-permute-done((bf16[96,3072]{1,0:T(8,128)(2,1)S(1)}, bf16[96,3072]{1,0:T(8,128)(2,1)S(1)}, u32[]{:S(2)}, u32[]{:S(2)}) %collective-permute-start.12) | collective-permute-done | bytes 589856 | tf_op jit(solution)/shard_map/ppermute | solution.py:25
  279.7 11.4 %collective-permute-done.13 = bf16[96,3072]{1,0:T(8,128)(2,1)S(1)} collective-permute-done((bf16[96,3072]{1,0:T(8,128)(2,1)S(1)}, bf16[96,3072]{1,0:T(8,128)(2,1)S(1)}, u32[]{:S(2)}, u32[]{:S(2)}) %collective-permute-start.13) | collective-permute-done | bytes 589856 | tf_op jit(solution)/shard_map/ppermute | solution.py:25
  298.4 11.0 %collective-permute-done.14 = bf16[96,3072]{1,0:T(8,128)(2,1)S(1)} collective-permute-done((bf16[96,3072]{1,0:T(8,128)(2,1)S(1)}, bf16[96,3072]{1,0:T(8,128)(2,1)S(1)}, u32[]{:S(2)}, u32[]{:S(2)}) %collective-permute-start.14) | collective-permute-done | bytes 589856 | tf_op jit(solution)/shard_map/ppermute | solution.py:25
  316.3 11.4 %collective-permute-done.15 = bf16[96,3072]{1,0:T(8,128)(2,1)S(1)} collective-permute-done((bf16[96,3072]{1,0:T(8,128)(2,1)S(1)}, bf16[96,3072]{1,0:T(8,128)(2,1)S(1)}, u32[]{:S(2)}, u32[]{:S(2)}) %collective-permute-start.15) | collective-permute-done | bytes 589856 | tf_op jit(solution)/shard_map/ppermute | solution.py:25
  334.7 11.4 %collective-permute-done.16 = bf16[96,3072]{1,0:T(8,128)(2,1)S(1)} collective-permute-done((bf16[96,3072]{1,0:T(8,128)(2,1)S(1)}, bf16[96,3072]{1,0:T(8,128)(2,1)S(1)}, u32[]{:S(2)}, u32[]{:S(2)}) %collective-permute-start.16) | collective-permute-done | bytes 589856 | tf_op jit(solution)/shard_map/ppermute | solution.py:25
  353.2 11.2 %collective-permute-done.17 = bf16[96,3072]{1,0:T(8,128)(2,1)S(1)} collective-permute-done((bf16[96,3072]{1,0:T(8,128)(2,1)S(1)}, bf16[96,3072]{1,0:T(8,128)(2,1)S(1)}, u32[]{:S(2)}, u32[]{:S(2)}) %collective-permute-start.17) | collective-permute-done | bytes 589856 | tf_op jit(solution)/shard_map/ppermute | solution.py:25
  369.5 10.6 %fusion.290 = (f32[96]{0:T(128)}, f32[96]{0:T(128)S(1)}, f32[96]{0:T(128)}, f32[96]{0:T(128)}, f32[96]{0:T(128)}, /*index=5*/f32[96]{0:T(128)}, f32[96]{0:T(128)...) fusion(bf16[6,96,3072]{2,1,0:T(8,128)(2,1)S(1)} %bitcast_dynami, ...), kind=kOutput, calls=%fused_computation.414 | convolution fusion | flops 1829632000 | bytes 31276928 | tf_op jit(solution)/shard_map/dot_general | solution.py:47
  871.7 12.3 %collective-permute-done.59 = bf16[96,3072]{1,0:T(8,128)(2,1)S(1)} collective-permute-done((bf16[96,3072]{1,0:T(8,128)(2,1)S(1)}, bf16[96,3072]{1,0:T(8,128)(2,1)S(1)}, u32[]{:S(2)}, u32[]{:S(2)}) %collective-permute-start.59) | collective-permute-done | bytes 589856 | tf_op jit(solution)/shard_map/ppermute | solution.py:123
  889.2 14.8 %add_add_fusion = f32[768,3072]{1,0:T(8,128)} fusion(f32[768,3072]{1,0:T(8,128)} %fusion.100, f32[768,3072]{1,0:T(8,128)} %fusion.84, f32[768,3072]{1,0:T(8,128)} %fusion.92, bf16[384,768]{1,0:T(8,128)(2,1)S(1)} %bitcast.978, bf16[96,3072]{1,0:T(8,128)(2,1)S(1)} %collective-permute-done.60, bf16[96,3072]{1,0:T(8,128)(2,1)S(1)} %collective-permute-done.59, ...), kind=kOutput, calls=%fused_computation.74 | convolution fusion | flops 1828454400 | bytes 40697856 | tf_op jit(solution)/shard_map/dot_general | solution.py:127
  906.8 54.2 %collective-permute-done.61 = bf16[384,3072]{1,0:T(8,128)(2,1)} collective-permute-done((bf16[384,3072]{1,0:T(8,128)(2,1)S(1)}, bf16[384,3072]{1,0:T(8,128)(2,1)}, u32[]{:S(2)}, u32[]{:S(2)}) %collective-permute-start.61) | collective-permute-done | bytes 2359328 | tf_op jit(solution)/shard_map/ppermute | solution.py:133
  (493 shorter events, 637.1 us)
Async XLA Ops:
  12.5 33.5 %collective-permute-start = (bf16[96,3072]{1,0:T(8,128)(2,1)}, bf16[96,3072]{1,0:T(8,128)(2,1)}, u32[]{:S(2)}, u32[]{:S(2)}) collective-permute-start(bf16[96,3072]{1,0:T(8,128)(2,1)} %get-tuple-element.149), channel_id=1, source_target_pairs={{0,8},{1,9},{2,10},{3,11},{4,12},{5,13},{6,14},{7,15},{8,16},{9,17... | collective-permute-start | bytes 1769480 | tf_op jit(solution)/shard_map/ppermute | solution.py:25
  14.5 355.0 %collective-permute-start.21 = (bf16[4,96,3072]{2,1,0:T(8,128)(2,1)}, bf16[4,96,3072]{2,1,0:T(8,128)(2,1)}, u32[]{:S(2)}, u32[]{:S(2)}) collective-permute-start(bf16[4,96,3072]{2,1,0:T(8,128)(2,1)} %param.5), channel_id=1, source_target_pairs={{0,4},{1,5},{2,6},{3,7},{4,0},{5,1},{6,2},{7,3},{8,12},{9,13},{10,... | collective-permute-start | bytes 7077896 | tf_op jit(solution)/shard_map/ppermute | solution.py:77
  492.2 218.9 %collective-permute-start.54 = (bf16[96,2,384]{2,1,0:T(2,128)(2,1)}, bf16[96,2,384]{2,1,0:T(2,128)(2,1)}, u32[]{:S(2)}, u32[]{:S(2)}) collective-permute-start(bf16[96,2,384]{2,1,0:T(2,128)(2,1)} %pad_maximum_fusion.13), channel_id=1, source_target_pairs={{0,1},{1,2},{2,3},{3,0},{4,5},{5,6},{6,7},{7,4},{8,9},{9,10},{10,1... | collective-permute-start | bytes 442376 | tf_op jit(solution)/shard_map/ppermute | solution.py:124
  513.8 201.3 %collective-permute-start.55 = (bf16[96,2,384]{2,1,0:T(2,128)(2,1)}, bf16[96,2,384]{2,1,0:T(2,128)(2,1)}, u32[]{:S(2)}, u32[]{:S(2)}) collective-permute-start(bf16[96,2,384]{2,1,0:T(2,128)(2,1)} %pad_maximum_fusion.14), channel_id=1, source_target_pairs={{0,2},{1,3},{2,0},{3,1},{4,6},{5,7},{6,4},{7,5},{8,10},{9,11},{10,... | collective-permute-start | bytes 442376 | tf_op jit(solution)/shard_map/ppermute | solution.py:124
  518.6 197.1 %collective-permute-start.56 = (bf16[96,2,384]{2,1,0:T(2,128)(2,1)}, bf16[96,2,384]{2,1,0:T(2,128)(2,1)}, u32[]{:S(2)}, u32[]{:S(2)}) collective-permute-start(bf16[96,2,384]{2,1,0:T(2,128)(2,1)} %pad_maximum_fusion.15), channel_id=1, source_target_pairs={{0,3},{1,0},{2,1},{3,2},{4,7},{5,4},{6,5},{7,6},{8,11},{9,8},{10,9... | collective-permute-start | bytes 442376 | tf_op jit(solution)/shard_map/ppermute | solution.py:124
  562.2 170.6 %collective-permute-start.40 = (bf16[96,2,384]{2,1,0:T(2,128)(2,1)}, bf16[96,2,384]{2,1,0:T(2,128)(2,1)}, u32[]{:S(2)}, u32[]{:S(2)}) collective-permute-start(bf16[96,2,384]{2,1,0:T(2,128)(2,1)} %pad_maximum_fusion.7), channel_id=1, source_target_pairs={{0,1},{1,2},{2,3},{3,0},{4,5},{5,6},{6,7},{7,4},{8,9},{9,10},{10,1... | collective-permute-start | bytes 442376 | tf_op jit(solution)/shard_map/ppermute | solution.py:124
  701.4 21.1 %collective-permute-start.35 = (bf16[96,3072]{1,0:T(8,128)(2,1)S(1)}, bf16[96,3072]{1,0:T(8,128)(2,1)S(1)}, u32[]{:S(2)}, u32[]{:S(2)}) collective-permute-start(bf16[96,3072]{1,0:T(8,128)(2,1)S(1)} %fusion.257), channel_id=1, source_target_pairs={{8,0},{9,1},{10,2},{11,3},{12,4},{13,5},{14,6},{15,7},{16,8},{17,9... | collective-permute-start | bytes 1769480 | tf_op jit(solution)/shard_map/ppermute | solution.py:25
  711.1 24.4 %collective-permute-start.41 = (bf16[96,2,384]{2,1,0:T(2,128)(2,1)}, bf16[96,2,384]{2,1,0:T(2,128)(2,1)}, u32[]{:S(2)}, u32[]{:S(2)}) collective-permute-start(bf16[96,2,384]{2,1,0:T(2,128)(2,1)} %pad_maximum_fusion.8), channel_id=1, source_target_pairs={{0,2},{1,3},{2,0},{3,1},{4,6},{5,7},{6,4},{7,5},{8,10},{9,11},{10,... | collective-permute-start | bytes 442376 | tf_op jit(solution)/shard_map/ppermute | solution.py:124
  715.7 27.6 %collective-permute-start.18 = (bf16[96,2,384]{2,1,0:T(2,128)(2,1)}, bf16[96,2,384]{2,1,0:T(2,128)(2,1)S(1)}, u32[]{:S(2)}, u32[]{:S(2)}) collective-permute-start(bf16[96,2,384]{2,1,0:T(2,128)(2,1)} %pad_maximum_fusion.4), channel_id=1, source_target_pairs={{0,1},{1,2},{2,3},{3,0},{4,5},{5,6},{6,7},{7,4},{8,9},{9,10},{10,1... | collective-permute-start | bytes 442376 | tf_op jit(solution)/shard_map/ppermute | solution.py:124
  722.5 22.7 %collective-permute-start.19 = (bf16[96,2,384]{2,1,0:T(2,128)(2,1)}, bf16[96,2,384]{2,1,0:T(2,128)(2,1)}, u32[]{:S(2)}, u32[]{:S(2)}) collective-permute-start(bf16[96,2,384]{2,1,0:T(2,128)(2,1)} %pad_maximum_fusion.5), channel_id=1, source_target_pairs={{0,2},{1,3},{2,0},{3,1},{4,6},{5,7},{6,4},{7,5},{8,10},{9,11},{10,... | collective-permute-start | bytes 442376 | tf_op jit(solution)/shard_map/ppermute | solution.py:124
  735.5 25.9 %collective-permute-start.36 = (bf16[96,3072]{1,0:T(8,128)(2,1)S(1)}, bf16[96,3072]{1,0:T(8,128)(2,1)S(1)}, u32[]{:S(2)}, u32[]{:S(2)}) collective-permute-start(bf16[96,3072]{1,0:T(8,128)(2,1)S(1)} %fusion.260), channel_id=1, source_target_pairs={{8,0},{9,1},{10,2},{11,3},{12,4},{13,5},{14,6},{15,7},{16,8},{17,9... | collective-permute-start | bytes 1769480 | tf_op jit(solution)/shard_map/ppermute | solution.py:25
  775.6 25.5 %collective-permute-start.37 = (bf16[96,3072]{1,0:T(8,128)(2,1)}, bf16[96,3072]{1,0:T(8,128)(2,1)}, u32[]{:S(2)}, u32[]{:S(2)}) collective-permute-start(bf16[96,3072]{1,0:T(8,128)(2,1)} %slice_bitcast_fusion.3), channel_id=1, source_target_pairs={{0,1},{1,2},{2,3},{3,0},{4,5},{5,6},{6,7},{7,4},{8,9},{9,10},{10,1... | collective-permute-start | bytes 1769480 | tf_op jit(solution)/shard_map/ppermute | solution.py:123
  776.1 30.8 %collective-permute-start.38 = (bf16[96,3072]{1,0:T(8,128)(2,1)}, bf16[96,3072]{1,0:T(8,128)(2,1)}, u32[]{:S(2)}, u32[]{:S(2)}) collective-permute-start(bf16[96,3072]{1,0:T(8,128)(2,1)} %slice_bitcast_fusion.3), channel_id=1, source_target_pairs={{0,2},{1,3},{2,0},{3,1},{4,6},{5,7},{6,4},{7,5},{8,10},{9,11},{10,... | collective-permute-start | bytes 1769480 | tf_op jit(solution)/shard_map/ppermute | solution.py:123
  779.7 27.2 %collective-permute-start.39 = (bf16[96,3072]{1,0:T(8,128)(2,1)}, bf16[96,3072]{1,0:T(8,128)(2,1)}, u32[]{:S(2)}, u32[]{:S(2)}) collective-permute-start(bf16[96,3072]{1,0:T(8,128)(2,1)} %slice_bitcast_fusion.3), channel_id=1, source_target_pairs={{0,3},{1,0},{2,1},{3,2},{4,7},{5,4},{6,5},{7,6},{8,11},{9,8},{10,9... | collective-permute-start | bytes 1769480 | tf_op jit(solution)/shard_map/ppermute | solution.py:123
  791.5 23.4 %collective-permute-start.50 = (bf16[96,3072]{1,0:T(8,128)(2,1)S(1)}, bf16[96,3072]{1,0:T(8,128)(2,1)S(1)}, u32[]{:S(2)}, u32[]{:S(2)}) collective-permute-start(bf16[96,3072]{1,0:T(8,128)(2,1)S(1)} %fusion.266), channel_id=1, source_target_pairs={{8,0},{9,1},{10,2},{11,3},{12,4},{13,5},{14,6},{15,7},{16,8},{17,9... | collective-permute-start | bytes 1769480 | tf_op jit(solution)/shard_map/ppermute | solution.py:25
  800.7 37.8 %collective-permute-start.44 = (bf16[96,3072]{1,0:T(8,128)(2,1)}, bf16[96,3072]{1,0:T(8,128)(2,1)}, u32[]{:S(2)}, u32[]{:S(2)}) collective-permute-start(bf16[96,3072]{1,0:T(8,128)(2,1)} %slice_bitcast_fusion.2), channel_id=1, source_target_pairs={{0,1},{1,2},{2,3},{3,0},{4,5},{5,6},{6,7},{7,4},{8,9},{9,10},{10,1... | collective-permute-start | bytes 1769480 | tf_op jit(solution)/shard_map/ppermute | solution.py:123
  801.2 41.8 %collective-permute-start.45 = (bf16[96,3072]{1,0:T(8,128)(2,1)}, bf16[96,3072]{1,0:T(8,128)(2,1)}, u32[]{:S(2)}, u32[]{:S(2)}) collective-permute-start(bf16[96,3072]{1,0:T(8,128)(2,1)} %slice_bitcast_fusion.2), channel_id=1, source_target_pairs={{0,2},{1,3},{2,0},{3,1},{4,6},{5,7},{6,4},{7,5},{8,10},{9,11},{10,... | collective-permute-start | bytes 1769480 | tf_op jit(solution)/shard_map/ppermute | solution.py:123
  806.9 36.1 %collective-permute-start.46 = (bf16[96,3072]{1,0:T(8,128)(2,1)}, bf16[96,3072]{1,0:T(8,128)(2,1)}, u32[]{:S(2)}, u32[]{:S(2)}) collective-permute-start(bf16[96,3072]{1,0:T(8,128)(2,1)} %slice_bitcast_fusion.2), channel_id=1, source_target_pairs={{0,3},{1,0},{2,1},{3,2},{4,7},{5,4},{6,5},{7,6},{8,11},{9,8},{10,9... | collective-permute-start | bytes 1769480 | tf_op jit(solution)/shard_map/ppermute | solution.py:123
  834.5 24.7 %collective-permute-start.52 = (bf16[96,3072]{1,0:T(8,128)(2,1)S(1)}, bf16[96,3072]{1,0:T(8,128)(2,1)S(1)}, u32[]{:S(2)}, u32[]{:S(2)}) collective-permute-start(bf16[96,3072]{1,0:T(8,128)(2,1)S(1)} %slice_bitcast_fusion.1), channel_id=1, source_target_pairs={{0,2},{1,3},{2,0},{3,1},{4,6},{5,7},{6,4},{7,5},{8,10},{9,11},{10,... | collective-permute-start | bytes 1769480 | tf_op jit(solution)/shard_map/ppermute | solution.py:123
  838.4 26.4 %collective-permute-start.53 = (bf16[96,3072]{1,0:T(8,128)(2,1)S(1)}, bf16[96,3072]{1,0:T(8,128)(2,1)S(1)}, u32[]{:S(2)}, u32[]{:S(2)}) collective-permute-start(bf16[96,3072]{1,0:T(8,128)(2,1)S(1)} %slice_bitcast_fusion.1), channel_id=1, source_target_pairs={{0,3},{1,0},{2,1},{3,2},{4,7},{5,4},{6,5},{7,6},{8,11},{9,8},{10,9... | collective-permute-start | bytes 1769480 | tf_op jit(solution)/shard_map/ppermute | solution.py:123
  842.9 28.8 %collective-permute-start.58 = (bf16[96,3072]{1,0:T(8,128)(2,1)S(1)}, bf16[96,3072]{1,0:T(8,128)(2,1)S(1)}, u32[]{:S(2)}, u32[]{:S(2)}) collective-permute-start(bf16[96,3072]{1,0:T(8,128)(2,1)S(1)} %slice_bitcast_fusion), channel_id=1, source_target_pairs={{0,1},{1,2},{2,3},{3,0},{4,5},{5,6},{6,7},{7,4},{8,9},{9,10},{10,1... | collective-permute-start | bytes 1769480 | tf_op jit(solution)/shard_map/ppermute | solution.py:123
  843.0 41.0 %collective-permute-start.59 = (bf16[96,3072]{1,0:T(8,128)(2,1)S(1)}, bf16[96,3072]{1,0:T(8,128)(2,1)S(1)}, u32[]{:S(2)}, u32[]{:S(2)}) collective-permute-start(bf16[96,3072]{1,0:T(8,128)(2,1)S(1)} %slice_bitcast_fusion), channel_id=1, source_target_pairs={{0,2},{1,3},{2,0},{3,1},{4,6},{5,7},{6,4},{7,5},{8,10},{9,11},{10,... | collective-permute-start | bytes 1769480 | tf_op jit(solution)/shard_map/ppermute | solution.py:123
  845.2 44.0 %collective-permute-start.60 = (bf16[96,3072]{1,0:T(8,128)(2,1)S(1)}, bf16[96,3072]{1,0:T(8,128)(2,1)S(1)}, u32[]{:S(2)}, u32[]{:S(2)}) collective-permute-start(bf16[96,3072]{1,0:T(8,128)(2,1)S(1)} %slice_bitcast_fusion), channel_id=1, source_target_pairs={{0,3},{1,0},{2,1},{3,2},{4,7},{5,4},{6,5},{7,6},{8,11},{9,8},{10,9... | collective-permute-start | bytes 1769480 | tf_op jit(solution)/shard_map/ppermute | solution.py:123
  906.7 54.3 %collective-permute-start.61 = (bf16[384,3072]{1,0:T(8,128)(2,1)S(1)}, bf16[384,3072]{1,0:T(8,128)(2,1)}, u32[]{:S(2)}, u32[]{:S(2)}) collective-permute-start(bf16[384,3072]{1,0:T(8,128)(2,1)S(1)} %fusion.82), channel_id=1, source_target_pairs={{0,4},{1,5},{2,6},{3,7},{4,0},{5,1},{6,2},{7,3},{8,12},{9,13},{10,... | collective-permute-start | bytes 7077896 | tf_op jit(solution)/shard_map/ppermute | solution.py:133
  (115 other events, 1253.9 us)

commit v6 on v5

--- a/solution.py
+++ b/solution.py
@@ -54,7 +54,11 @@
 
 def on_device(inputs, projection, cotangent):
     weight = projection[0]
+    split = 2
     micro, rows_mb, width = inputs.shape
+    micro, rows_mb = micro * split, rows_mb // split
+    inputs = inputs.reshape(micro, rows_mb, width)
+    cotangent = cotangent.reshape(micro, rows_mb, width)
     section = lax.axis_index("pipe")
     sections = lax.axis_size("pipe")
     replicas = lax.axis_size("dp")

time: 977 us -> 976 us (level)
  starting transfers between devices: 189 us -> 234 us
  waiting for transfers between devices: 338 us -> 294 us
  matrix products: 216 us -> 250 us
  other arithmetic: 143 us -> 122 us
  local copies, waits for them, and re-layouts: 77.8 us -> 61.1 us
    dot_general x4 -> x8, matrix products: 35.9 us -> 69.1 us  [on_device(): lax.dot_general(normed_rows, slope_rows, (((0,), (0,)), ((), ())), prefer...]
    ppermute x12 -> x24, waiting for transfers between devices: 31.9 us -> 7.39 us  [on_device(): slope_rows.append(lax.ppermute(finished, 'dp', pairs))]
    ppermute x36 -> x44, waiting for transfers between devices: 251 us -> 230 us  [relay(): return lax.ppermute(array, ('pipe', 'dp'), pairs)]
    dynamic_update_slice x18 -> x22, local copies, waits for them, and re-layouts: 19.4 us -> 1.01 us  [on_device(): lax.dynamic_update_index_in_dim(kept_gates, gate_value, slot, 0)]
    ppermute x12 -> x24, starting transfers between devices: 18.7 us -> 34.5 us  [on_device(): slope_rows.append(lax.ppermute(finished, 'dp', pairs))]
    ppermute x12 -> x24, starting transfers between devices: 22.9 us -> 37.7 us  [on_device(): normed_rows.append(lax.ppermute(wanted, 'dp', pairs))]
    ppermute x36 -> x44, starting transfers between devices: 146 us -> 161 us  [relay(): return lax.ppermute(array, ('pipe', 'dp'), pairs)]
    dot_general x19 -> x23, matrix products: 79.7 us -> 93.4 us  [forward_layer(): gate_value = jnp.dot(normed, weight, preferred_element_type=jnp.float32)]
  transfers between devices with their start and end apart: 62 -> 94, of which waited for: 40 -> 38; matrix products, arithmetic and copies ran while one was open for 34% -> 39% of each run, Pallas kernels for 0% -> 0%
where the time goes in v6:
time: 976 us; the launch traced here: 963 us
  waiting for transfers between devices  294 us (30%)
  matrix products  250 us (26%)
  starting transfers between devices  234 us (24%)
  other arithmetic  122 us (12%)
  local copies, waits for them, and re-layouts  61.1 us (6%)
    ppermute x44, waiting for transfers between devices, relay(): return lax.ppermute(array, ('pipe', 'dp'), pairs)  230 us
    ppermute x44, starting transfers between devices, relay(): return lax.ppermute(array, ('pipe', 'dp'), pairs)  161 us
    dot_general x23, matrix products, forward_layer(): gate_value = jnp.dot(normed, weight, preferred_element_type=jnp.float32)  93.4 us
    dot_general x22, matrix products, backward_layer(): back = jnp.dot(slope, weight_t, preferred_element_type=jnp.float32)  87.4 us
    dot_general x8, matrix products, on_device(): lax.dot_general(normed_rows, slope_rows, (((0,), (0,)), ((), ())), prefer...  69.1 us
    ppermute x1, waiting for transfers between devices, on_device(): lax.ppermute(theirs, 'dp', [(r, (r + ring) % replicas) for r in range(rep...  53.2 us
    dynamic_update_slice x23, other arithmetic, on_device(): kept_slopes = lax.dynamic_update_index_in_dim(kept_slopes, slope, slot, 0)  45.8 us
    ppermute x24, starting transfers between devices, on_device(): normed_rows.append(lax.ppermute(wanted, 'dp', pairs))  37.7 us
  transfers between devices with their start and end apart: 94, of which 38 were waited for; matrix products, arithmetic and copies ran while one was open for 39% of the time, Pallas kernels for 0%

profile of v6, /device:TPU:6, one launch (start us, length us, event | category | flops | bytes accessed | tf_op | source)
XLA Modules:
  0.0 963.0 jit_solution(15732720207093913206)
XLA Ops:
  1.2 9.9 %fusion.351 = (bf16[48,3072]{1,0:T(8,128)(2,1)S(1)}, f32[48,3072]{1,0:T(8,128)S(1)}) fusion(bf16[8,48,3072]{2,1,0:T(8,128)(2,1)} %bitcast.1209, s32[]{:T(128)S(6)} %min.277, pred[]{:T(512)S(6)} %eq.38, bf16[1,3072,3072]{2,1,0:T(8,128)(2,1)} %param.4, f32[48]{0:T(128)S(1)} %add_rsqrt_fusion.52), kind=kOutput, calls=%fused_computation.503 | convolution fusion | flops 907739136 | bytes 20351168 | tf_op jit(solution)/shard_map/dot_general | solution.py:37
  13.9 24.6 %copy.4 = bf16[1,3072,3072]{1,2,0:T(8,128)(2,1)} copy(bf16[1,3072,3072]{2,1,0:T(8,128)(2,1)} %param.4) | data formatting | bytes 37748736 | tf_op args[1]
  67.3 9.3 collective-permute-done.2
  83.0 9.3 collective-permute-done.3
  98.1 9.3 collective-permute-done.4
  113.3 9.3 collective-permute-done.5
  128.5 9.3 collective-permute-done.6
  143.8 9.2 collective-permute-done.7
  158.8 9.3 collective-permute-done.8
  174.0 9.3 collective-permute-done.9
  189.2 9.3 collective-permute-done.10
  204.6 9.1 collective-permute-done.11
  219.6 9.3 collective-permute-done.12
  234.7 9.3 collective-permute-done.13
  249.9 9.3 collective-permute-done.14
  280.3 9.3 collective-permute-done.16
  295.4 9.3 collective-permute-done.17
  310.6 9.3 collective-permute-done.18
  326.0 9.2 collective-permute-done.19
  341.0 9.3 collective-permute-done.20
  356.1 9.3 collective-permute-done.21
  396.8 12.7 %fusion.374 = (f32[48]{0:T(128)}, f32[48]{0:T(128)S(1)}, f32[48]{0:T(128)}, f32[48]{0:T(128)}, f32[48]{0:T(128)S(1)}, /*index=5*/f32[48]{0:T(128)S(1)}, f32[48]{...) fusion(bf16[10,48,3072]{2,1,0:T(8,128)(2,1)S(1)} %bitcast_dynam, ...), kind=kOutput, calls=%fused_computation.526 | convolution fusion | flops 914816000 | bytes 25080512 | tf_op jit(solution)/shard_map/dot_general | solution.py:47
  876.4 25.3 %add_add_fusion = f32[768,3072]{1,0:T(8,128)} fusion(f32[768,3072]{1,0:T(8,128)} %fusion.148, f32[768,3072]{1,0:T(8,128)} %fusion.140, f32[768,3072]{1,0:T(8,128)} %fusion.132, f32[768,3072]{1,0:T(8,128)} %fusion.124, f32[768,3072]{1,0:T(8,128)} %fusion.116, f32[768,3072]{1,0:T(8,128)} %fusion.100, f32[768,3072]{1,0:T(8,128)} %fusion.108, ...), kind=kOutput, calls=%fused_computation.90 | convolution fusion | flops 927203328 | bytes 76972032 | tf_op jit(solution)/shard_map/dot_general | solution.py:131
  904.5 53.2 %collective-permute-done.93 = bf16[384,3072]{1,0:T(8,128)(2,1)} collective-permute-done((bf16[384,3072]{1,0:T(8,128)(2,1)S(1)}, bf16[384,3072]{1,0:T(8,128)(2,1)}, u32[]{:S(2)}, u32[]{:S(2)}) %collective-permute-start.93) | collective-permute-done | bytes 2359328 | tf_op jit(solution)/shard_map/ppermute | solution.py:137
  (627 shorter events, 658.0 us)
Async XLA Ops:
  11.1 30.2 %collective-permute-start = (bf16[48,3072]{1,0:T(8,128)(2,1)S(1)}, bf16[48,3072]{1,0:T(8,128)(2,1)S(1)}, u32[]{:S(2)}, u32[]{:S(2)}) collective-permute-start(bf16[48,3072]{1,0:T(8,128)(2,1)S(1)} %get-tuple-element.225), channel_id=1, source_target_pairs={{0,8},{1,9},{2,10},{3,11},{4,12},{5,13},{6,14},{7,15},{8,16},{9,17... | collective-permute-start | bytes 884744 | tf_op jit(solution)/shard_map/ppermute | solution.py:25
  13.0 383.7 %collective-permute-start.25 = (bf16[8,48,3072]{2,1,0:T(8,128)(2,1)}, bf16[8,48,3072]{2,1,0:T(8,128)(2,1)}, u32[]{:S(2)}, u32[]{:S(2)}) collective-permute-start(bf16[8,48,3072]{2,1,0:T(8,128)(2,1)} %bitcast.48), channel_id=1, source_target_pairs={{0,4},{1,5},{2,6},{3,7},{4,0},{5,1},{6,2},{7,3},{8,12},{9,13},{10,... | collective-permute-start | bytes 7077896 | tf_op jit(solution)/shard_map/ppermute | solution.py:81
  369.2 270.1 %collective-permute-start.79 = (bf16[48,2,384]{2,1,0:T(2,128)(2,1)}, bf16[48,2,384]{2,1,0:T(2,128)(2,1)}, u32[]{:S(2)}, u32[]{:S(2)}) collective-permute-start(bf16[48,2,384]{2,1,0:T(2,128)(2,1)} %pad_maximum_fusion.26), channel_id=1, source_target_pairs={{0,1},{1,2},{2,3},{3,0},{4,5},{5,6},{6,7},{7,4},{8,9},{9,10},{10,1... | collective-permute-start | bytes 221192 | tf_op jit(solution)/shard_map/ppermute | solution.py:128
  371.9 267.8 %collective-permute-start.80 = (bf16[48,2,384]{2,1,0:T(2,128)(2,1)}, bf16[48,2,384]{2,1,0:T(2,128)(2,1)}, u32[]{:S(2)}, u32[]{:S(2)}) collective-permute-start(bf16[48,2,384]{2,1,0:T(2,128)(2,1)} %pad_maximum_fusion.27), channel_id=1, source_target_pairs={{0,2},{1,3},{2,0},{3,1},{4,6},{5,7},{6,4},{7,5},{8,10},{9,11},{10,... | collective-permute-start | bytes 221192 | tf_op jit(solution)/shard_map/ppermute | solution.py:128
  376.3 265.7 %collective-permute-start.81 = (bf16[48,2,384]{2,1,0:T(2,128)(2,1)}, bf16[48,2,384]{2,1,0:T(2,128)(2,1)}, u32[]{:S(2)}, u32[]{:S(2)}) collective-permute-start(bf16[48,2,384]{2,1,0:T(2,128)(2,1)} %pad_maximum_fusion.28), channel_id=1, source_target_pairs={{0,3},{1,0},{2,1},{3,2},{4,7},{5,4},{6,5},{7,6},{8,11},{9,8},{10,9... | collective-permute-start | bytes 221192 | tf_op jit(solution)/shard_map/ppermute | solution.py:128
  379.6 264.2 %collective-permute-start.86 = (bf16[48,2,384]{2,1,0:T(2,128)(2,1)}, bf16[48,2,384]{2,1,0:T(2,128)(2,1)}, u32[]{:S(2)}, u32[]{:S(2)}) collective-permute-start(bf16[48,2,384]{2,1,0:T(2,128)(2,1)} %pad_maximum_fusion.29), channel_id=1, source_target_pairs={{0,1},{1,2},{2,3},{3,0},{4,5},{5,6},{6,7},{7,4},{8,9},{9,10},{10,1... | collective-permute-start | bytes 221192 | tf_op jit(solution)/shard_map/ppermute | solution.py:128
  719.2 33.2 %collective-permute-start.50 = (bf16[48,3072]{1,0:T(8,128)(2,1)}, bf16[48,3072]{1,0:T(8,128)(2,1)}, u32[]{:S(2)}, u32[]{:S(2)}) collective-permute-start(bf16[48,3072]{1,0:T(8,128)(2,1)} %slice_bitcast_fusion.6), channel_id=1, source_target_pairs={{0,3},{1,0},{2,1},{3,2},{4,7},{5,4},{6,5},{7,6},{8,11},{9,8},{10,9... | collective-permute-start | bytes 884744 | tf_op jit(solution)/shard_map/ppermute | solution.py:127
  721.6 30.9 %collective-permute-start.49 = (bf16[48,3072]{1,0:T(8,128)(2,1)}, bf16[48,3072]{1,0:T(8,128)(2,1)}, u32[]{:S(2)}, u32[]{:S(2)}) collective-permute-start(bf16[48,3072]{1,0:T(8,128)(2,1)} %slice_bitcast_fusion.6), channel_id=1, source_target_pairs={{0,2},{1,3},{2,0},{3,1},{4,6},{5,7},{6,4},{7,5},{8,10},{9,11},{10,... | collective-permute-start | bytes 884744 | tf_op jit(solution)/shard_map/ppermute | solution.py:127
  728.7 28.2 %collective-permute-start.48 = (bf16[48,3072]{1,0:T(8,128)(2,1)}, bf16[48,3072]{1,0:T(8,128)(2,1)}, u32[]{:S(2)}, u32[]{:S(2)}) collective-permute-start(bf16[48,3072]{1,0:T(8,128)(2,1)} %slice_bitcast_fusion.6), channel_id=1, source_target_pairs={{0,1},{1,2},{2,3},{3,0},{4,5},{5,6},{6,7},{7,4},{8,9},{9,10},{10,1... | collective-permute-start | bytes 884744 | tf_op jit(solution)/shard_map/ppermute | solution.py:127
  743.1 32.2 %collective-permute-start.57 = (bf16[48,3072]{1,0:T(8,128)(2,1)}, bf16[48,3072]{1,0:T(8,128)(2,1)}, u32[]{:S(2)}, u32[]{:S(2)}) collective-permute-start(bf16[48,3072]{1,0:T(8,128)(2,1)} %slice_bitcast_fusion.5), channel_id=1, source_target_pairs={{0,3},{1,0},{2,1},{3,2},{4,7},{5,4},{6,5},{7,6},{8,11},{9,8},{10,9... | collective-permute-start | bytes 884744 | tf_op jit(solution)/shard_map/ppermute | solution.py:127
  745.5 30.6 %collective-permute-start.56 = (bf16[48,3072]{1,0:T(8,128)(2,1)}, bf16[48,3072]{1,0:T(8,128)(2,1)}, u32[]{:S(2)}, u32[]{:S(2)}) collective-permute-start(bf16[48,3072]{1,0:T(8,128)(2,1)} %slice_bitcast_fusion.5), channel_id=1, source_target_pairs={{0,2},{1,3},{2,0},{3,1},{4,6},{5,7},{6,4},{7,5},{8,10},{9,11},{10,... | collective-permute-start | bytes 884744 | tf_op jit(solution)/shard_map/ppermute | solution.py:127
  752.4 28.1 %collective-permute-start.55 = (bf16[48,3072]{1,0:T(8,128)(2,1)}, bf16[48,3072]{1,0:T(8,128)(2,1)}, u32[]{:S(2)}, u32[]{:S(2)}) collective-permute-start(bf16[48,3072]{1,0:T(8,128)(2,1)} %slice_bitcast_fusion.5), channel_id=1, source_target_pairs={{0,1},{1,2},{2,3},{3,0},{4,5},{5,6},{6,7},{7,4},{8,9},{9,10},{10,1... | collective-permute-start | bytes 884744 | tf_op jit(solution)/shard_map/ppermute | solution.py:127
  767.0 32.0 %collective-permute-start.64 = (bf16[48,3072]{1,0:T(8,128)(2,1)}, bf16[48,3072]{1,0:T(8,128)(2,1)}, u32[]{:S(2)}, u32[]{:S(2)}) collective-permute-start(bf16[48,3072]{1,0:T(8,128)(2,1)} %slice_bitcast_fusion.4), channel_id=1, source_target_pairs={{0,3},{1,0},{2,1},{3,2},{4,7},{5,4},{6,5},{7,6},{8,11},{9,8},{10,9... | collective-permute-start | bytes 884744 | tf_op jit(solution)/shard_map/ppermute | solution.py:127
  770.2 29.0 %collective-permute-start.63 = (bf16[48,3072]{1,0:T(8,128)(2,1)}, bf16[48,3072]{1,0:T(8,128)(2,1)}, u32[]{:S(2)}, u32[]{:S(2)}) collective-permute-start(bf16[48,3072]{1,0:T(8,128)(2,1)} %slice_bitcast_fusion.4), channel_id=1, source_target_pairs={{0,2},{1,3},{2,0},{3,1},{4,6},{5,7},{6,4},{7,5},{8,10},{9,11},{10,... | collective-permute-start | bytes 884744 | tf_op jit(solution)/shard_map/ppermute | solution.py:127
  775.3 28.4 %collective-permute-start.62 = (bf16[48,3072]{1,0:T(8,128)(2,1)}, bf16[48,3072]{1,0:T(8,128)(2,1)}, u32[]{:S(2)}, u32[]{:S(2)}) collective-permute-start(bf16[48,3072]{1,0:T(8,128)(2,1)} %slice_bitcast_fusion.4), channel_id=1, source_target_pairs={{0,1},{1,2},{2,3},{3,0},{4,5},{5,6},{6,7},{7,4},{8,9},{9,10},{10,1... | collective-permute-start | bytes 884744 | tf_op jit(solution)/shard_map/ppermute | solution.py:127
  789.8 31.8 %collective-permute-start.71 = (bf16[48,3072]{1,0:T(8,128)(2,1)S(1)}, bf16[48,3072]{1,0:T(8,128)(2,1)}, u32[]{:S(2)}, u32[]{:S(2)}) collective-permute-start(bf16[48,3072]{1,0:T(8,128)(2,1)S(1)} %slice_bitcast_fusion.3), channel_id=1, source_target_pairs={{0,3},{1,0},{2,1},{3,2},{4,7},{5,4},{6,5},{7,6},{8,11},{9,8},{10,9... | collective-permute-start | bytes 884744 | tf_op jit(solution)/shard_map/ppermute | solution.py:127
  792.2 30.2 %collective-permute-start.70 = (bf16[48,3072]{1,0:T(8,128)(2,1)S(1)}, bf16[48,3072]{1,0:T(8,128)(2,1)}, u32[]{:S(2)}, u32[]{:S(2)}) collective-permute-start(bf16[48,3072]{1,0:T(8,128)(2,1)S(1)} %slice_bitcast_fusion.3), channel_id=1, source_target_pairs={{0,2},{1,3},{2,0},{3,1},{4,6},{5,7},{6,4},{7,5},{8,10},{9,11},{10,... | collective-permute-start | bytes 884744 | tf_op jit(solution)/shard_map/ppermute | solution.py:127
  799.1 27.7 %collective-permute-start.69 = (bf16[48,3072]{1,0:T(8,128)(2,1)S(1)}, bf16[48,3072]{1,0:T(8,128)(2,1)}, u32[]{:S(2)}, u32[]{:S(2)}) collective-permute-start(bf16[48,3072]{1,0:T(8,128)(2,1)S(1)} %slice_bitcast_fusion.3), channel_id=1, source_target_pairs={{0,1},{1,2},{2,3},{3,0},{4,5},{5,6},{6,7},{7,4},{8,9},{9,10},{10,1... | collective-permute-start | bytes 884744 | tf_op jit(solution)/shard_map/ppermute | solution.py:127
  813.1 32.1 %collective-permute-start.78 = (bf16[48,3072]{1,0:T(8,128)(2,1)S(1)}, bf16[48,3072]{1,0:T(8,128)(2,1)}, u32[]{:S(2)}, u32[]{:S(2)}) collective-permute-start(bf16[48,3072]{1,0:T(8,128)(2,1)S(1)} %slice_bitcast_fusion.2), channel_id=1, source_target_pairs={{0,3},{1,0},{2,1},{3,2},{4,7},{5,4},{6,5},{7,6},{8,11},{9,8},{10,9... | collective-permute-start | bytes 884744 | tf_op jit(solution)/shard_map/ppermute | solution.py:127
  816.1 29.2 %collective-permute-start.77 = (bf16[48,3072]{1,0:T(8,128)(2,1)S(1)}, bf16[48,3072]{1,0:T(8,128)(2,1)}, u32[]{:S(2)}, u32[]{:S(2)}) collective-permute-start(bf16[48,3072]{1,0:T(8,128)(2,1)S(1)} %slice_bitcast_fusion.2), channel_id=1, source_target_pairs={{0,2},{1,3},{2,0},{3,1},{4,6},{5,7},{6,4},{7,5},{8,10},{9,11},{10,... | collective-permute-start | bytes 884744 | tf_op jit(solution)/shard_map/ppermute | solution.py:127
  821.6 28.3 %collective-permute-start.76 = (bf16[48,3072]{1,0:T(8,128)(2,1)S(1)}, bf16[48,3072]{1,0:T(8,128)(2,1)}, u32[]{:S(2)}, u32[]{:S(2)}) collective-permute-start(bf16[48,3072]{1,0:T(8,128)(2,1)S(1)} %slice_bitcast_fusion.2), channel_id=1, source_target_pairs={{0,1},{1,2},{2,3},{3,0},{4,5},{5,6},{6,7},{7,4},{8,9},{9,10},{10,1... | collective-permute-start | bytes 884744 | tf_op jit(solution)/shard_map/ppermute | solution.py:127
  836.1 26.2 %collective-permute-start.85 = (bf16[48,3072]{1,0:T(8,128)(2,1)S(1)}, bf16[48,3072]{1,0:T(8,128)(2,1)}, u32[]{:S(2)}, u32[]{:S(2)}) collective-permute-start(bf16[48,3072]{1,0:T(8,128)(2,1)S(1)} %slice_bitcast_fusion.1), channel_id=1, source_target_pairs={{0,3},{1,0},{2,1},{3,2},{4,7},{5,4},{6,5},{7,6},{8,11},{9,8},{10,9... | collective-permute-start | bytes 884744 | tf_op jit(solution)/shard_map/ppermute | solution.py:127
  838.4 24.6 %collective-permute-start.84 = (bf16[48,3072]{1,0:T(8,128)(2,1)S(1)}, bf16[48,3072]{1,0:T(8,128)(2,1)}, u32[]{:S(2)}, u32[]{:S(2)}) collective-permute-start(bf16[48,3072]{1,0:T(8,128)(2,1)S(1)} %slice_bitcast_fusion.1), channel_id=1, source_target_pairs={{0,2},{1,3},{2,0},{3,1},{4,6},{5,7},{6,4},{7,5},{8,10},{9,11},{10,... | collective-permute-start | bytes 884744 | tf_op jit(solution)/shard_map/ppermute | solution.py:127
  904.4 53.3 %collective-permute-start.93 = (bf16[384,3072]{1,0:T(8,128)(2,1)S(1)}, bf16[384,3072]{1,0:T(8,128)(2,1)}, u32[]{:S(2)}, u32[]{:S(2)}) collective-permute-start(bf16[384,3072]{1,0:T(8,128)(2,1)S(1)} %fusion.98), channel_id=1, source_target_pairs={{0,4},{1,5},{2,6},{3,7},{4,0},{5,1},{6,2},{7,3},{8,12},{9,13},{10,... | collective-permute-start | bytes 7077896 | tf_op jit(solution)/shard_map/ppermute | solution.py:137
  (141 other events, 1834.9 us)

commit v7 on v5

--- a/solution.py
+++ b/solution.py
@@ -76,6 +76,12 @@
     half = replicas // 2
     cotangent = lax.ppermute(cotangent, "dp", [(r, (r + half) % replicas) for r in range(replicas)])
     weight_t = with_layout_constraint(jnp.transpose(weight), Layout((0, 1)))
+    split = 2
+    kept_inputs = kept_inputs.reshape(split * (micro + 2), rows_mb // split, width)
+    kept_gates = kept_gates.reshape(split * (micro + 2), rows_mb // split, width)
+    micro, rows_mb = micro * split, rows_mb // split
+    cotangent = cotangent.reshape(micro, rows_mb, width)
+    ticks = micro + sections - 1
     kept_slopes = jnp.zeros((micro + 2, rows_mb, width), jnp.bfloat16)
     incoming = jnp.zeros((rows_mb, width), jnp.bfloat16)
     cols = width // replicas
@@ -83,14 +89,16 @@
     rep = lax.axis_index("dp")
     side = rep // ring
     place = rep % ring
-    partial = jnp.zeros((2 * cols, width), jnp.float32)
+    mine = jnp.zeros((cols, width), jnp.float32)
+    theirs = jnp.zeros((cols, width), jnp.float32)
     for tick in range(ticks):
         batch = tick - (sections - 1 - section)
         slot = jnp.clip(batch + 1, 0, micro + 1)
         first = lax.dynamic_index_in_dim(cotangent, jnp.clip(batch, 0, micro - 1), 0, keepdims=False)
         source = jnp.where(section == sections - 1, first, incoming)
-        stored_input = lax.dynamic_index_in_dim(kept_inputs, slot, 0, keepdims=False)
-        stored_gate = lax.dynamic_index_in_dim(kept_gates, slot, 0, keepdims=False)
+        stored = jnp.clip(batch + split, 0, split * (micro // split + 2) - 1)
+        stored_input = lax.dynamic_index_in_dim(kept_inputs, stored, 0, keepdims=False)
+        stored_gate = lax.dynamic_index_in_dim(kept_gates, stored, 0, keepdims=False)
         down, slope = backward_layer(stored_input, stored_gate, source, weight_t)
         kept_slopes = lax.dynamic_update_index_in_dim(kept_slopes, slope, slot, 0)
         if tick + 1 < ticks:
@@ -98,7 +106,7 @@
         done = tick - (sections - 1)
         if done >= 0:
             finished, kept_slopes = lax.optimization_barrier((kept_slopes[done + 1], kept_slopes))
-            floats, factor = norm_factor(kept_inputs[done + 1])
+            floats, factor = norm_factor(kept_inputs[done + split])
             normed = (floats * factor).astype(jnp.bfloat16).reshape(rows_mb, replicas, cols)
             slope_rows = []
             normed_rows = []
@@ -123,14 +131,19 @@
                 slope_rows.append(lax.ppermute(finished, "dp", pairs))
                 normed_rows.append(lax.ppermute(wanted, "dp", pairs))
             slope_rows = jnp.concatenate(slope_rows, axis=0)
-            normed_rows = jnp.concatenate(normed_rows, axis=0).reshape(ring * rows_mb, 2 * cols)
-            partial = partial + lax.dot_general(
-                normed_rows, slope_rows, (((0,), (0,)), ((), ())), preferred_element_type=jnp.float32
+            normed_rows = jnp.concatenate(normed_rows, axis=0)
+            contract = (((0,), (0,)), ((), ()))
+            theirs = theirs + lax.dot_general(
+                lax.dynamic_index_in_dim(normed_rows, 1 - side, 1, keepdims=False),
+                slope_rows, contract, preferred_element_type=jnp.float32,
             )
-    partial = partial.reshape(2, cols, width)
-    mine = lax.dynamic_index_in_dim(partial, side, 0, keepdims=False)
-    theirs = lax.dynamic_index_in_dim(partial, 1 - side, 0, keepdims=False).astype(jnp.bfloat16)
-    theirs = lax.ppermute(theirs, "dp", [(r, (r + ring) % replicas) for r in range(replicas)])
+            mine = mine + lax.dot_general(
+                lax.dynamic_index_in_dim(normed_rows, side, 1, keepdims=False),
+                slope_rows, contract, preferred_element_type=jnp.float32,
+            )
+    theirs = lax.ppermute(
+        theirs.astype(jnp.bfloat16), "dp", [(r, (r + ring) % replicas) for r in range(replicas)]
+    )
     factor_out = 1.0 / math.sqrt(micro * rows_mb * replicas)
     return ((mine + theirs.astype(jnp.float32)) * factor_out).astype(jnp.bfloat16)[None]
 

time: 977 us -> 1110 us (1.14)
  matrix products: 216 us -> 346 us
  starting transfers between devices: 189 us -> 238 us
  waiting for transfers between devices: 338 us -> 307 us
  local copies, waits for them, and re-layouts: 77.8 us -> 58.5 us
    dot_general x19, matrix products: 79.7 us -> 202 us  [forward_layer(): gate_value = jnp.dot(normed, weight, preferred_element_type=jnp.float32)]
    dynamic_update_slice x1 -> x19, other arithmetic: 0.1 us -> 26.1 us  [on_device(): kept_inputs = lax.dynamic_update_index_in_dim(kept_inputs, source, slot, 0)]
    ppermute x12 -> x24, waiting for transfers between devices: 31.9 us -> 7.38 us  [on_device(): slope_rows.append(lax.ppermute(finished, 'dp', pairs))]
    ppermute x1, waiting for transfers between devices: 54.2 us -> 30.1 us  [on_device(): lax.ppermute(theirs.astype(jnp.bfloat16), 'dp', [(r, (r + ring) % replica...]
    convert_element_type x0 -> x18, other arithmetic: none -> 20.6 us  [forward_layer(): output = (floats + jax.nn.silu(gate_value)).astype(jnp.bfloat16)]
    dynamic_update_slice x36 -> x0, local copies, waits for them, and re-layouts: 20.2 us -> none  [the longest x18 19.4 us: on_device(): lax.dynamic_update_index_in_dim(kept_gates, gate_value, slot, 0)]
    dot_general x4 -> x16, matrix products: 35.9 us -> 55.5 us  [the longest x8 31.2 us: on_device(): lax.dot_general(lax.dynamic_index_in_dim(normed_rows, 1 - side, 1, keepdi...]
    ppermute x36 -> x40, starting transfers between devices: 146 us -> 165 us  [relay(): return lax.ppermute(array, ('pipe', 'dp'), pairs)]
  transfers between devices with their start and end apart: 62 -> 90, of which waited for: 40 -> 33; matrix products, arithmetic and copies ran while one was open for 34% -> 25% of each run, Pallas kernels for 0% -> 0%
where the time goes in v7:
time: 1110 us; the launch traced here: 1090 us
  matrix products  346 us (31%)
  waiting for transfers between devices  307 us (28%)
  starting transfers between devices  238 us (21%)
  other arithmetic  142 us (13%)
  local copies, waits for them, and re-layouts  58.5 us (5%)
    ppermute x40, waiting for transfers between devices, relay(): return lax.ppermute(array, ('pipe', 'dp'), pairs)  265 us
    dot_general x19, matrix products, forward_layer(): gate_value = jnp.dot(normed, weight, preferred_element_type=jnp.float32)  202 us
    ppermute x40, starting transfers between devices, relay(): return lax.ppermute(array, ('pipe', 'dp'), pairs)  165 us
    dot_general x22, matrix products, backward_layer(): back = jnp.dot(slope, weight_t, preferred_element_type=jnp.float32)  88.3 us
    unnamed x229, local copies, waits for them, and re-layouts  40.2 us
    ppermute x24, starting transfers between devices, on_device(): normed_rows.append(lax.ppermute(wanted, 'dp', pairs))  38 us
    ppermute x24, starting transfers between devices, on_device(): slope_rows.append(lax.ppermute(finished, 'dp', pairs))  34.5 us
    dynamic_update_slice x23, other arithmetic, on_device(): kept_slopes = lax.dynamic_update_index_in_dim(kept_slopes, slope, slot, 0)  33 us
  transfers between devices with their start and end apart: 90, of which 33 were waited for; matrix products, arithmetic and copies ran while one was open for 25% of the time, Pallas kernels for 0%

profile of v7, /device:TPU:6, one launch (start us, length us, event | category | flops | bytes accessed | tf_op | source)
XLA Modules:
  0.0 1094.5 jit_solution(15820780285247442943)
XLA Ops:
  20.4 11.3 %collective-permute-done = bf16[96,3072]{1,0:T(8,128)(2,1)} collective-permute-done((bf16[96,3072]{1,0:T(8,128)(2,1)}, bf16[96,3072]{1,0:T(8,128)(2,1)}, u32[]{:S(2)}, u32[]{:S(2)}) %collective-permute-start) | collective-permute-done | bytes 589856 | tf_op jit(solution)/shard_map/ppermute | solution.py:25
  47.0 12.9 %collective-permute-done.1 = bf16[96,3072]{1,0:T(8,128)(2,1)} collective-permute-done((bf16[96,3072]{1,0:T(8,128)(2,1)}, bf16[96,3072]{1,0:T(8,128)(2,1)}, u32[]{:S(2)}, u32[]{:S(2)}) %collective-permute-start.1) | collective-permute-done | bytes 589856 | tf_op jit(solution)/shard_map/ppermute | solution.py:25
  75.5 12.7 %collective-permute-done.2 = bf16[96,3072]{1,0:T(8,128)(2,1)} collective-permute-done((bf16[96,3072]{1,0:T(8,128)(2,1)}, bf16[96,3072]{1,0:T(8,128)(2,1)}, u32[]{:S(2)}, u32[]{:S(2)}) %collective-permute-start.2) | collective-permute-done | bytes 589856 | tf_op jit(solution)/shard_map/ppermute | solution.py:25
  103.5 12.9 %collective-permute-done.3 = bf16[96,3072]{1,0:T(8,128)(2,1)} collective-permute-done((bf16[96,3072]{1,0:T(8,128)(2,1)}, bf16[96,3072]{1,0:T(8,128)(2,1)}, u32[]{:S(2)}, u32[]{:S(2)}) %collective-permute-start.3) | collective-permute-done | bytes 589856 | tf_op jit(solution)/shard_map/ppermute | solution.py:25
  131.7 12.9 %collective-permute-done.4 = bf16[96,3072]{1,0:T(8,128)(2,1)} collective-permute-done((bf16[96,3072]{1,0:T(8,128)(2,1)}, bf16[96,3072]{1,0:T(8,128)(2,1)}, u32[]{:S(2)}, u32[]{:S(2)}) %collective-permute-start.4) | collective-permute-done | bytes 589856 | tf_op jit(solution)/shard_map/ppermute | solution.py:25
  160.3 12.5 %collective-permute-done.5 = bf16[96,3072]{1,0:T(8,128)(2,1)} collective-permute-done((bf16[96,3072]{1,0:T(8,128)(2,1)}, bf16[96,3072]{1,0:T(8,128)(2,1)}, u32[]{:S(2)}, u32[]{:S(2)}) %collective-permute-start.5) | collective-permute-done | bytes 589856 | tf_op jit(solution)/shard_map/ppermute | solution.py:25
  188.1 12.9 %collective-permute-done.6 = bf16[96,3072]{1,0:T(8,128)(2,1)} collective-permute-done((bf16[96,3072]{1,0:T(8,128)(2,1)}, bf16[96,3072]{1,0:T(8,128)(2,1)}, u32[]{:S(2)}, u32[]{:S(2)}) %collective-permute-start.6) | collective-permute-done | bytes 589856 | tf_op jit(solution)/shard_map/ppermute | solution.py:25
  216.3 12.9 %collective-permute-done.7 = bf16[96,3072]{1,0:T(8,128)(2,1)} collective-permute-done((bf16[96,3072]{1,0:T(8,128)(2,1)}, bf16[96,3072]{1,0:T(8,128)(2,1)}, u32[]{:S(2)}, u32[]{:S(2)}) %collective-permute-start.7) | collective-permute-done | bytes 589856 | tf_op jit(solution)/shard_map/ppermute | solution.py:25
  230.8 10.7 bitcast_dynamic-update-slice_fusion.9
  244.7 12.7 %collective-permute-done.8 = bf16[96,3072]{1,0:T(8,128)(2,1)} collective-permute-done((bf16[96,3072]{1,0:T(8,128)(2,1)}, bf16[96,3072]{1,0:T(8,128)(2,1)}, u32[]{:S(2)}, u32[]{:S(2)}) %collective-permute-start.8) | collective-permute-done | bytes 589856 | tf_op jit(solution)/shard_map/ppermute | solution.py:25
  272.8 12.9 %collective-permute-done.9 = bf16[96,3072]{1,0:T(8,128)(2,1)} collective-permute-done((bf16[96,3072]{1,0:T(8,128)(2,1)}, bf16[96,3072]{1,0:T(8,128)(2,1)}, u32[]{:S(2)}, u32[]{:S(2)}) %collective-permute-start.9) | collective-permute-done | bytes 589856 | tf_op jit(solution)/shard_map/ppermute | solution.py:25
  287.3 10.6 bitcast_dynamic-update-slice_fusion.7
  301.0 12.9 %collective-permute-done.10 = bf16[96,3072]{1,0:T(8,128)(2,1)} collective-permute-done((bf16[96,3072]{1,0:T(8,128)(2,1)}, bf16[96,3072]{1,0:T(8,128)(2,1)}, u32[]{:S(2)}, u32[]{:S(2)}) %collective-permute-start.10) | collective-permute-done | bytes 589856 | tf_op jit(solution)/shard_map/ppermute | solution.py:25
  315.5 10.7 bitcast_dynamic-update-slice_fusion.6
  329.5 12.7 %collective-permute-done.11 = bf16[96,3072]{1,0:T(8,128)(2,1)} collective-permute-done((bf16[96,3072]{1,0:T(8,128)(2,1)}, bf16[96,3072]{1,0:T(8,128)(2,1)}, u32[]{:S(2)}, u32[]{:S(2)}) %collective-permute-start.11) | collective-permute-done | bytes 589856 | tf_op jit(solution)/shard_map/ppermute | solution.py:25
  357.5 12.9 %collective-permute-done.12 = bf16[96,3072]{1,0:T(8,128)(2,1)} collective-permute-done((bf16[96,3072]{1,0:T(8,128)(2,1)}, bf16[96,3072]{1,0:T(8,128)(2,1)}, u32[]{:S(2)}, u32[]{:S(2)}) %collective-permute-start.12) | collective-permute-done | bytes 589856 | tf_op jit(solution)/shard_map/ppermute | solution.py:25
  385.7 12.9 %collective-permute-done.13 = bf16[96,3072]{1,0:T(8,128)(2,1)} collective-permute-done((bf16[96,3072]{1,0:T(8,128)(2,1)}, bf16[96,3072]{1,0:T(8,128)(2,1)}, u32[]{:S(2)}, u32[]{:S(2)}) %collective-permute-start.13) | collective-permute-done | bytes 589856 | tf_op jit(solution)/shard_map/ppermute | solution.py:25
  414.3 12.5 %collective-permute-done.14 = bf16[96,3072]{1,0:T(8,128)(2,1)} collective-permute-done((bf16[96,3072]{1,0:T(8,128)(2,1)}, bf16[96,3072]{1,0:T(8,128)(2,1)}, u32[]{:S(2)}, u32[]{:S(2)}) %collective-permute-start.14) | collective-permute-done | bytes 589856 | tf_op jit(solution)/shard_map/ppermute | solution.py:25
  442.0 12.9 %collective-permute-done.15 = bf16[96,3072]{1,0:T(8,128)(2,1)} collective-permute-done((bf16[96,3072]{1,0:T(8,128)(2,1)}, bf16[96,3072]{1,0:T(8,128)(2,1)}, u32[]{:S(2)}, u32[]{:S(2)}) %collective-permute-start.15) | collective-permute-done | bytes 589856 | tf_op jit(solution)/shard_map/ppermute | solution.py:25
  470.2 12.9 %collective-permute-done.16 = bf16[96,3072]{1,0:T(8,128)(2,1)} collective-permute-done((bf16[96,3072]{1,0:T(8,128)(2,1)}, bf16[96,3072]{1,0:T(8,128)(2,1)}, u32[]{:S(2)}, u32[]{:S(2)}) %collective-permute-start.16) | collective-permute-done | bytes 589856 | tf_op jit(solution)/shard_map/ppermute | solution.py:25
  498.9 24.6 %copy.5 = bf16[1,3072,3072]{1,2,0:T(8,128)(2,1)} copy(bf16[1,3072,3072]{2,1,0:T(8,128)(2,1)} %param.4) | data formatting | bytes 37748736 | tf_op args[1]
  556.0 13.2 %fusion.348 = (f32[48]{0:T(128)S(1)}, f32[48]{0:T(128)S(1)}, f32[48]{0:T(128)S(1)}, f32[48]{0:T(128)S(1)}, f32[48]{0:T(128)S(1)}, /*index=5*/f32[48]{0:T(128)S(1...) fusion(bf16[12,48,3072]{2,1,0:T(8,128)(2,1)} %bitcast.1165, ...), kind=kOutput, calls=%fused_computation.507 | convolution fusion | flops 914816000 | bytes 25080512 | tf_op jit(solution)/shard_map/dot_general | solution.py:47
  1050.6 30.1 %collective-permute-done.89 = bf16[384,3072]{1,0:T(8,128)(2,1)} collective-permute-done((bf16[384,3072]{1,0:T(8,128)(2,1)}, bf16[384,3072]{1,0:T(8,128)(2,1)}, u32[]{:S(2)}, u32[]{:S(2)}) %collective-permute-start.89) | collective-permute-done | bytes 2359328 | tf_op jit(solution)/shard_map/ppermute | solution.py:144
  1080.8 13.5 %fusion.88 = bf16[1,384,3072]{2,1,0:T(8,128)(2,1)} fusion(bf16[384,3072]{1,0:T(8,128)(2,1)} %collective-permute-done.89, f32[384,3072]{1,0:T(8,128)} %fusion.512, f32[384,3072]{1,0:T(8,128)} %fusion.514, f32[384,3072]{1,0:T(8,128)} %fusion.516, f32[384,3072]{1,0:T(8,128)} %fusion.518, f32[384,3072]{1,0:T(8,128)} %fusion.520, f32[384,3072]{1,0:T(8,128)} %fusion.522, ...), kind=kLoop, calls=%fused_computation.86 | loop fusion | flops 12976128 | bytes 42467328 | tf_op jit(solution)/shard_map/broadcast_in_dim | solution.py:148
  (686 shorter events, 761.4 us)
Async XLA Ops:
  496.5 27.1 %collective-permute-start.17 = (bf16[96,3072]{1,0:T(8,128)(2,1)}, bf16[96,3072]{1,0:T(8,128)(2,1)}, u32[]{:S(2)}, u32[]{:S(2)}) collective-permute-start(bf16[96,3072]{1,0:T(8,128)(2,1)} %fusion.146), channel_id=1, source_target_pairs={{0,8},{1,9},{2,10},{3,11},{4,12},{5,13},{6,14},{7,15},{8,16},{9,17... | collective-permute-start | bytes 1769480 | tf_op jit(solution)/shard_map/ppermute | solution.py:25
  498.4 57.4 %collective-permute-start.21 = (bf16[4,96,3072]{2,1,0:T(8,128)(2,1)}, bf16[4,96,3072]{2,1,0:T(8,128)(2,1)}, u32[]{:S(2)}, u32[]{:S(2)}) collective-permute-start(bf16[4,96,3072]{2,1,0:T(8,128)(2,1)} %param.5), channel_id=1, source_target_pairs={{0,4},{1,5},{2,6},{3,7},{4,0},{5,1},{6,2},{7,3},{8,12},{9,13},{10,... | collective-permute-start | bytes 7077896 | tf_op jit(solution)/shard_map/ppermute | solution.py:77
  528.8 260.8 %collective-permute-start.75 = (bf16[48,2,384]{2,0,1:T(8,128)(2,1)}, bf16[48,2,384]{2,0,1:T(8,128)(2,1)}, u32[]{:S(2)}, u32[]{:S(2)}) collective-permute-start(bf16[48,2,384]{2,0,1:T(8,128)(2,1)} %pad_maximum_fusion.26), channel_id=1, source_target_pairs={{0,1},{1,2},{2,3},{3,0},{4,5},{5,6},{6,7},{7,4},{8,9},{9,10},{10,1... | collective-permute-start | bytes 221192 | tf_op jit(solution)/shard_map/ppermute | solution.py:132
  531.3 259.1 %collective-permute-start.76 = (bf16[48,2,384]{2,0,1:T(8,128)(2,1)}, bf16[48,2,384]{2,0,1:T(8,128)(2,1)}, u32[]{:S(2)}, u32[]{:S(2)}) collective-permute-start(bf16[48,2,384]{2,0,1:T(8,128)(2,1)} %pad_maximum_fusion.27), channel_id=1, source_target_pairs={{0,2},{1,3},{2,0},{3,1},{4,6},{5,7},{6,4},{7,5},{8,10},{9,11},{10,... | collective-permute-start | bytes 221192 | tf_op jit(solution)/shard_map/ppermute | solution.py:132
  535.6 257.1 %collective-permute-start.77 = (bf16[48,2,384]{2,0,1:T(8,128)(2,1)}, bf16[48,2,384]{2,0,1:T(8,128)(2,1)}, u32[]{:S(2)}, u32[]{:S(2)}) collective-permute-start(bf16[48,2,384]{2,0,1:T(8,128)(2,1)} %pad_maximum_fusion.28), channel_id=1, source_target_pairs={{0,3},{1,0},{2,1},{3,2},{4,7},{5,4},{6,5},{7,6},{8,11},{9,8},{10,9... | collective-permute-start | bytes 221192 | tf_op jit(solution)/shard_map/ppermute | solution.py:132
  537.2 256.7 %collective-permute-start.82 = (bf16[48,2,384]{2,0,1:T(8,128)(2,1)}, bf16[48,2,384]{2,0,1:T(8,128)(2,1)}, u32[]{:S(2)}, u32[]{:S(2)}) collective-permute-start(bf16[48,2,384]{2,0,1:T(8,128)(2,1)} %pad_maximum_fusion.29), channel_id=1, source_target_pairs={{0,1},{1,2},{2,3},{3,0},{4,5},{5,6},{6,7},{7,4},{8,9},{9,10},{10,1... | collective-permute-start | bytes 221192 | tf_op jit(solution)/shard_map/ppermute | solution.py:132
  846.3 34.9 %collective-permute-start.39 = (bf16[48,3072]{1,0:T(8,128)(2,1)S(1)}, bf16[48,3072]{1,0:T(8,128)(2,1)}, u32[]{:S(2)}, u32[]{:S(2)}) collective-permute-start(bf16[48,3072]{1,0:T(8,128)(2,1)S(1)} %slice_bitcast_fusion.7), channel_id=1, source_target_pairs={{0,3},{1,0},{2,1},{3,2},{4,7},{5,4},{6,5},{7,6},{8,11},{9,8},{10,9... | collective-permute-start | bytes 884744 | tf_op jit(solution)/shard_map/ppermute | solution.py:131
  849.2 24.4 %collective-permute-start.38 = (bf16[48,3072]{1,0:T(8,128)(2,1)S(1)}, bf16[48,3072]{1,0:T(8,128)(2,1)}, u32[]{:S(2)}, u32[]{:S(2)}) collective-permute-start(bf16[48,3072]{1,0:T(8,128)(2,1)S(1)} %slice_bitcast_fusion.7), channel_id=1, source_target_pairs={{0,2},{1,3},{2,0},{3,1},{4,6},{5,7},{6,4},{7,5},{8,10},{9,11},{10,... | collective-permute-start | bytes 884744 | tf_op jit(solution)/shard_map/ppermute | solution.py:131
  849.6 22.9 %collective-permute-start.37 = (bf16[48,3072]{1,0:T(8,128)(2,1)S(1)}, bf16[48,3072]{1,0:T(8,128)(2,1)}, u32[]{:S(2)}, u32[]{:S(2)}) collective-permute-start(bf16[48,3072]{1,0:T(8,128)(2,1)S(1)} %slice_bitcast_fusion.7), channel_id=1, source_target_pairs={{0,1},{1,2},{2,3},{3,0},{4,5},{5,6},{6,7},{7,4},{8,9},{9,10},{10,1... | collective-permute-start | bytes 884744 | tf_op jit(solution)/shard_map/ppermute | solution.py:131
  863.4 40.0 %collective-permute-start.46 = (bf16[48,3072]{1,0:T(8,128)(2,1)S(1)}, bf16[48,3072]{1,0:T(8,128)(2,1)}, u32[]{:S(2)}, u32[]{:S(2)}) collective-permute-start(bf16[48,3072]{1,0:T(8,128)(2,1)S(1)} %slice_bitcast_fusion.6), channel_id=1, source_target_pairs={{0,3},{1,0},{2,1},{3,2},{4,7},{5,4},{6,5},{7,6},{8,11},{9,8},{10,9... | collective-permute-start | bytes 884744 | tf_op jit(solution)/shard_map/ppermute | solution.py:131
  865.9 33.8 %collective-permute-start.45 = (bf16[48,3072]{1,0:T(8,128)(2,1)S(1)}, bf16[48,3072]{1,0:T(8,128)(2,1)}, u32[]{:S(2)}, u32[]{:S(2)}) collective-permute-start(bf16[48,3072]{1,0:T(8,128)(2,1)S(1)} %slice_bitcast_fusion.6), channel_id=1, source_target_pairs={{0,2},{1,3},{2,0},{3,1},{4,6},{5,7},{6,4},{7,5},{8,10},{9,11},{10,... | collective-permute-start | bytes 884744 | tf_op jit(solution)/shard_map/ppermute | solution.py:131
  872.6 25.5 %collective-permute-start.44 = (bf16[48,3072]{1,0:T(8,128)(2,1)S(1)}, bf16[48,3072]{1,0:T(8,128)(2,1)}, u32[]{:S(2)}, u32[]{:S(2)}) collective-permute-start(bf16[48,3072]{1,0:T(8,128)(2,1)S(1)} %slice_bitcast_fusion.6), channel_id=1, source_target_pairs={{0,1},{1,2},{2,3},{3,0},{4,5},{5,6},{6,7},{7,4},{8,9},{9,10},{10,1... | collective-permute-start | bytes 884744 | tf_op jit(solution)/shard_map/ppermute | solution.py:131
  889.7 36.2 %collective-permute-start.53 = (bf16[48,3072]{1,0:T(8,128)(2,1)S(1)}, bf16[48,3072]{1,0:T(8,128)(2,1)}, u32[]{:S(2)}, u32[]{:S(2)}) collective-permute-start(bf16[48,3072]{1,0:T(8,128)(2,1)S(1)} %slice_bitcast_fusion.5), channel_id=1, source_target_pairs={{0,3},{1,0},{2,1},{3,2},{4,7},{5,4},{6,5},{7,6},{8,11},{9,8},{10,9... | collective-permute-start | bytes 884744 | tf_op jit(solution)/shard_map/ppermute | solution.py:131
  892.7 26.5 %collective-permute-start.52 = (bf16[48,3072]{1,0:T(8,128)(2,1)S(1)}, bf16[48,3072]{1,0:T(8,128)(2,1)}, u32[]{:S(2)}, u32[]{:S(2)}) collective-permute-start(bf16[48,3072]{1,0:T(8,128)(2,1)S(1)} %slice_bitcast_fusion.5), channel_id=1, source_target_pairs={{0,2},{1,3},{2,0},{3,1},{4,6},{5,7},{6,4},{7,5},{8,10},{9,11},{10,... | collective-permute-start | bytes 884744 | tf_op jit(solution)/shard_map/ppermute | solution.py:131
  909.0 39.4 %collective-permute-start.60 = (bf16[48,3072]{1,0:T(8,128)(2,1)S(1)}, bf16[48,3072]{1,0:T(8,128)(2,1)}, u32[]{:S(2)}, u32[]{:S(2)}) collective-permute-start(bf16[48,3072]{1,0:T(8,128)(2,1)S(1)} %slice_bitcast_fusion.4), channel_id=1, source_target_pairs={{0,3},{1,0},{2,1},{3,2},{4,7},{5,4},{6,5},{7,6},{8,11},{9,8},{10,9... | collective-permute-start | bytes 884744 | tf_op jit(solution)/shard_map/ppermute | solution.py:131
  911.4 30.1 %collective-permute-start.59 = (bf16[48,3072]{1,0:T(8,128)(2,1)S(1)}, bf16[48,3072]{1,0:T(8,128)(2,1)}, u32[]{:S(2)}, u32[]{:S(2)}) collective-permute-start(bf16[48,3072]{1,0:T(8,128)(2,1)S(1)} %slice_bitcast_fusion.4), channel_id=1, source_target_pairs={{0,2},{1,3},{2,0},{3,1},{4,6},{5,7},{6,4},{7,5},{8,10},{9,11},{10,... | collective-permute-start | bytes 884744 | tf_op jit(solution)/shard_map/ppermute | solution.py:131
  931.3 39.6 %collective-permute-start.67 = (bf16[48,3072]{1,0:T(8,128)(2,1)S(1)}, bf16[48,3072]{1,0:T(8,128)(2,1)}, u32[]{:S(2)}, u32[]{:S(2)}) collective-permute-start(bf16[48,3072]{1,0:T(8,128)(2,1)S(1)} %slice_bitcast_fusion.3), channel_id=1, source_target_pairs={{0,3},{1,0},{2,1},{3,2},{4,7},{5,4},{6,5},{7,6},{8,11},{9,8},{10,9... | collective-permute-start | bytes 884744 | tf_op jit(solution)/shard_map/ppermute | solution.py:131
  934.3 29.8 %collective-permute-start.66 = (bf16[48,3072]{1,0:T(8,128)(2,1)S(1)}, bf16[48,3072]{1,0:T(8,128)(2,1)}, u32[]{:S(2)}, u32[]{:S(2)}) collective-permute-start(bf16[48,3072]{1,0:T(8,128)(2,1)S(1)} %slice_bitcast_fusion.3), channel_id=1, source_target_pairs={{0,2},{1,3},{2,0},{3,1},{4,6},{5,7},{6,4},{7,5},{8,10},{9,11},{10,... | collective-permute-start | bytes 884744 | tf_op jit(solution)/shard_map/ppermute | solution.py:131
  939.9 23.1 %collective-permute-start.65 = (bf16[48,3072]{1,0:T(8,128)(2,1)S(1)}, bf16[48,3072]{1,0:T(8,128)(2,1)}, u32[]{:S(2)}, u32[]{:S(2)}) collective-permute-start(bf16[48,3072]{1,0:T(8,128)(2,1)S(1)} %slice_bitcast_fusion.3), channel_id=1, source_target_pairs={{0,1},{1,2},{2,3},{3,0},{4,5},{5,6},{6,7},{7,4},{8,9},{9,10},{10,1... | collective-permute-start | bytes 884744 | tf_op jit(solution)/shard_map/ppermute | solution.py:131
  953.9 39.6 %collective-permute-start.74 = (bf16[48,3072]{1,0:T(8,128)(2,1)S(1)}, bf16[48,3072]{1,0:T(8,128)(2,1)}, u32[]{:S(2)}, u32[]{:S(2)}) collective-permute-start(bf16[48,3072]{1,0:T(8,128)(2,1)S(1)} %slice_bitcast_fusion.2), channel_id=1, source_target_pairs={{0,3},{1,0},{2,1},{3,2},{4,7},{5,4},{6,5},{7,6},{8,11},{9,8},{10,9... | collective-permute-start | bytes 884744 | tf_op jit(solution)/shard_map/ppermute | solution.py:131
  956.3 30.3 %collective-permute-start.73 = (bf16[48,3072]{1,0:T(8,128)(2,1)S(1)}, bf16[48,3072]{1,0:T(8,128)(2,1)}, u32[]{:S(2)}, u32[]{:S(2)}) collective-permute-start(bf16[48,3072]{1,0:T(8,128)(2,1)S(1)} %slice_bitcast_fusion.2), channel_id=1, source_target_pairs={{0,2},{1,3},{2,0},{3,1},{4,6},{5,7},{6,4},{7,5},{8,10},{9,11},{10,... | collective-permute-start | bytes 884744 | tf_op jit(solution)/shard_map/ppermute | solution.py:131
  976.3 28.9 %collective-permute-start.81 = (bf16[48,3072]{1,0:T(8,128)(2,1)S(1)}, bf16[48,3072]{1,0:T(8,128)(2,1)S(1)}, u32[]{:S(2)}, u32[]{:S(2)}) collective-permute-start(bf16[48,3072]{1,0:T(8,128)(2,1)S(1)} %slice_bitcast_fusion.1), channel_id=1, source_target_pairs={{0,3},{1,0},{2,1},{3,2},{4,7},{5,4},{6,5},{7,6},{8,11},{9,8},{10,9... | collective-permute-start | bytes 884744 | tf_op jit(solution)/shard_map/ppermute | solution.py:131
  979.3 25.8 %collective-permute-start.80 = (bf16[48,3072]{1,0:T(8,128)(2,1)S(1)}, bf16[48,3072]{1,0:T(8,128)(2,1)S(1)}, u32[]{:S(2)}, u32[]{:S(2)}) collective-permute-start(bf16[48,3072]{1,0:T(8,128)(2,1)S(1)} %slice_bitcast_fusion.1), channel_id=1, source_target_pairs={{0,2},{1,3},{2,0},{3,1},{4,6},{5,7},{6,4},{7,5},{8,10},{9,11},{10,... | collective-permute-start | bytes 884744 | tf_op jit(solution)/shard_map/ppermute | solution.py:131
  1029.0 51.8 %collective-permute-start.89 = (bf16[384,3072]{1,0:T(8,128)(2,1)}, bf16[384,3072]{1,0:T(8,128)(2,1)}, u32[]{:S(2)}, u32[]{:S(2)}) collective-permute-start(bf16[384,3072]{1,0:T(8,128)(2,1)} %add_convert_fusion), channel_id=1, source_target_pairs={{0,4},{1,5},{2,6},{3,7},{4,0},{5,1},{6,2},{7,3},{8,12},{9,13},{10,... | collective-permute-start | bytes 7077896 | tf_op jit(solution)/shard_map/ppermute | solution.py:144
  (164 other events, 2685.6 us)

commit v8 on v7

--- a/solution.py
+++ b/solution.py
@@ -54,7 +54,11 @@
 
 def on_device(inputs, projection, cotangent):
     weight = projection[0]
+    split = 2
     micro, rows_mb, width = inputs.shape
+    micro, rows_mb = micro * split, rows_mb // split
+    inputs = inputs.reshape(micro, rows_mb, width)
+    cotangent = cotangent.reshape(micro, rows_mb, width)
     section = lax.axis_index("pipe")
     sections = lax.axis_size("pipe")
     replicas = lax.axis_size("dp")
@@ -76,12 +80,6 @@
     half = replicas // 2
     cotangent = lax.ppermute(cotangent, "dp", [(r, (r + half) % replicas) for r in range(replicas)])
     weight_t = with_layout_constraint(jnp.transpose(weight), Layout((0, 1)))
-    split = 2
-    kept_inputs = kept_inputs.reshape(split * (micro + 2), rows_mb // split, width)
-    kept_gates = kept_gates.reshape(split * (micro + 2), rows_mb // split, width)
-    micro, rows_mb = micro * split, rows_mb // split
-    cotangent = cotangent.reshape(micro, rows_mb, width)
-    ticks = micro + sections - 1
     kept_slopes = jnp.zeros((micro + 2, rows_mb, width), jnp.bfloat16)
     incoming = jnp.zeros((rows_mb, width), jnp.bfloat16)
     cols = width // replicas
@@ -96,9 +94,8 @@
         slot = jnp.clip(batch + 1, 0, micro + 1)
         first = lax.dynamic_index_in_dim(cotangent, jnp.clip(batch, 0, micro - 1), 0, keepdims=False)
         source = jnp.where(section == sections - 1, first, incoming)
-        stored = jnp.clip(batch + split, 0, split * (micro // split + 2) - 1)
-        stored_input = lax.dynamic_index_in_dim(kept_inputs, stored, 0, keepdims=False)
-        stored_gate = lax.dynamic_index_in_dim(kept_gates, stored, 0, keepdims=False)
+        stored_input = lax.dynamic_index_in_dim(kept_inputs, slot, 0, keepdims=False)
+        stored_gate = lax.dynamic_index_in_dim(kept_gates, slot, 0, keepdims=False)
         down, slope = backward_layer(stored_input, stored_gate, source, weight_t)
         kept_slopes = lax.dynamic_update_index_in_dim(kept_slopes, slope, slot, 0)
         if tick + 1 < ticks:
@@ -106,7 +103,7 @@
         done = tick - (sections - 1)
         if done >= 0:
             finished, kept_slopes = lax.optimization_barrier((kept_slopes[done + 1], kept_slopes))
-            floats, factor = norm_factor(kept_inputs[done + split])
+            floats, factor = norm_factor(kept_inputs[done + 1])
             normed = (floats * factor).astype(jnp.bfloat16).reshape(rows_mb, replicas, cols)
             slope_rows = []
             normed_rows = []

time: 1110 us -> 1120 us (level)
  matrix products: 346 us -> 389 us
  waiting for transfers between devices: 307 us -> 282 us
  other arithmetic: 142 us -> 130 us
    dot_general x19 -> x23, matrix products: 202 us -> 246 us  [forward_layer(): gate_value = jnp.dot(normed, weight, preferred_element_type=jnp.float32)]
    ppermute x40 -> x44, waiting for transfers between devices: 265 us -> 245 us  [relay(): return lax.ppermute(array, ('pipe', 'dp'), pairs)]
    convert_element_type x18 -> x22, other arithmetic: 20.6 us -> 4.62 us  [forward_layer(): output = (floats + jax.nn.silu(gate_value)).astype(jnp.bfloat16)]
    ppermute x40 -> x44, starting transfers between devices: 165 us -> 174 us  [relay(): return lax.ppermute(array, ('pipe', 'dp'), pairs)]
    unnamed x229 -> x183, local copies, waits for them, and re-layouts: 40.2 us -> 36.9 us
    dynamic_update_slice x19 -> x23, other arithmetic: 26.1 us -> 23.7 us  [on_device(): kept_inputs = lax.dynamic_update_index_in_dim(kept_inputs, source, slot, 0)]
  transfers between devices with their start and end apart: 90 -> 94, of which waited for: 33 -> 40; matrix products, arithmetic and copies ran while one was open for 25% -> 25% of each run, Pallas kernels for 0% -> 0%
where the time goes in v8:
time: 1120 us; the launch traced here: 1100 us
  matrix products  389 us (35%)
  waiting for transfers between devices  282 us (25%)
  starting transfers between devices  248 us (22%)
  other arithmetic  130 us (12%)
  local copies, waits for them, and re-layouts  49 us (4%)
    dot_general x23, matrix products, forward_layer(): gate_value = jnp.dot(normed, weight, preferred_element_type=jnp.float32)  246 us
    ppermute x44, waiting for transfers between devices, relay(): return lax.ppermute(array, ('pipe', 'dp'), pairs)  245 us
    ppermute x44, starting transfers between devices, relay(): return lax.ppermute(array, ('pipe', 'dp'), pairs)  174 us
    dot_general x22, matrix products, backward_layer(): back = jnp.dot(slope, weight_t, preferred_element_type=jnp.float32)  87.9 us
    ppermute x24, starting transfers between devices, on_device(): normed_rows.append(lax.ppermute(wanted, 'dp', pairs))  39 us
    unnamed x183, local copies, waits for them, and re-layouts  36.9 us
    ppermute x24, starting transfers between devices, on_device(): slope_rows.append(lax.ppermute(finished, 'dp', pairs))  34.5 us
    dynamic_update_slice x23, other arithmetic, on_device(): kept_slopes = lax.dynamic_update_index_in_dim(kept_slopes, slope, slot, 0)  32 us
  transfers between devices with their start and end apart: 94, of which 40 were waited for; matrix products, arithmetic and copies ran while one was open for 25% of the time, Pallas kernels for 0%

profile of v8, /device:TPU:6, one launch (start us, length us, event | category | flops | bytes accessed | tf_op | source)
XLA Modules:
  0.0 1102.0 jit_solution(12294773102226269875)
XLA Ops:
  4.4 10.8 bitcast_dynamic-update-slice_fusion.21
  52.3 10.7 bitcast_dynamic-update-slice_fusion.19
  75.7 10.7 bitcast_dynamic-update-slice_fusion.18
  99.1 10.7 bitcast_dynamic-update-slice_fusion.17
  146.0 10.7 bitcast_dynamic-update-slice_fusion.15
  169.4 10.7 bitcast_dynamic-update-slice_fusion.14
  192.8 10.7 bitcast_dynamic-update-slice_fusion.13
  216.2 10.7 bitcast_dynamic-update-slice_fusion.12
  239.6 10.7 bitcast_dynamic-update-slice_fusion.11
  263.0 10.7 bitcast_dynamic-update-slice_fusion.10
  286.5 10.7 bitcast_dynamic-update-slice_fusion.9
  333.3 10.7 bitcast_dynamic-update-slice_fusion.7
  356.7 10.7 bitcast_dynamic-update-slice_fusion.6
  380.1 10.7 bitcast_dynamic-update-slice_fusion.5
  403.6 10.7 bitcast_dynamic-update-slice_fusion.4
  427.1 10.7 bitcast_dynamic-update-slice_fusion.3
  450.5 10.7 bitcast_dynamic-update-slice_fusion.2
  474.0 10.7 bitcast_dynamic-update-slice_fusion.1
  497.5 10.7 bitcast_dynamic-update-slice_fusion
  510.6 24.6 %copy.5 = bf16[1,3072,3072]{1,2,0:T(8,128)(2,1)} copy(bf16[1,3072,3072]{2,1,0:T(8,128)(2,1)} %param.4) | data formatting | bytes 37748736 | tf_op args[1]
  556.7 10.7 fusion.93
  567.4 12.8 %fusion.305 = (f32[48]{0:T(128)}, f32[48]{0:T(128)}, f32[48]{0:T(128)}, f32[48]{0:T(128)}, f32[48]{0:T(128)}, /*index=5*/f32[48]{0:T(128)}, f32[48]{0:T(128)}, f...) fusion(bf16[10,48,3072]{2,1,0:T(8,128)(2,1)S(1)} %get-tuple-ele, ...), kind=kOutput, calls=%fused_computation.458 | convolution fusion | flops 914816000 | bytes 25080512 | tf_op jit(solution)/shard_map/dot_general | solution.py:47
  1060.4 26.3 %collective-permute-done.93 = bf16[384,3072]{1,0:T(8,128)(2,1)} collective-permute-done((bf16[384,3072]{1,0:T(8,128)(2,1)}, bf16[384,3072]{1,0:T(8,128)(2,1)}, u32[]{:S(2)}, u32[]{:S(2)}) %collective-permute-start.93) | collective-permute-done | bytes 2359328 | tf_op jit(solution)/shard_map/ppermute | solution.py:141
  1086.7 14.8 %fusion.96 = bf16[1,384,3072]{2,1,0:T(8,128)(2,1)} fusion(bf16[384,3072]{1,0:T(8,128)(2,1)} %collective-permute-done.93, f32[384,3072]{1,0:T(8,128)} %fusion.539, f32[384,3072]{1,0:T(8,128)} %fusion.541, f32[384,3072]{1,0:T(8,128)} %fusion.543, f32[384,3072]{1,0:T(8,128)} %fusion.545, f32[384,3072]{1,0:T(8,128)} %fusion.547, f32[384,3072]{1,0:T(8,128)} %fusion.549, ...), kind=kLoop, calls=%fused_computation.94 | loop fusion | flops 12976128 | bytes 42467328 | tf_op jit(solution)/shard_map/broadcast_in_dim | solution.py:145
  (666 shorter events, 806.2 us)
Async XLA Ops:
  508.4 26.8 %collective-permute-start.21 = (bf16[48,3072]{1,0:T(8,128)(2,1)S(1)}, bf16[48,3072]{1,0:T(8,128)(2,1)S(1)}, u32[]{:S(2)}, u32[]{:S(2)}) collective-permute-start(bf16[48,3072]{1,0:T(8,128)(2,1)S(1)} %fusion.368), channel_id=1, source_target_pairs={{0,8},{1,9},{2,10},{3,11},{4,12},{5,13},{6,14},{7,15},{8,16},{9,17... | collective-permute-start | bytes 884744 | tf_op jit(solution)/shard_map/ppermute | solution.py:25
  510.3 57.1 %collective-permute-start.25 = (bf16[8,48,3072]{2,1,0:T(8,128)(2,1)}, bf16[8,48,3072]{2,1,0:T(8,128)(2,1)}, u32[]{:S(2)}, u32[]{:S(2)}) collective-permute-start(bf16[8,48,3072]{2,1,0:T(8,128)(2,1)} %bitcast.49), channel_id=1, source_target_pairs={{0,4},{1,5},{2,6},{3,7},{4,0},{5,1},{6,2},{7,3},{8,12},{9,13},{10,... | collective-permute-start | bytes 7077896 | tf_op jit(solution)/shard_map/ppermute | solution.py:81
  540.0 267.0 %collective-permute-start.79 = (bf16[48,2,384]{2,0,1:T(8,128)(2,1)}, bf16[48,2,384]{2,0,1:T(8,128)(2,1)}, u32[]{:S(2)}, u32[]{:S(2)}) collective-permute-start(bf16[48,2,384]{2,0,1:T(8,128)(2,1)} %pad_maximum_fusion.26), channel_id=1, source_target_pairs={{0,1},{1,2},{2,3},{3,0},{4,5},{5,6},{6,7},{7,4},{8,9},{9,10},{10,1... | collective-permute-start | bytes 221192 | tf_op jit(solution)/shard_map/ppermute | solution.py:129
  542.6 265.2 %collective-permute-start.80 = (bf16[48,2,384]{2,0,1:T(8,128)(2,1)}, bf16[48,2,384]{2,0,1:T(8,128)(2,1)}, u32[]{:S(2)}, u32[]{:S(2)}) collective-permute-start(bf16[48,2,384]{2,0,1:T(8,128)(2,1)} %pad_maximum_fusion.27), channel_id=1, source_target_pairs={{0,2},{1,3},{2,0},{3,1},{4,6},{5,7},{6,4},{7,5},{8,10},{9,11},{10,... | collective-permute-start | bytes 221192 | tf_op jit(solution)/shard_map/ppermute | solution.py:129
  546.8 263.3 %collective-permute-start.81 = (bf16[48,2,384]{2,0,1:T(8,128)(2,1)}, bf16[48,2,384]{2,0,1:T(8,128)(2,1)}, u32[]{:S(2)}, u32[]{:S(2)}) collective-permute-start(bf16[48,2,384]{2,0,1:T(8,128)(2,1)} %pad_maximum_fusion.28), channel_id=1, source_target_pairs={{0,3},{1,0},{2,1},{3,2},{4,7},{5,4},{6,5},{7,6},{8,11},{9,8},{10,9... | collective-permute-start | bytes 221192 | tf_op jit(solution)/shard_map/ppermute | solution.py:129
  548.5 262.8 %collective-permute-start.86 = (bf16[48,2,384]{2,0,1:T(8,128)(2,1)}, bf16[48,2,384]{2,0,1:T(8,128)(2,1)}, u32[]{:S(2)}, u32[]{:S(2)}) collective-permute-start(bf16[48,2,384]{2,0,1:T(8,128)(2,1)} %pad_maximum_fusion.29), channel_id=1, source_target_pairs={{0,1},{1,2},{2,3},{3,0},{4,5},{5,6},{6,7},{7,4},{8,9},{9,10},{10,1... | collective-permute-start | bytes 221192 | tf_op jit(solution)/shard_map/ppermute | solution.py:129
  862.3 35.2 %collective-permute-start.43 = (bf16[48,3072]{1,0:T(8,128)(2,1)S(1)}, bf16[48,3072]{1,0:T(8,128)(2,1)S(1)}, u32[]{:S(2)}, u32[]{:S(2)}) collective-permute-start(bf16[48,3072]{1,0:T(8,128)(2,1)S(1)} %slice_bitcast_fusion.7), channel_id=1, source_target_pairs={{0,3},{1,0},{2,1},{3,2},{4,7},{5,4},{6,5},{7,6},{8,11},{9,8},{10,9... | collective-permute-start | bytes 884744 | tf_op jit(solution)/shard_map/ppermute | solution.py:128
  865.4 24.4 %collective-permute-start.42 = (bf16[48,3072]{1,0:T(8,128)(2,1)S(1)}, bf16[48,3072]{1,0:T(8,128)(2,1)}, u32[]{:S(2)}, u32[]{:S(2)}) collective-permute-start(bf16[48,3072]{1,0:T(8,128)(2,1)S(1)} %slice_bitcast_fusion.7), channel_id=1, source_target_pairs={{0,2},{1,3},{2,0},{3,1},{4,6},{5,7},{6,4},{7,5},{8,10},{9,11},{10,... | collective-permute-start | bytes 884744 | tf_op jit(solution)/shard_map/ppermute | solution.py:128
  866.5 22.3 %collective-permute-start.41 = (bf16[48,3072]{1,0:T(8,128)(2,1)S(1)}, bf16[48,3072]{1,0:T(8,128)(2,1)}, u32[]{:S(2)}, u32[]{:S(2)}) collective-permute-start(bf16[48,3072]{1,0:T(8,128)(2,1)S(1)} %slice_bitcast_fusion.7), channel_id=1, source_target_pairs={{0,1},{1,2},{2,3},{3,0},{4,5},{5,6},{6,7},{7,4},{8,9},{9,10},{10,1... | collective-permute-start | bytes 884744 | tf_op jit(solution)/shard_map/ppermute | solution.py:128
  879.7 40.0 %collective-permute-start.50 = (bf16[48,3072]{1,0:T(8,128)(2,1)S(1)}, bf16[48,3072]{1,0:T(8,128)(2,1)}, u32[]{:S(2)}, u32[]{:S(2)}) collective-permute-start(bf16[48,3072]{1,0:T(8,128)(2,1)S(1)} %slice_bitcast_fusion.6), channel_id=1, source_target_pairs={{0,3},{1,0},{2,1},{3,2},{4,7},{5,4},{6,5},{7,6},{8,11},{9,8},{10,9... | collective-permute-start | bytes 884744 | tf_op jit(solution)/shard_map/ppermute | solution.py:128
  882.7 32.2 %collective-permute-start.49 = (bf16[48,3072]{1,0:T(8,128)(2,1)S(1)}, bf16[48,3072]{1,0:T(8,128)(2,1)}, u32[]{:S(2)}, u32[]{:S(2)}) collective-permute-start(bf16[48,3072]{1,0:T(8,128)(2,1)S(1)} %slice_bitcast_fusion.6), channel_id=1, source_target_pairs={{0,2},{1,3},{2,0},{3,1},{4,6},{5,7},{6,4},{7,5},{8,10},{9,11},{10,... | collective-permute-start | bytes 884744 | tf_op jit(solution)/shard_map/ppermute | solution.py:128
  888.8 25.1 %collective-permute-start.48 = (bf16[48,3072]{1,0:T(8,128)(2,1)S(1)}, bf16[48,3072]{1,0:T(8,128)(2,1)}, u32[]{:S(2)}, u32[]{:S(2)}) collective-permute-start(bf16[48,3072]{1,0:T(8,128)(2,1)S(1)} %slice_bitcast_fusion.6), channel_id=1, source_target_pairs={{0,1},{1,2},{2,3},{3,0},{4,5},{5,6},{6,7},{7,4},{8,9},{9,10},{10,1... | collective-permute-start | bytes 884744 | tf_op jit(solution)/shard_map/ppermute | solution.py:128
  904.9 37.2 %collective-permute-start.57 = (bf16[48,3072]{1,0:T(8,128)(2,1)S(1)}, bf16[48,3072]{1,0:T(8,128)(2,1)}, u32[]{:S(2)}, u32[]{:S(2)}) collective-permute-start(bf16[48,3072]{1,0:T(8,128)(2,1)S(1)} %slice_bitcast_fusion.5), channel_id=1, source_target_pairs={{0,3},{1,0},{2,1},{3,2},{4,7},{5,4},{6,5},{7,6},{8,11},{9,8},{10,9... | collective-permute-start | bytes 884744 | tf_op jit(solution)/shard_map/ppermute | solution.py:128
  907.9 27.5 %collective-permute-start.56 = (bf16[48,3072]{1,0:T(8,128)(2,1)S(1)}, bf16[48,3072]{1,0:T(8,128)(2,1)}, u32[]{:S(2)}, u32[]{:S(2)}) collective-permute-start(bf16[48,3072]{1,0:T(8,128)(2,1)S(1)} %slice_bitcast_fusion.5), channel_id=1, source_target_pairs={{0,2},{1,3},{2,0},{3,1},{4,6},{5,7},{6,4},{7,5},{8,10},{9,11},{10,... | collective-permute-start | bytes 884744 | tf_op jit(solution)/shard_map/ppermute | solution.py:128
  925.2 39.2 %collective-permute-start.64 = (bf16[48,3072]{1,0:T(8,128)(2,1)S(1)}, bf16[48,3072]{1,0:T(8,128)(2,1)S(1)}, u32[]{:S(2)}, u32[]{:S(2)}) collective-permute-start(bf16[48,3072]{1,0:T(8,128)(2,1)S(1)} %slice_bitcast_fusion.4), channel_id=1, source_target_pairs={{0,3},{1,0},{2,1},{3,2},{4,7},{5,4},{6,5},{7,6},{8,11},{9,8},{10,9... | collective-permute-start | bytes 884744 | tf_op jit(solution)/shard_map/ppermute | solution.py:128
  928.3 29.4 %collective-permute-start.63 = (bf16[48,3072]{1,0:T(8,128)(2,1)S(1)}, bf16[48,3072]{1,0:T(8,128)(2,1)}, u32[]{:S(2)}, u32[]{:S(2)}) collective-permute-start(bf16[48,3072]{1,0:T(8,128)(2,1)S(1)} %slice_bitcast_fusion.4), channel_id=1, source_target_pairs={{0,2},{1,3},{2,0},{3,1},{4,6},{5,7},{6,4},{7,5},{8,10},{9,11},{10,... | collective-permute-start | bytes 884744 | tf_op jit(solution)/shard_map/ppermute | solution.py:128
  947.5 39.3 %collective-permute-start.71 = (bf16[48,3072]{1,0:T(8,128)(2,1)S(1)}, bf16[48,3072]{1,0:T(8,128)(2,1)S(1)}, u32[]{:S(2)}, u32[]{:S(2)}) collective-permute-start(bf16[48,3072]{1,0:T(8,128)(2,1)S(1)} %slice_bitcast_fusion.3), channel_id=1, source_target_pairs={{0,3},{1,0},{2,1},{3,2},{4,7},{5,4},{6,5},{7,6},{8,11},{9,8},{10,9... | collective-permute-start | bytes 884744 | tf_op jit(solution)/shard_map/ppermute | solution.py:128
  950.5 28.7 %collective-permute-start.70 = (bf16[48,3072]{1,0:T(8,128)(2,1)S(1)}, bf16[48,3072]{1,0:T(8,128)(2,1)}, u32[]{:S(2)}, u32[]{:S(2)}) collective-permute-start(bf16[48,3072]{1,0:T(8,128)(2,1)S(1)} %slice_bitcast_fusion.3), channel_id=1, source_target_pairs={{0,2},{1,3},{2,0},{3,1},{4,6},{5,7},{6,4},{7,5},{8,10},{9,11},{10,... | collective-permute-start | bytes 884744 | tf_op jit(solution)/shard_map/ppermute | solution.py:128
  969.1 39.4 %collective-permute-start.78 = (bf16[48,3072]{1,0:T(8,128)(2,1)S(1)}, bf16[48,3072]{1,0:T(8,128)(2,1)S(1)}, u32[]{:S(2)}, u32[]{:S(2)}) collective-permute-start(bf16[48,3072]{1,0:T(8,128)(2,1)S(1)} %slice_bitcast_fusion.2), channel_id=1, source_target_pairs={{0,3},{1,0},{2,1},{3,2},{4,7},{5,4},{6,5},{7,6},{8,11},{9,8},{10,9... | collective-permute-start | bytes 884744 | tf_op jit(solution)/shard_map/ppermute | solution.py:128
  972.1 29.7 %collective-permute-start.77 = (bf16[48,3072]{1,0:T(8,128)(2,1)S(1)}, bf16[48,3072]{1,0:T(8,128)(2,1)S(1)}, u32[]{:S(2)}, u32[]{:S(2)}) collective-permute-start(bf16[48,3072]{1,0:T(8,128)(2,1)S(1)} %slice_bitcast_fusion.2), channel_id=1, source_target_pairs={{0,2},{1,3},{2,0},{3,1},{4,6},{5,7},{6,4},{7,5},{8,10},{9,11},{10,... | collective-permute-start | bytes 884744 | tf_op jit(solution)/shard_map/ppermute | solution.py:128
  978.2 22.3 %collective-permute-start.76 = (bf16[48,3072]{1,0:T(8,128)(2,1)S(1)}, bf16[48,3072]{1,0:T(8,128)(2,1)}, u32[]{:S(2)}, u32[]{:S(2)}) collective-permute-start(bf16[48,3072]{1,0:T(8,128)(2,1)S(1)} %slice_bitcast_fusion.2), channel_id=1, source_target_pairs={{0,1},{1,2},{2,3},{3,0},{4,5},{5,6},{6,7},{7,4},{8,9},{9,10},{10,1... | collective-permute-start | bytes 884744 | tf_op jit(solution)/shard_map/ppermute | solution.py:128
  991.5 27.0 %collective-permute-start.85 = (bf16[48,3072]{1,0:T(8,128)(2,1)S(1)}, bf16[48,3072]{1,0:T(8,128)(2,1)S(1)}, u32[]{:S(2)}, u32[]{:S(2)}) collective-permute-start(bf16[48,3072]{1,0:T(8,128)(2,1)S(1)} %slice_bitcast_fusion.1), channel_id=1, source_target_pairs={{0,3},{1,0},{2,1},{3,2},{4,7},{5,4},{6,5},{7,6},{8,11},{9,8},{10,9... | collective-permute-start | bytes 884744 | tf_op jit(solution)/shard_map/ppermute | solution.py:128
  994.5 24.0 %collective-permute-start.84 = (bf16[48,3072]{1,0:T(8,128)(2,1)S(1)}, bf16[48,3072]{1,0:T(8,128)(2,1)S(1)}, u32[]{:S(2)}, u32[]{:S(2)}) collective-permute-start(bf16[48,3072]{1,0:T(8,128)(2,1)S(1)} %slice_bitcast_fusion.1), channel_id=1, source_target_pairs={{0,2},{1,3},{2,0},{3,1},{4,6},{5,7},{6,4},{7,5},{8,10},{9,11},{10,... | collective-permute-start | bytes 884744 | tf_op jit(solution)/shard_map/ppermute | solution.py:128
  1039.1 47.6 %collective-permute-start.93 = (bf16[384,3072]{1,0:T(8,128)(2,1)}, bf16[384,3072]{1,0:T(8,128)(2,1)}, u32[]{:S(2)}, u32[]{:S(2)}) collective-permute-start(bf16[384,3072]{1,0:T(8,128)(2,1)} %add_convert_fusion), channel_id=1, source_target_pairs={{0,4},{1,5},{2,6},{3,7},{4,0},{5,1},{6,2},{7,3},{8,12},{9,13},{10,... | collective-permute-start | bytes 7077896 | tf_op jit(solution)/shard_map/ppermute | solution.py:141
  (145 other events, 2495.1 us)

commit v9 on v6

--- a/solution.py
+++ b/solution.py
@@ -88,6 +88,7 @@
     side = rep // ring
     place = rep % ring
     partial = jnp.zeros((2 * cols, width), jnp.float32)
+    pending_slopes, pending_normed = [], []
     for tick in range(ticks):
         batch = tick - (sections - 1 - section)
         slot = jnp.clip(batch + 1, 0, micro + 1)
@@ -126,11 +127,16 @@
                 ]
                 slope_rows.append(lax.ppermute(finished, "dp", pairs))
                 normed_rows.append(lax.ppermute(wanted, "dp", pairs))
-            slope_rows = jnp.concatenate(slope_rows, axis=0)
-            normed_rows = jnp.concatenate(normed_rows, axis=0).reshape(ring * rows_mb, 2 * cols)
-            partial = partial + lax.dot_general(
-                normed_rows, slope_rows, (((0,), (0,)), ((), ())), preferred_element_type=jnp.float32
-            )
+            pending_slopes += slope_rows
+            pending_normed += normed_rows
+            if done % split == split - 1 or done == micro - 1:
+                slope_rows = jnp.concatenate(pending_slopes, axis=0)
+                normed_rows = jnp.concatenate(pending_normed, axis=0)
+                normed_rows = normed_rows.reshape(normed_rows.shape[0], 2 * cols)
+                partial = partial + lax.dot_general(
+                    normed_rows, slope_rows, (((0,), (0,)), ((), ())), preferred_element_type=jnp.float32
+                )
+                pending_slopes, pending_normed = [], []
     partial = partial.reshape(2, cols, width)
     mine = lax.dynamic_index_in_dim(partial, side, 0, keepdims=False)
     theirs = lax.dynamic_index_in_dim(partial, 1 - side, 0, keepdims=False).astype(jnp.bfloat16)

time: 976 us -> 935 us (0.958)
  matrix products: 250 us -> 204 us
  local copies, waits for them, and re-layouts: 61.1 us -> 98.7 us
  other arithmetic: 122 us -> 94.8 us
  waiting for transfers between devices: 294 us -> 281 us
    dot_general x8 -> x4, matrix products: 69.1 us -> 26.4 us  [on_device(): lax.dot_general(normed_rows, slope_rows, (((0,), (0,)), ((), ())), prefer...]
    unnamed x159 -> x161, local copies, waits for them, and re-layouts: 32.2 us -> 56.4 us
    dynamic_update_slice x22, local copies, waits for them, and re-layouts: 1.01 us -> 19.4 us  [on_device(): lax.dynamic_update_index_in_dim(kept_gates, gate_value, slot, 0)]
    dynamic_update_slice x23, other arithmetic: 45.8 us -> 32.1 us  [on_device(): kept_slopes = lax.dynamic_update_index_in_dim(kept_slopes, slope, slot, 0)]
    ppermute x44, waiting for transfers between devices: 230 us -> 217 us  [relay(): return lax.ppermute(array, ('pipe', 'dp'), pairs)]
  transfers between devices with their start and end apart: 94 -> 94, of which waited for: 38 -> 40; matrix products, arithmetic and copies ran while one was open for 39% -> 38% of each run, Pallas kernels for 0% -> 0%
where the time goes in v9:
time: 935 us; the launch traced here: 922 us
  waiting for transfers between devices  281 us (30%)
  starting transfers between devices  241 us (26%)
  matrix products  204 us (22%)
  local copies, waits for them, and re-layouts  98.7 us (11%)
  other arithmetic  94.8 us (10%)
    ppermute x44, waiting for transfers between devices, relay(): return lax.ppermute(array, ('pipe', 'dp'), pairs)  217 us
    ppermute x44, starting transfers between devices, relay(): return lax.ppermute(array, ('pipe', 'dp'), pairs)  167 us
    dot_general x23, matrix products, forward_layer(): gate_value = jnp.dot(normed, weight, preferred_element_type=jnp.float32)  94.4 us
    dot_general x22, matrix products, backward_layer(): back = jnp.dot(slope, weight_t, preferred_element_type=jnp.float32)  83 us
    unnamed x161, local copies, waits for them, and re-layouts  56.4 us
    ppermute x1, waiting for transfers between devices, on_device(): lax.ppermute(theirs, 'dp', [(r, (r + ring) % replicas) for r in range(rep...  49.1 us
    ppermute x24, starting transfers between devices, on_device(): normed_rows.append(lax.ppermute(wanted, 'dp', pairs))  36.6 us
    ppermute x24, starting transfers between devices, on_device(): slope_rows.append(lax.ppermute(finished, 'dp', pairs))  36.4 us
  transfers between devices with their start and end apart: 94, of which 40 were waited for; matrix products, arithmetic and copies ran while one was open for 38% of the time, Pallas kernels for 0%

profile of v9, /device:TPU:6, one launch (start us, length us, event | category | flops | bytes accessed | tf_op | source)
XLA Modules:
  0.0 922.1 jit_solution(9130249915864156775)
XLA Ops:
  1.2 10.1 %fusion.285 = (bf16[48,3072]{1,0:T(8,128)(2,1)S(1)}, f32[48,3072]{1,0:T(8,128)S(1)}) fusion(bf16[8,48,3072]{2,1,0:T(8,128)(2,1)} %bitcast.1201, s32[]{:T(128)S(6)} %min.277, pred[]{:T(512)S(6)} %eq.38, bf16[1,3072,3072]{2,1,0:T(8,128)(2,1)} %param.4, f32[48]{0:T(128)S(1)} %add_rsqrt_fusion.52), kind=kOutput, calls=%fused_computation.439 | convolution fusion | flops 907739136 | bytes 20351168 | tf_op jit(solution)/shard_map/dot_general | solution.py:37
  14.1 24.6 %copy.4 = bf16[1,3072,3072]{1,2,0:T(8,128)(2,1)} copy(bf16[1,3072,3072]{2,1,0:T(8,128)(2,1)} %param.4) | data formatting | bytes 37748736 | tf_op args[1]
  44.2 8.4 fusion.311
  70.7 8.5 collective-permute-done.2
  86.0 8.5 collective-permute-done.3
  101.2 8.5 collective-permute-done.4
  116.4 8.5 collective-permute-done.5
  131.6 8.5 collective-permute-done.6
  161.9 8.5 collective-permute-done.8
  177.1 8.5 collective-permute-done.9
  192.3 8.5 collective-permute-done.10
  207.6 8.4 collective-permute-done.11
  222.6 8.5 collective-permute-done.12
  237.8 8.5 collective-permute-done.13
  253.0 8.5 collective-permute-done.14
  283.4 8.5 collective-permute-done.16
  298.5 8.5 collective-permute-done.17
  313.7 8.5 collective-permute-done.18
  329.1 8.3 collective-permute-done.19
  344.1 8.5 collective-permute-done.20
  359.2 8.5 collective-permute-done.21
  373.5 9.3 %fusion.308 = (f32[48]{0:T(128)S(1)}, f32[48]{0:T(128)S(1)}, f32[48]{0:T(128)S(1)}, f32[48]{0:T(128)S(1)}, f32[48]{0:T(128)S(1)}, /*index=5*/f32[48]{0:T(128)S(1...) fusion(bf16[10,48,3072]{2,1,0:T(8,128)(2,1)S(1)} %bitcast_dynam, ...), kind=kOutput, calls=%fused_computation.462 | convolution fusion | flops 914816000 | bytes 25080512 | tf_op jit(solution)/shard_map/dot_general | solution.py:47
  853.6 11.0 %add_add_fusion = f32[768,3072]{1,0:T(8,128)} fusion(f32[768,3072]{1,0:T(8,128)} %fusion.554, f32[768,3072]{1,0:T(8,128)S(1)} %bitcast.1197, f32[768,3072]{1,0:T(8,128)} %fusion.553, bf16[384,768]{1,0:T(8,128)(2,1)S(1)} %bitcast.1236, bf16[384,3072]{1,0:T(8,128)(2,1)} %constant_dynamic-update-slice_fusion.56), kind=kOutput, calls=%fused_computation.90 | convolution fusion | flops 1819017216 | bytes 40697856 | tf_op jit(solution)/shard_map/dot_general | solution.py:136
  867.3 49.1 %collective-permute-done.93 = bf16[384,3072]{1,0:T(8,128)(2,1)} collective-permute-done((bf16[384,3072]{1,0:T(8,128)(2,1)S(1)}, bf16[384,3072]{1,0:T(8,128)(2,1)}, u32[]{:S(2)}, u32[]{:S(2)}) %collective-permute-start.93) | collective-permute-done | bytes 2359328 | tf_op jit(solution)/shard_map/ppermute | solution.py:143
  (633 shorter events, 653.6 us)
Async XLA Ops:
  11.2 32.7 %collective-permute-start = (bf16[48,3072]{1,0:T(8,128)(2,1)S(1)}, bf16[48,3072]{1,0:T(8,128)(2,1)S(1)}, u32[]{:S(2)}, u32[]{:S(2)}) collective-permute-start(bf16[48,3072]{1,0:T(8,128)(2,1)S(1)} %get-tuple-element.225), channel_id=1, source_target_pairs={{0,8},{1,9},{2,10},{3,11},{4,12},{5,13},{6,14},{7,15},{8,16},{9,17... | collective-permute-start | bytes 884744 | tf_op jit(solution)/shard_map/ppermute | solution.py:25
  13.1 360.4 %collective-permute-start.28 = (bf16[8,48,3072]{2,1,0:T(8,128)(2,1)}, bf16[8,48,3072]{2,1,0:T(8,128)(2,1)}, u32[]{:S(2)}, u32[]{:S(2)}) collective-permute-start(bf16[8,48,3072]{2,1,0:T(8,128)(2,1)} %bitcast.48), channel_id=1, source_target_pairs={{0,4},{1,5},{2,6},{3,7},{4,0},{5,1},{6,2},{7,3},{8,12},{9,13},{10,... | collective-permute-start | bytes 7077896 | tf_op jit(solution)/shard_map/ppermute | solution.py:81
  384.1 41.4 %collective-permute-start.29 = (bf16[48,3072]{1,0:T(8,128)(2,1)S(1)}, bf16[48,3072]{1,0:T(8,128)(2,1)S(1)}, u32[]{:S(2)}, u32[]{:S(2)}) collective-permute-start(bf16[48,3072]{1,0:T(8,128)(2,1)S(1)} %fusion.216), channel_id=1, source_target_pairs={{8,0},{9,1},{10,2},{11,3},{12,4},{13,5},{14,6},{15,7},{16,8},{17,9... | collective-permute-start | bytes 884744 | tf_op jit(solution)/shard_map/ppermute | solution.py:25
  390.8 155.4 %collective-permute-start.84 = (bf16[48,2,384]{2,1,0:T(2,128)(2,1)}, bf16[48,2,384]{2,1,0:T(2,128)(2,1)}, u32[]{:S(2)}, u32[]{:S(2)}) collective-permute-start(bf16[48,2,384]{2,1,0:T(2,128)(2,1)} %pad_maximum_fusion.23), channel_id=1, source_target_pairs={{0,3},{1,0},{2,1},{3,2},{4,7},{5,4},{6,5},{7,6},{8,11},{9,8},{10,9... | collective-permute-start | bytes 221192 | tf_op jit(solution)/shard_map/ppermute | solution.py:129
  395.6 147.5 %collective-permute-start.83 = (bf16[48,2,384]{2,1,0:T(2,128)(2,1)}, bf16[48,2,384]{2,1,0:T(2,128)(2,1)}, u32[]{:S(2)}, u32[]{:S(2)}) collective-permute-start(bf16[48,2,384]{2,1,0:T(2,128)(2,1)} %pad_maximum_fusion.22), channel_id=1, source_target_pairs={{0,2},{1,3},{2,0},{3,1},{4,6},{5,7},{6,4},{7,5},{8,10},{9,11},{10,... | collective-permute-start | bytes 221192 | tf_op jit(solution)/shard_map/ppermute | solution.py:129
  396.4 138.9 %collective-permute-start.82 = (bf16[48,2,384]{2,1,0:T(2,128)(2,1)}, bf16[48,2,384]{2,1,0:T(2,128)(2,1)}, u32[]{:S(2)}, u32[]{:S(2)}) collective-permute-start(bf16[48,2,384]{2,1,0:T(2,128)(2,1)} %pad_maximum_fusion.21), channel_id=1, source_target_pairs={{0,1},{1,2},{2,3},{3,0},{4,5},{5,6},{6,7},{7,4},{8,9},{9,10},{10,1... | collective-permute-start | bytes 221192 | tf_op jit(solution)/shard_map/ppermute | solution.py:129
  399.3 124.4 %collective-permute-start.81 = (bf16[48,2,384]{2,1,0:T(2,128)(2,1)}, bf16[48,2,384]{2,1,0:T(2,128)(2,1)}, u32[]{:S(2)}, u32[]{:S(2)}) collective-permute-start(bf16[48,2,384]{2,1,0:T(2,128)(2,1)} %pad_maximum_fusion.20), channel_id=1, source_target_pairs={{0,3},{1,0},{2,1},{3,2},{4,7},{5,4},{6,5},{7,6},{8,11},{9,8},{10,9... | collective-permute-start | bytes 221192 | tf_op jit(solution)/shard_map/ppermute | solution.py:129
  523.8 66.4 %collective-permute-start.56 = (bf16[48,2,384]{2,1,0:T(2,128)(2,1)S(1)}, bf16[48,2,384]{2,1,0:T(2,128)(2,1)S(1)}, u32[]{:S(2)}, u32[]{:S(2)}) collective-permute-start(bf16[48,2,384]{2,1,0:T(2,128)(2,1)S(1)} %copy-done.23), channel_id=1, source_target_pairs={{0,3},{1,0},{2,1},{3,2},{4,7},{5,4},{6,5},{7,6},{8,11},{9,8},{10,9... | collective-permute-start | bytes 221192 | tf_op jit(solution)/shard_map/ppermute | solution.py:129
  527.9 54.2 %collective-permute-start.55 = (bf16[48,2,384]{2,1,0:T(2,128)(2,1)S(1)}, bf16[48,2,384]{2,1,0:T(2,128)(2,1)S(1)}, u32[]{:S(2)}, u32[]{:S(2)}) collective-permute-start(bf16[48,2,384]{2,1,0:T(2,128)(2,1)S(1)} %copy-done.26), channel_id=1, source_target_pairs={{0,2},{1,3},{2,0},{3,1},{4,6},{5,7},{6,4},{7,5},{8,10},{9,11},{10,... | collective-permute-start | bytes 221192 | tf_op jit(solution)/shard_map/ppermute | solution.py:129
  543.1 36.4 %collective-permute-start.54 = (bf16[48,2,384]{2,1,0:T(2,128)(2,1)S(1)}, bf16[48,2,384]{2,1,0:T(2,128)(2,1)S(1)}, u32[]{:S(2)}, u32[]{:S(2)}) collective-permute-start(bf16[48,2,384]{2,1,0:T(2,128)(2,1)S(1)} %copy-done.27), channel_id=1, source_target_pairs={{0,1},{1,2},{2,3},{3,0},{4,5},{5,6},{6,7},{7,4},{8,9},{9,10},{10,1... | collective-permute-start | bytes 221192 | tf_op jit(solution)/shard_map/ppermute | solution.py:129
  566.3 68.7 %collective-permute-start.27 = (bf16[48,2,384]{2,1,0:T(2,128)(2,1)S(1)}, bf16[48,2,384]{2,1,0:T(2,128)(2,1)S(1)}, u32[]{:S(2)}, u32[]{:S(2)}) collective-permute-start(bf16[48,2,384]{2,1,0:T(2,128)(2,1)S(1)} %copy-done.19), channel_id=1, source_target_pairs={{0,3},{1,0},{2,1},{3,2},{4,7},{5,4},{6,5},{7,6},{8,11},{9,8},{10,9... | collective-permute-start | bytes 221192 | tf_op jit(solution)/shard_map/ppermute | solution.py:129
  579.5 48.0 %collective-permute-start.26 = (bf16[48,2,384]{2,1,0:T(2,128)(2,1)S(1)}, bf16[48,2,384]{2,1,0:T(2,128)(2,1)S(1)}, u32[]{:S(2)}, u32[]{:S(2)}) collective-permute-start(bf16[48,2,384]{2,1,0:T(2,128)(2,1)S(1)} %copy-done.20), channel_id=1, source_target_pairs={{0,2},{1,3},{2,0},{3,1},{4,6},{5,7},{6,4},{7,5},{8,10},{9,11},{10,... | collective-permute-start | bytes 221192 | tf_op jit(solution)/shard_map/ppermute | solution.py:129
  582.1 35.4 %collective-permute-start.25 = (bf16[48,2,384]{2,1,0:T(2,128)(2,1)S(1)}, bf16[48,2,384]{2,1,0:T(2,128)(2,1)S(1)}, u32[]{:S(2)}, u32[]{:S(2)}) collective-permute-start(bf16[48,2,384]{2,1,0:T(2,128)(2,1)S(1)} %copy-done.21), channel_id=1, source_target_pairs={{0,1},{1,2},{2,3},{3,0},{4,5},{5,6},{6,7},{7,4},{8,9},{9,10},{10,1... | collective-permute-start | bytes 221192 | tf_op jit(solution)/shard_map/ppermute | solution.py:129
  606.6 64.4 %collective-permute-start.70 = (bf16[48,2,384]{2,1,0:T(2,128)(2,1)S(1)}, bf16[48,2,384]{2,1,0:T(2,128)(2,1)S(1)}, u32[]{:S(2)}, u32[]{:S(2)}) collective-permute-start(bf16[48,2,384]{2,1,0:T(2,128)(2,1)S(1)} %copy-done.16), channel_id=1, source_target_pairs={{0,3},{1,0},{2,1},{3,2},{4,7},{5,4},{6,5},{7,6},{8,11},{9,8},{10,9... | collective-permute-start | bytes 221192 | tf_op jit(solution)/shard_map/ppermute | solution.py:129
  617.5 53.4 %collective-permute-start.69 = (bf16[48,2,384]{2,1,0:T(2,128)(2,1)S(1)}, bf16[48,2,384]{2,1,0:T(2,128)(2,1)S(1)}, u32[]{:S(2)}, u32[]{:S(2)}) collective-permute-start(bf16[48,2,384]{2,1,0:T(2,128)(2,1)S(1)} %copy-done.17), channel_id=1, source_target_pairs={{0,2},{1,3},{2,0},{3,1},{4,6},{5,7},{6,4},{7,5},{8,10},{9,11},{10,... | collective-permute-start | bytes 221192 | tf_op jit(solution)/shard_map/ppermute | solution.py:129
  621.4 49.4 %collective-permute-start.68 = (bf16[48,2,384]{2,1,0:T(2,128)(2,1)S(1)}, bf16[48,2,384]{2,1,0:T(2,128)(2,1)S(1)}, u32[]{:S(2)}, u32[]{:S(2)}) collective-permute-start(bf16[48,2,384]{2,1,0:T(2,128)(2,1)S(1)} %copy-done.18), channel_id=1, source_target_pairs={{0,1},{1,2},{2,3},{3,0},{4,5},{5,6},{6,7},{7,4},{8,9},{9,10},{10,1... | collective-permute-start | bytes 221192 | tf_op jit(solution)/shard_map/ppermute | solution.py:129
  680.7 36.1 %collective-permute-start.46 = (bf16[48,3072]{1,0:T(8,128)(2,1)}, bf16[48,3072]{1,0:T(8,128)(2,1)}, u32[]{:S(2)}, u32[]{:S(2)}) collective-permute-start(bf16[48,3072]{1,0:T(8,128)(2,1)} %slice_bitcast_fusion.7), channel_id=1, source_target_pairs={{0,3},{1,0},{2,1},{3,2},{4,7},{5,4},{6,5},{7,6},{8,11},{9,8},{10,9... | collective-permute-start | bytes 884744 | tf_op jit(solution)/shard_map/ppermute | solution.py:128
  707.5 33.1 %collective-permute-start.50 = (bf16[48,3072]{1,0:T(8,128)(2,1)}, bf16[48,3072]{1,0:T(8,128)(2,1)}, u32[]{:S(2)}, u32[]{:S(2)}) collective-permute-start(bf16[48,3072]{1,0:T(8,128)(2,1)} %slice_bitcast_fusion.6), channel_id=1, source_target_pairs={{0,3},{1,0},{2,1},{3,2},{4,7},{5,4},{6,5},{7,6},{8,11},{9,8},{10,9... | collective-permute-start | bytes 884744 | tf_op jit(solution)/shard_map/ppermute | solution.py:128
  722.1 34.3 %collective-permute-start.58 = (bf16[48,3072]{1,0:T(8,128)(2,1)}, bf16[48,3072]{1,0:T(8,128)(2,1)}, u32[]{:S(2)}, u32[]{:S(2)}) collective-permute-start(bf16[48,3072]{1,0:T(8,128)(2,1)} %slice_bitcast_fusion.5), channel_id=1, source_target_pairs={{0,1},{1,2},{2,3},{3,0},{4,5},{5,6},{6,7},{7,4},{8,9},{9,10},{10,1... | collective-permute-start | bytes 884744 | tf_op jit(solution)/shard_map/ppermute | solution.py:128
  723.3 36.0 %collective-permute-start.59 = (bf16[48,3072]{1,0:T(8,128)(2,1)}, bf16[48,3072]{1,0:T(8,128)(2,1)}, u32[]{:S(2)}, u32[]{:S(2)}) collective-permute-start(bf16[48,3072]{1,0:T(8,128)(2,1)} %slice_bitcast_fusion.5), channel_id=1, source_target_pairs={{0,2},{1,3},{2,0},{3,1},{4,6},{5,7},{6,4},{7,5},{8,10},{9,11},{10,... | collective-permute-start | bytes 884744 | tf_op jit(solution)/shard_map/ppermute | solution.py:128
  729.5 32.9 %collective-permute-start.60 = (bf16[48,3072]{1,0:T(8,128)(2,1)}, bf16[48,3072]{1,0:T(8,128)(2,1)}, u32[]{:S(2)}, u32[]{:S(2)}) collective-permute-start(bf16[48,3072]{1,0:T(8,128)(2,1)} %slice_bitcast_fusion.5), channel_id=1, source_target_pairs={{0,3},{1,0},{2,1},{3,2},{4,7},{5,4},{6,5},{7,6},{8,11},{9,8},{10,9... | collective-permute-start | bytes 884744 | tf_op jit(solution)/shard_map/ppermute | solution.py:128
  767.1 32.7 %collective-permute-start.72 = (bf16[48,3072]{1,0:T(8,128)(2,1)S(1)}, bf16[48,3072]{1,0:T(8,128)(2,1)}, u32[]{:S(2)}, u32[]{:S(2)}) collective-permute-start(bf16[48,3072]{1,0:T(8,128)(2,1)S(1)} %slice_bitcast_fusion.3), channel_id=1, source_target_pairs={{0,1},{1,2},{2,3},{3,0},{4,5},{5,6},{6,7},{7,4},{8,9},{9,10},{10,1... | collective-permute-start | bytes 884744 | tf_op jit(solution)/shard_map/ppermute | solution.py:128
  768.0 34.6 %collective-permute-start.73 = (bf16[48,3072]{1,0:T(8,128)(2,1)S(1)}, bf16[48,3072]{1,0:T(8,128)(2,1)S(1)}, u32[]{:S(2)}, u32[]{:S(2)}) collective-permute-start(bf16[48,3072]{1,0:T(8,128)(2,1)S(1)} %slice_bitcast_fusion.3), channel_id=1, source_target_pairs={{0,2},{1,3},{2,0},{3,1},{4,6},{5,7},{6,4},{7,5},{8,10},{9,11},{10,... | collective-permute-start | bytes 884744 | tf_op jit(solution)/shard_map/ppermute | solution.py:128
  867.2 49.2 %collective-permute-start.93 = (bf16[384,3072]{1,0:T(8,128)(2,1)S(1)}, bf16[384,3072]{1,0:T(8,128)(2,1)}, u32[]{:S(2)}, u32[]{:S(2)}) collective-permute-start(bf16[384,3072]{1,0:T(8,128)(2,1)S(1)} %fusion.98), channel_id=1, source_target_pairs={{0,4},{1,5},{2,6},{3,7},{4,0},{5,1},{6,2},{7,3},{8,12},{9,13},{10,... | collective-permute-start | bytes 7077896 | tf_op jit(solution)/shard_map/ppermute | solution.py:143
  (120 other events, 1756.1 us)
